TPU v7x, 512 devices: a whole 4x8x8 slice. The times are simulated.
512 devices in a mesh: seq: 128 (over y, z, core), head: 4 (over x).
Axes of the slice: x: 4, y: 8, z: 8, core: 2. Of those that a mesh axis runs over, the one named last changes fastest.
Arguments:
- query_tokens: bfloat16 [32768, 512], P('seq', 'head'), parts along dimension 1, may hold values from -27 to 27
- key_tokens: bfloat16 [32768, 512], P('seq', 'head'), parts along dimension 1, may hold values from -8 to 8
- value_tokens: bfloat16 [32768, 512], P('seq', 'head'), parts along dimension 1, may hold values from -6 to 6
- grad_out: bfloat16 [32768, 512], P('seq', 'head'), parts along dimension 1, may hold values from -6 to 6
- far_block: int32 [128, 128, 2], replicated, may hold values from -1 to 1, as said below
Outputs:
- attention_out: float32 [32768, 512], P('seq', 'head'), parts along dimension 1
- query_grad: float32 [32768, 512], P('seq', 'head'), parts along dimension 1
- key_grad: float32 [32768, 512], P('seq', 'head'), parts along dimension 1
- value_grad: float32 [32768, 512], P('seq', 'head'), parts along dimension 1
There are 4 independent parts, one for each index of `head`. A program takes and returns all parts, laid end to end along the dimension named above; an argument that names none is the same for every part. Nothing has to cross between parts.
Inputs may be any that keep to these rules, and one draw needn't show every extreme that they name: `far_block`: entry (f, g, b) is -1 unless |f - g| is 2, 3 or a power of two from 4 up to below 128. For each (f, g) either both entries are -1, or entry b equals b (query block b of frame f sees block b of frame g).
All inputs are finite; a program needn't handle non-finite values.
Results may differ from a plain program's by a relative error of at most 0.012.
The roundings to bfloat16 on the way count: a program that leaves them out, or rounds other values in their place, can miss the bound.
Values may be sent and summed in bfloat16 or wider, within the bound.
No kernel may reach another device: no remote copies, remote signals or barrier semaphores. Data moves between devices by JAX's collectives and lax.ppermute only.
A program may use at most 64 MiB of HBM per device.

v0:
```python
import jax
import jax.numpy as jnp
from jax import lax
from jax.sharding import PartitionSpec as P

HD = 128
BLK = 128


def extended(shard, sides, width):
    for axis, dim in sides:
        size, length = (lax.axis_size(axis), shard.shape[dim])
        up = [(i, (i + 1) % size) for i in range(size - 1)]
        down = [(j, i) for i, j in up]
        last = lax.slice_in_dim(shard, length - width, length, axis=dim)
        leading = lax.slice_in_dim(shard, 0, width, axis=dim)
        before = lax.ppermute(last, axis, up)
        after = lax.ppermute(leading, axis, down)
        shard = jnp.concatenate([before, shard, after], axis=dim)
    return shard


def from_behind(value, axis, steps):
    count = lax.axis_size(axis)
    leading, last = (max(0, -steps), min(count, count - steps))
    return lax.ppermute(value, axis, [(source, source + steps) for source in range(leading, last)])


def offsets_for(frame_count):
    distances = [2, 3]
    power_step = 4
    while power_step < frame_count:
        distances.append(power_step)
        power_step = power_step * 2
    return [sign_value * distance_step for distance_step in distances for sign_value in (1, -1)]


def far_window(entries, is_valid):
    pair_start = jnp.maximum(entries[0], 0)
    pair_index = jnp.arange(2, dtype=jnp.int32)
    far_hit = (
        is_valid & (entries[:, None] >= 0) & (entries[:, None] - pair_start == pair_index[None, :])
    )
    far_hit = jnp.repeat(jnp.repeat(far_hit, BLK, axis=0), BLK, axis=1)
    return (pair_start, far_hit)


def attend_parts(queries, grads_out, keys_all, visible):
    score_scale = HD ** (-0.5)
    across = (((1,), (1,)), ((), ()))
    key_part = keys_all[:, :HD]
    value_part = keys_all[:, HD:]
    scores = (
        lax.dot_general(queries, key_part, across, preferred_element_type=jnp.float32) * score_scale
    )
    scores = jnp.where(visible, scores, -jnp.inf)
    row_max = jnp.max(scores, axis=1, keepdims=True)
    row_total = jnp.sum(jnp.exp(scores - row_max), axis=1, keepdims=True)
    log_total = row_max + jnp.log(row_total)
    weights = jnp.exp(scores - log_total).astype(jnp.bfloat16)
    out_rows = jnp.dot(weights, value_part, preferred_element_type=jnp.float32)
    row_delta = jnp.sum(out_rows * grads_out.astype(jnp.float32), axis=1, keepdims=True)
    dweights = lax.dot_general(grads_out, value_part, across, preferred_element_type=jnp.float32)
    dscores = (weights.astype(jnp.float32) * (dweights - row_delta)).astype(jnp.bfloat16)
    query_rows_grad = jnp.dot(dscores, key_part, preferred_element_type=jnp.float32) * score_scale
    return (out_rows, query_rows_grad, weights, dscores, log_total, row_delta)


def key_terms(weights, dscores, queries, grads_out):
    score_scale = HD ** (-0.5)
    over_rows = (((0,), (0,)), ((), ()))
    key_side = (
        lax.dot_general(dscores, queries, over_rows, preferred_element_type=jnp.float32)
        * score_scale
    )
    value_side = lax.dot_general(weights, grads_out, over_rows, preferred_element_type=jnp.float32)
    return jnp.concatenate([key_side, value_side], axis=1)


def shards(query_tokens, key_tokens, value_tokens, grad_out, far_block):
    tok_rows = query_tokens.shape[0]
    frame_count = lax.axis_size("seq")
    device = lax.axis_index("seq")
    offsets = offsets_for(frame_count)
    joined = jnp.concatenate([key_tokens, value_tokens], axis=1)
    near_keys = extended(joined, (("seq", 0),), tok_rows)
    neighbour = device + jnp.arange(3, dtype=jnp.int32) - 1
    near_ok = jnp.repeat((neighbour >= 0) & (neighbour < frame_count), tok_rows)
    pieces = [near_keys]
    mask_list = [jnp.broadcast_to(near_ok[None, :], (tok_rows, 3 * tok_rows))]
    sent_starts = []
    for offset in offsets:
        viewer = jnp.clip(device - offset, 0, frame_count - 1)
        sent_start = jnp.maximum(far_block[viewer, device, 0], 0)
        arrived = from_behind(joined, "seq", -offset)
        other_frame = device + offset
        is_valid = (other_frame >= 0) & (other_frame < frame_count)
        safe_frame = jnp.clip(other_frame, 0, frame_count - 1)
        entries = far_block[device, safe_frame]
        pair_start, far_hit = far_window(entries, is_valid)
        pieces.append(arrived)
        mask_list.append(far_hit)
        sent_starts.append(sent_start)
    keys_all = jnp.concatenate(pieces, axis=0)
    visible = jnp.concatenate(mask_list, axis=1)
    attention_out, query_grad, weights, dscores, log_total, row_delta = attend_parts(
        query_tokens, grad_out, keys_all, visible
    )
    near_terms = key_terms(
        weights[:, : 3 * tok_rows], dscores[:, : 3 * tok_rows], query_tokens, grad_out
    )
    from_after = from_behind(near_terms[:tok_rows], "seq", -1)
    from_before = from_behind(near_terms[2 * tok_rows :], "seq", 1)
    grad_total = near_terms[tok_rows : 2 * tok_rows] + from_after + from_before
    far_terms = key_terms(
        weights[:, 3 * tok_rows :], dscores[:, 3 * tok_rows :], query_tokens, grad_out
    )
    for slot_index in range(len(offsets)):
        first_row = slot_index * 2 * BLK
        grad_piece = far_terms[first_row : first_row + 2 * BLK]
        returned = from_behind(grad_piece, "seq", offsets[slot_index])
        current = grad_total
        grad_total = current + returned
    key_grad = grad_total[:, :HD]
    value_grad = grad_total[:, HD:]
    return (attention_out, query_grad, key_grad, value_grad)


def solution(mesh):
    return jax.shard_map(
        shards,
        mesh=mesh,
        in_specs=(P("seq", "head"), P("seq", "head"), P("seq", "head"), P("seq", "head"), P()),
        out_specs=(P("seq", "head"), P("seq", "head"), P("seq", "head"), P("seq", "head")),
        check_vma=False,
    )
```

profile of v0, /device:TPU:88, one launch (start us, length us, event | category | flops | bytes accessed | tf_op | source)
XLA Modules:
  0.0 229.3 jit_solution(11348308612695378627)
XLA Ops:
  2.5 5.0 %collective-permute-start.15 = (bf16[256,256]{1,0:T(8,128)(2,1)S(1)}, bf16[256,256]{1,0:T(8,128)(2,1)S(1)}, u32[]{:S(2)}, u32[]{:S(2)}) collective-permute-start(bf16[256,256]{1,0:T(8,128)(2,1)S(1)} %constant_dynamic-update-slice_fusion.14), channel_id=1, source_target_pairs={{0,256},{4,260},{8,264},{12,268},{16,272},{20,276},{24,280},{28,28... | collective-permute-start | bytes 393224 | tf_op jit(solution)/shard_map/ppermute | solution.py:26
  8.8 8.2 %collective-permute-start.13 = (bf16[256,256]{1,0:T(8,128)(2,1)S(1)}, bf16[256,256]{1,0:T(8,128)(2,1)S(1)}, u32[]{:S(2)}, u32[]{:S(2)}) collective-permute-start(bf16[256,256]{1,0:T(8,128)(2,1)S(1)} %constant_dynamic-update-slice_fusion.14), channel_id=1, source_target_pairs={{0,128},{4,132},{8,136},{12,140},{16,144},{20,148},{24,152},{28,15... | collective-permute-start | bytes 393224 | tf_op jit(solution)/shard_map/ppermute | solution.py:26
  43.5 9.7 %collective-permute-start.1 = (bf16[256,256]{1,0:T(8,128)(2,1)S(1)}, bf16[256,256]{1,0:T(8,128)(2,1)S(1)}, u32[]{:S(2)}, u32[]{:S(2)}) collective-permute-start(bf16[256,256]{1,0:T(8,128)(2,1)S(1)} %constant_dynamic-update-slice_fusion.14), channel_id=1, source_target_pairs={{4,0},{8,4},{12,8},{16,12},{20,16},{24,20},{28,24},{32,28},{36,32}... | collective-permute-start | bytes 393224 | tf_op jit(solution)/shard_map/ppermute | solution.py:18
  53.3 2.4 %collective-permute-done.1 = bf16[256,256]{1,0:T(8,128)(2,1)S(1)} collective-permute-done((bf16[256,256]{1,0:T(8,128)(2,1)S(1)}, bf16[256,256]{1,0:T(8,128)(2,1)S(1)}, u32[]{:S(2)}, u32[]{:S(2)}) %collective-permute-start.1) | collective-permute-done | bytes 131104 | tf_op jit(solution)/shard_map/ppermute | solution.py:18
  57.6 10.8 %collective-permute-start.4 = (bf16[256,256]{1,0:T(8,128)(2,1)S(1)}, bf16[256,256]{1,0:T(8,128)(2,1)S(1)}, u32[]{:S(2)}, u32[]{:S(2)}) collective-permute-start(bf16[256,256]{1,0:T(8,128)(2,1)S(1)} %constant_dynamic-update-slice_fusion.14), channel_id=1, source_target_pairs={{12,0},{16,4},{20,8},{24,12},{28,16},{32,20},{36,24},{40,28},{44,3... | collective-permute-start | bytes 393224 | tf_op jit(solution)/shard_map/ppermute | solution.py:26
  71.0 6.9 %collective-permute-start.6 = (bf16[256,256]{1,0:T(8,128)(2,1)S(1)}, bf16[256,256]{1,0:T(8,128)(2,1)S(1)}, u32[]{:S(2)}, u32[]{:S(2)}) collective-permute-start(bf16[256,256]{1,0:T(8,128)(2,1)S(1)} %constant_dynamic-update-slice_fusion.14), channel_id=1, source_target_pairs={{16,0},{20,4},{24,8},{28,12},{32,16},{36,20},{40,24},{44,28},{48,3... | collective-permute-start | bytes 393224 | tf_op jit(solution)/shard_map/ppermute | solution.py:26
  81.4 5.8 %collective-permute-start.8 = (bf16[256,256]{1,0:T(8,128)(2,1)S(1)}, bf16[256,256]{1,0:T(8,128)(2,1)S(1)}, u32[]{:S(2)}, u32[]{:S(2)}) collective-permute-start(bf16[256,256]{1,0:T(8,128)(2,1)S(1)} %constant_dynamic-update-slice_fusion.14), channel_id=1, source_target_pairs={{32,0},{36,4},{40,8},{44,12},{48,16},{52,20},{56,24},{60,28},{64,3... | collective-permute-start | bytes 393224 | tf_op jit(solution)/shard_map/ppermute | solution.py:26
  87.3 3.3 %collective-permute-done.7 = bf16[256,256]{1,0:T(8,128)(2,1)S(1)} collective-permute-done((bf16[256,256]{1,0:T(8,128)(2,1)S(1)}, bf16[256,256]{1,0:T(8,128)(2,1)S(1)}, u32[]{:S(2)}, u32[]{:S(2)}) %collective-permute-start.7) | collective-permute-done | bytes 131104 | tf_op jit(solution)/shard_map/ppermute | solution.py:26
  90.6 6.6 %collective-permute-start.9 = (bf16[256,256]{1,0:T(8,128)(2,1)S(1)}, bf16[256,256]{1,0:T(8,128)(2,1)S(1)}, u32[]{:S(2)}, u32[]{:S(2)}) collective-permute-start(bf16[256,256]{1,0:T(8,128)(2,1)S(1)} %constant_dynamic-update-slice_fusion.14), channel_id=1, source_target_pairs={{0,32},{4,36},{8,40},{12,44},{16,48},{20,52},{24,56},{28,60},{32,6... | collective-permute-start | bytes 393224 | tf_op jit(solution)/shard_map/ppermute | solution.py:26
  99.2 6.0 %collective-permute-done.9 = bf16[256,256]{1,0:T(8,128)(2,1)S(1)} collective-permute-done((bf16[256,256]{1,0:T(8,128)(2,1)S(1)}, bf16[256,256]{1,0:T(8,128)(2,1)S(1)}, u32[]{:S(2)}, u32[]{:S(2)}) %collective-permute-start.9) | collective-permute-done | bytes 131104 | tf_op jit(solution)/shard_map/ppermute | solution.py:26
  105.2 9.3 %collective-permute-start.11 = (bf16[256,256]{1,0:T(8,128)(2,1)S(1)}, bf16[256,256]{1,0:T(8,128)(2,1)S(1)}, u32[]{:S(2)}, u32[]{:S(2)}) collective-permute-start(bf16[256,256]{1,0:T(8,128)(2,1)S(1)} %constant_dynamic-update-slice_fusion.14), channel_id=1, source_target_pairs={{0,64},{4,68},{8,72},{12,76},{16,80},{20,84},{24,88},{28,92},{32,9... | collective-permute-start | bytes 393224 | tf_op jit(solution)/shard_map/ppermute | solution.py:26
  117.0 6.5 %collective-permute-done.12 = bf16[256,256]{1,0:T(8,128)(2,1)S(1)} collective-permute-done((bf16[256,256]{1,0:T(8,128)(2,1)S(1)}, bf16[256,256]{1,0:T(8,128)(2,1)S(1)}, u32[]{:S(2)}, u32[]{:S(2)}) %collective-permute-start.12) | collective-permute-done | bytes 131104 | tf_op jit(solution)/shard_map/ppermute | solution.py:26
  131.3 2.4 %collective-permute-start.17 = (f32[256,256]{0,1:T(8,128)S(1)}, f32[256,256]{0,1:T(8,128)}, u32[]{:S(2)}, u32[]{:S(2)}) collective-permute-start(f32[256,256]{0,1:T(8,128)S(1)} %get-tuple-element.51), channel_id=1, source_target_pairs={{0,4},{4,8},{8,12},{12,16},{16,20},{20,24},{24,28},{28,32},{32,36}... | collective-permute-start | bytes 786440 | tf_op jit(solution)/shard_map/ppermute | solution.py:26
  138.7 5.2 %collective-permute-start.29 = (f32[256,256]{0,1:T(8,128)S(1)}, f32[256,256]{0,1:T(8,128)}, u32[]{:S(2)}, u32[]{:S(2)}) collective-permute-start(f32[256,256]{0,1:T(8,128)S(1)} %get-tuple-element.47), channel_id=1, source_target_pairs={{128,0},{132,4},{136,8},{140,12},{144,16},{148,20},{152,24},{156,2... | collective-permute-start | bytes 786440 | tf_op jit(solution)/shard_map/ppermute | solution.py:26
  146.7 9.8 %collective-permute-start.30 = (f32[256,256]{0,1:T(8,128)}, f32[256,256]{0,1:T(8,128)}, u32[]{:S(2)}, u32[]{:S(2)}) collective-permute-start(f32[256,256]{0,1:T(8,128)} %get-tuple-element.49), channel_id=1, source_target_pairs={{0,256},{4,260},{8,264},{12,268},{16,272},{20,276},{24,280},{28,28... | collective-permute-start | bytes 786440 | tf_op jit(solution)/shard_map/ppermute | solution.py:26
  156.6 4.5 %collective-permute-start.18 = (f32[256,256]{0,1:T(8,128)}, f32[256,256]{0,1:T(8,128)}, u32[]{:S(2)}, u32[]{:S(2)}) collective-permute-start(f32[256,256]{0,1:T(8,128)} %get-tuple-element.36), channel_id=1, source_target_pairs={{0,8},{4,12},{8,16},{12,20},{16,24},{20,28},{24,32},{28,36},{32,40... | collective-permute-start | bytes 786440 | tf_op jit(solution)/shard_map/ppermute | solution.py:26
  161.1 7.9 %collective-permute-start.19 = (f32[256,256]{0,1:T(8,128)}, f32[256,256]{0,1:T(8,128)}, u32[]{:S(2)}, u32[]{:S(2)}) collective-permute-start(f32[256,256]{0,1:T(8,128)} %get-tuple-element.37), channel_id=1, source_target_pairs={{8,0},{12,4},{16,8},{20,12},{24,16},{28,20},{32,24},{36,28},{40,32... | collective-permute-start | bytes 786440 | tf_op jit(solution)/shard_map/ppermute | solution.py:26
  169.1 2.3 collective-permute-start.20
  171.4 6.3 %collective-permute-start.21 = (f32[256,256]{0,1:T(8,128)}, f32[256,256]{0,1:T(8,128)}, u32[]{:S(2)}, u32[]{:S(2)}) collective-permute-start(f32[256,256]{0,1:T(8,128)} %get-tuple-element.39), channel_id=1, source_target_pairs={{12,0},{16,4},{20,8},{24,12},{28,16},{32,20},{36,24},{40,28},{44,3... | collective-permute-start | bytes 786440 | tf_op jit(solution)/shard_map/ppermute | solution.py:26
  180.6 6.7 %collective-permute-start.23 = (f32[256,256]{0,1:T(8,128)}, f32[256,256]{0,1:T(8,128)S(1)}, u32[]{:S(2)}, u32[]{:S(2)}) collective-permute-start(f32[256,256]{0,1:T(8,128)} %get-tuple-element.41), channel_id=1, source_target_pairs={{16,0},{20,4},{24,8},{28,12},{32,16},{36,20},{40,24},{44,28},{48,3... | collective-permute-start | bytes 786440 | tf_op jit(solution)/shard_map/ppermute | solution.py:26
  189.2 8.7 %collective-permute-start.25 = (f32[256,256]{0,1:T(8,128)}, f32[256,256]{0,1:T(8,128)S(1)}, u32[]{:S(2)}, u32[]{:S(2)}) collective-permute-start(f32[256,256]{0,1:T(8,128)} %get-tuple-element.43), channel_id=1, source_target_pairs={{32,0},{36,4},{40,8},{44,12},{48,16},{52,20},{56,24},{60,28},{64,3... | collective-permute-start | bytes 786440 | tf_op jit(solution)/shard_map/ppermute | solution.py:26
  198.0 3.0 %collective-permute-start.26 = (f32[256,256]{0,1:T(8,128)}, f32[256,256]{0,1:T(8,128)S(1)}, u32[]{:S(2)}, u32[]{:S(2)}) collective-permute-start(f32[256,256]{0,1:T(8,128)} %get-tuple-element.44), channel_id=1, source_target_pairs={{0,64},{4,68},{8,72},{12,76},{16,80},{20,84},{24,88},{28,92},{32,9... | collective-permute-start | bytes 786440 | tf_op jit(solution)/shard_map/ppermute | solution.py:26
  201.0 2.7 %convolution_multiply_fusion.3 = f32[256,128]{1,0:T(8,128)} fusion(bf16[256,4352]{0,1:T(8,128)(2,1)S(1)} %fusion.4, bf16[4352,256]{1,0:T(8,128)(2,1)} %copy-done.2), kind=kOutput, calls=%fused_computation.40 | convolution fusion | flops 285245440 | bytes 3473408 | tf_op jit(solution)/shard_map/dot_general | solution.py:65
  203.7 22.0 %collective-permute-done.24 = f32[256,256]{0,1:T(8,128)S(1)} collective-permute-done((f32[256,256]{0,1:T(8,128)}, f32[256,256]{0,1:T(8,128)S(1)}, u32[]{:S(2)}, u32[]{:S(2)}) %collective-permute-start.24) | collective-permute-done | bytes 262176 | tf_op jit(solution)/shard_map/ppermute | solution.py:26
  (187 shorter events, 56.4 us)
Async XLA Ops:
  2.5 121.2 %collective-permute-start.15 = (bf16[256,256]{1,0:T(8,128)(2,1)S(1)}, bf16[256,256]{1,0:T(8,128)(2,1)S(1)}, u32[]{:S(2)}, u32[]{:S(2)}) collective-permute-start(bf16[256,256]{1,0:T(8,128)(2,1)S(1)} %constant_dynamic-update-slice_fusion.14), channel_id=1, source_target_pairs={{0,256},{4,260},{8,264},{12,268},{16,272},{20,276},{24,280},{28,28... | collective-permute-start | bytes 393224 | tf_op jit(solution)/shard_map/ppermute | solution.py:26
  7.5 116.1 %collective-permute-start.14 = (bf16[256,256]{1,0:T(8,128)(2,1)S(1)}, bf16[256,256]{1,0:T(8,128)(2,1)S(1)}, u32[]{:S(2)}, u32[]{:S(2)}) collective-permute-start(bf16[256,256]{1,0:T(8,128)(2,1)S(1)} %constant_dynamic-update-slice_fusion.14), channel_id=1, source_target_pairs={{256,0},{260,4},{264,8},{268,12},{272,16},{276,20},{280,24},{284,2... | collective-permute-start | bytes 393224 | tf_op jit(solution)/shard_map/ppermute | solution.py:26
  8.8 114.8 %collective-permute-start.13 = (bf16[256,256]{1,0:T(8,128)(2,1)S(1)}, bf16[256,256]{1,0:T(8,128)(2,1)S(1)}, u32[]{:S(2)}, u32[]{:S(2)}) collective-permute-start(bf16[256,256]{1,0:T(8,128)(2,1)S(1)} %constant_dynamic-update-slice_fusion.14), channel_id=1, source_target_pairs={{0,128},{4,132},{8,136},{12,140},{16,144},{20,148},{24,152},{28,15... | collective-permute-start | bytes 393224 | tf_op jit(solution)/shard_map/ppermute | solution.py:26
  17.0 40.6 %collective-permute-start.2 = (bf16[256,256]{1,0:T(8,128)(2,1)S(1)}, bf16[256,256]{1,0:T(8,128)(2,1)S(1)}, u32[]{:S(2)}, u32[]{:S(2)}) collective-permute-start(bf16[256,256]{1,0:T(8,128)(2,1)S(1)} %constant_dynamic-update-slice_fusion.14), channel_id=1, source_target_pairs={{8,0},{12,4},{16,8},{20,12},{24,16},{28,20},{32,24},{36,28},{40,32... | collective-permute-start | bytes 393224 | tf_op jit(solution)/shard_map/ppermute | solution.py:26
  19.0 24.5 %collective-permute-start = (bf16[256,256]{1,0:T(8,128)(2,1)S(1)}, bf16[256,256]{1,0:T(8,128)(2,1)S(1)}, u32[]{:S(2)}, u32[]{:S(2)}) collective-permute-start(bf16[256,256]{1,0:T(8,128)(2,1)S(1)} %constant_dynamic-update-slice_fusion.14), channel_id=1, source_target_pairs={{0,4},{4,8},{8,12},{12,16},{16,20},{20,24},{24,28},{28,32},{32,36}... | collective-permute-start | bytes 393224 | tf_op jit(solution)/shard_map/ppermute | solution.py:17
  81.4 15.8 %collective-permute-start.8 = (bf16[256,256]{1,0:T(8,128)(2,1)S(1)}, bf16[256,256]{1,0:T(8,128)(2,1)S(1)}, u32[]{:S(2)}, u32[]{:S(2)}) collective-permute-start(bf16[256,256]{1,0:T(8,128)(2,1)S(1)} %constant_dynamic-update-slice_fusion.14), channel_id=1, source_target_pairs={{32,0},{36,4},{40,8},{44,12},{48,16},{52,20},{56,24},{60,28},{64,3... | collective-permute-start | bytes 393224 | tf_op jit(solution)/shard_map/ppermute | solution.py:26
  90.6 14.6 %collective-permute-start.9 = (bf16[256,256]{1,0:T(8,128)(2,1)S(1)}, bf16[256,256]{1,0:T(8,128)(2,1)S(1)}, u32[]{:S(2)}, u32[]{:S(2)}) collective-permute-start(bf16[256,256]{1,0:T(8,128)(2,1)S(1)} %constant_dynamic-update-slice_fusion.14), channel_id=1, source_target_pairs={{0,32},{4,36},{8,40},{12,44},{16,48},{20,52},{24,56},{28,60},{32,6... | collective-permute-start | bytes 393224 | tf_op jit(solution)/shard_map/ppermute | solution.py:26
  97.3 17.2 %collective-permute-start.10 = (bf16[256,256]{1,0:T(8,128)(2,1)S(1)}, bf16[256,256]{1,0:T(8,128)(2,1)S(1)}, u32[]{:S(2)}, u32[]{:S(2)}) collective-permute-start(bf16[256,256]{1,0:T(8,128)(2,1)S(1)} %constant_dynamic-update-slice_fusion.14), channel_id=1, source_target_pairs={{64,0},{68,4},{72,8},{76,12},{80,16},{84,20},{88,24},{92,28},{96,3... | collective-permute-start | bytes 393224 | tf_op jit(solution)/shard_map/ppermute | solution.py:26
  128.7 15.3 %collective-permute-start.16 = (f32[256,256]{0,1:T(8,128)S(1)}, f32[256,256]{0,1:T(8,128)S(1)}, u32[]{:S(2)}, u32[]{:S(2)}) collective-permute-start(f32[256,256]{0,1:T(8,128)S(1)} %get-tuple-element.50), channel_id=1, source_target_pairs={{4,0},{8,4},{12,8},{16,12},{20,16},{24,20},{28,24},{32,28},{36,32}... | collective-permute-start | bytes 786440 | tf_op jit(solution)/shard_map/ppermute | solution.py:26
  131.3 15.4 %collective-permute-start.17 = (f32[256,256]{0,1:T(8,128)S(1)}, f32[256,256]{0,1:T(8,128)}, u32[]{:S(2)}, u32[]{:S(2)}) collective-permute-start(f32[256,256]{0,1:T(8,128)S(1)} %get-tuple-element.51), channel_id=1, source_target_pairs={{0,4},{4,8},{8,12},{12,16},{16,20},{20,24},{24,28},{28,32},{32,36}... | collective-permute-start | bytes 786440 | tf_op jit(solution)/shard_map/ppermute | solution.py:26
  134.6 22.0 %collective-permute-start.27 = (f32[256,256]{0,1:T(8,128)S(1)}, f32[256,256]{0,1:T(8,128)}, u32[]{:S(2)}, u32[]{:S(2)}) collective-permute-start(f32[256,256]{0,1:T(8,128)S(1)} %get-tuple-element.45), channel_id=1, source_target_pairs={{64,0},{68,4},{72,8},{76,12},{80,16},{84,20},{88,24},{92,28},{96,3... | collective-permute-start | bytes 786440 | tf_op jit(solution)/shard_map/ppermute | solution.py:26
  136.5 24.6 %collective-permute-start.28 = (f32[256,256]{0,1:T(8,128)S(1)}, f32[256,256]{0,1:T(8,128)}, u32[]{:S(2)}, u32[]{:S(2)}) collective-permute-start(f32[256,256]{0,1:T(8,128)S(1)} %get-tuple-element.46), channel_id=1, source_target_pairs={{0,128},{4,132},{8,136},{12,140},{16,144},{20,148},{24,152},{28,15... | collective-permute-start | bytes 786440 | tf_op jit(solution)/shard_map/ppermute | solution.py:26
  138.7 30.3 %collective-permute-start.29 = (f32[256,256]{0,1:T(8,128)S(1)}, f32[256,256]{0,1:T(8,128)}, u32[]{:S(2)}, u32[]{:S(2)}) collective-permute-start(f32[256,256]{0,1:T(8,128)S(1)} %get-tuple-element.47), channel_id=1, source_target_pairs={{128,0},{132,4},{136,8},{140,12},{144,16},{148,20},{152,24},{156,2... | collective-permute-start | bytes 786440 | tf_op jit(solution)/shard_map/ppermute | solution.py:26
  144.0 27.4 %collective-permute-start.31 = (f32[256,256]{0,1:T(8,128)S(1)}, f32[256,256]{0,1:T(8,128)}, u32[]{:S(2)}, u32[]{:S(2)}) collective-permute-start(f32[256,256]{0,1:T(8,128)S(1)} %get-tuple-element.48), channel_id=1, source_target_pairs={{256,0},{260,4},{264,8},{268,12},{272,16},{276,20},{280,24},{284,2... | collective-permute-start | bytes 786440 | tf_op jit(solution)/shard_map/ppermute | solution.py:26
  146.7 31.7 %collective-permute-start.30 = (f32[256,256]{0,1:T(8,128)}, f32[256,256]{0,1:T(8,128)}, u32[]{:S(2)}, u32[]{:S(2)}) collective-permute-start(f32[256,256]{0,1:T(8,128)} %get-tuple-element.49), channel_id=1, source_target_pairs={{0,256},{4,260},{8,264},{12,268},{16,272},{20,276},{24,280},{28,28... | collective-permute-start | bytes 786440 | tf_op jit(solution)/shard_map/ppermute | solution.py:26
  156.6 24.0 %collective-permute-start.18 = (f32[256,256]{0,1:T(8,128)}, f32[256,256]{0,1:T(8,128)}, u32[]{:S(2)}, u32[]{:S(2)}) collective-permute-start(f32[256,256]{0,1:T(8,128)} %get-tuple-element.36), channel_id=1, source_target_pairs={{0,8},{4,12},{8,16},{12,20},{16,24},{20,28},{24,32},{28,36},{32,40... | collective-permute-start | bytes 786440 | tf_op jit(solution)/shard_map/ppermute | solution.py:26
  161.1 26.2 %collective-permute-start.19 = (f32[256,256]{0,1:T(8,128)}, f32[256,256]{0,1:T(8,128)}, u32[]{:S(2)}, u32[]{:S(2)}) collective-permute-start(f32[256,256]{0,1:T(8,128)} %get-tuple-element.37), channel_id=1, source_target_pairs={{8,0},{12,4},{16,8},{20,12},{24,16},{28,20},{32,24},{36,28},{40,32... | collective-permute-start | bytes 786440 | tf_op jit(solution)/shard_map/ppermute | solution.py:26
  169.1 20.2 %collective-permute-start.20 = (f32[256,256]{0,1:T(8,128)}, f32[256,256]{0,1:T(8,128)}, u32[]{:S(2)}, u32[]{:S(2)}) collective-permute-start(f32[256,256]{0,1:T(8,128)} %get-tuple-element.38), channel_id=1, source_target_pairs={{0,12},{4,16},{8,20},{12,24},{16,28},{20,32},{24,36},{28,40},{32,4... | collective-permute-start | bytes 786440 | tf_op jit(solution)/shard_map/ppermute | solution.py:26
  171.4 26.6 %collective-permute-start.21 = (f32[256,256]{0,1:T(8,128)}, f32[256,256]{0,1:T(8,128)}, u32[]{:S(2)}, u32[]{:S(2)}) collective-permute-start(f32[256,256]{0,1:T(8,128)} %get-tuple-element.39), channel_id=1, source_target_pairs={{12,0},{16,4},{20,8},{24,12},{28,16},{32,20},{36,24},{40,28},{44,3... | collective-permute-start | bytes 786440 | tf_op jit(solution)/shard_map/ppermute | solution.py:26
  178.4 25.3 %collective-permute-start.22 = (f32[256,256]{0,1:T(8,128)}, f32[256,256]{0,1:T(8,128)S(1)}, u32[]{:S(2)}, u32[]{:S(2)}) collective-permute-start(f32[256,256]{0,1:T(8,128)} %get-tuple-element.40), channel_id=1, source_target_pairs={{0,16},{4,20},{8,24},{12,28},{16,32},{20,36},{24,40},{28,44},{32,4... | collective-permute-start | bytes 786440 | tf_op jit(solution)/shard_map/ppermute | solution.py:26
  180.6 23.1 %collective-permute-start.23 = (f32[256,256]{0,1:T(8,128)}, f32[256,256]{0,1:T(8,128)S(1)}, u32[]{:S(2)}, u32[]{:S(2)}) collective-permute-start(f32[256,256]{0,1:T(8,128)} %get-tuple-element.41), channel_id=1, source_target_pairs={{16,0},{20,4},{24,8},{28,12},{32,16},{36,20},{40,24},{44,28},{48,3... | collective-permute-start | bytes 786440 | tf_op jit(solution)/shard_map/ppermute | solution.py:26
  187.3 38.3 %collective-permute-start.24 = (f32[256,256]{0,1:T(8,128)}, f32[256,256]{0,1:T(8,128)S(1)}, u32[]{:S(2)}, u32[]{:S(2)}) collective-permute-start(f32[256,256]{0,1:T(8,128)} %get-tuple-element.42), channel_id=1, source_target_pairs={{0,32},{4,36},{8,40},{12,44},{16,48},{20,52},{24,56},{28,60},{32,6... | collective-permute-start | bytes 786440 | tf_op jit(solution)/shard_map/ppermute | solution.py:26
  189.2 36.4 %collective-permute-start.25 = (f32[256,256]{0,1:T(8,128)}, f32[256,256]{0,1:T(8,128)S(1)}, u32[]{:S(2)}, u32[]{:S(2)}) collective-permute-start(f32[256,256]{0,1:T(8,128)} %get-tuple-element.43), channel_id=1, source_target_pairs={{32,0},{36,4},{40,8},{44,12},{48,16},{52,20},{56,24},{60,28},{64,3... | collective-permute-start | bytes 786440 | tf_op jit(solution)/shard_map/ppermute | solution.py:26
  198.0 27.7 %collective-permute-start.26 = (f32[256,256]{0,1:T(8,128)}, f32[256,256]{0,1:T(8,128)S(1)}, u32[]{:S(2)}, u32[]{:S(2)}) collective-permute-start(f32[256,256]{0,1:T(8,128)} %get-tuple-element.44), channel_id=1, source_target_pairs={{0,64},{4,68},{8,72},{12,76},{16,80},{20,84},{24,88},{28,92},{32,9... | collective-permute-start | bytes 786440 | tf_op jit(solution)/shard_map/ppermute | solution.py:26
  (13 other events, 366.4 us)
where the time goes:
time: 231 us; the launch traced here: 229 us
  starting transfers between devices  146 us (63%)
  waiting for transfers between devices  42.9 us (19%)
  local copies, waits for them, and re-layouts  13.9 us (6%)
  between operations  10.6 us (5%)
  other arithmetic  9.28 us (4%)
  matrix products  7.08 us (3%)
    ppermute x30, starting transfers between devices, from_behind(): lax.ppermute(value, axis, [(source, source + steps) for source in range(l...  134 us
    ppermute x30, waiting for transfers between devices, from_behind(): lax.ppermute(value, axis, [(source, source + steps) for source in range(l...  40.4 us
    ppermute x1, starting transfers between devices, extended(): after = lax.ppermute(leading, axis, down)  9.69 us
    slice x14, local copies, waits for them, and re-layouts, far_window(): pair_start = jnp.maximum(entries[0], 0)  7.31 us
    unnamed x74, local copies, waits for them, and re-layouts  5.23 us
  transfers between devices with their start and end apart: 32, of which 9 were waited for; matrix products, arithmetic and copies ran while one was open for 9% of the time, Pallas kernels for 0%

commit v1 on v0

v1 whole, which is shorter than its diff:
```python
import jax
import jax.numpy as jnp
from jax import lax
from jax.sharding import PartitionSpec as P

HD = 128
BLK = 128


def offsets_for(frame_count):
    distances = [2, 3]
    power_step = 4
    while power_step < frame_count:
        distances.append(power_step)
        power_step = power_step * 2
    return [sign_value * distance_step for distance_step in distances for sign_value in (1, -1)]


def pieces_for(frame_count):
    half = frame_count // 2
    near = [(1, False), (-1, False)]
    far = []
    for offset in offsets_for(frame_count):
        if abs(offset) == half:
            if offset > 0:
                far.append((half, True))
        else:
            far.append((offset, False))
    return near, far


def receive(value, axis, shift, wrap):
    count = lax.axis_size(axis)
    if wrap:
        pairs = [(source, (source - shift) % count) for source in range(count)]
    else:
        pairs = [(source, source - shift) for source in range(count) if 0 <= source - shift < count]
    return lax.ppermute(value, axis, pairs)


def other_frame(device, shift, wrap, count):
    if wrap:
        return (device + shift) % count
    return device + shift


def shards(query_tokens, key_tokens, value_tokens, grad_out, far_block):
    rows = query_tokens.shape[0]
    blocks = rows // BLK
    count = lax.axis_size("seq")
    device = lax.axis_index("seq")
    scale = HD ** (-0.5)
    across = (((1,), (1,)), ((), ()))
    over_rows = (((0,), (0,)), ((), ()))
    near, far = pieces_for(count)

    pack = jnp.concatenate([key_tokens, value_tokens, query_tokens, grad_out], axis=1)
    got_near = [receive(pack, "seq", s, w) for s, w in near]
    got_far = [receive(pack, "seq", s, w) for s, w in far]

    near_frames = [other_frame(device, s, w, count) for s, w in near]
    far_frames = [other_frame(device, s, w, count) for s, w in far]
    near_ok = [(g >= 0) & (g < count) for g in near_frames]
    far_seen = []
    for g in far_frames:
        inside = (g >= 0) & (g < count)
        entries = far_block[device, jnp.clip(g, 0, count - 1)]
        far_seen.append([inside & (entries[b] >= 0) for b in range(blocks)])

    near_k = [key_tokens] + [p[:, :HD] for p in got_near]
    near_v = [value_tokens] + [p[:, HD : 2 * HD] for p in got_near]
    near_mask = [jnp.bool_(True)] + near_ok
    kn = jnp.concatenate(near_k, axis=0)
    vn = jnp.concatenate(near_v, axis=0)
    near_cols = jnp.concatenate(
        [jnp.broadcast_to(m, (rows,)) for m in near_mask], axis=0
    )

    outs, dqs, stats = [], [], []
    self_dk, self_dv = [], []
    for b in range(blocks):
        rs = slice(b * BLK, (b + 1) * BLK)
        qb = query_tokens[rs]
        dob = grad_out[rs]
        kf = jnp.concatenate([p[rs, :HD] for p in got_far], axis=0)
        vf = jnp.concatenate([p[rs, HD : 2 * HD] for p in got_far], axis=0)
        far_cols = jnp.concatenate(
            [jnp.broadcast_to(far_seen[i][b], (BLK,)) for i in range(len(far))], axis=0
        )
        k_all = jnp.concatenate([kn, kf], axis=0)
        v_all = jnp.concatenate([vn, vf], axis=0)
        cols = jnp.concatenate([near_cols, far_cols], axis=0)
        s = lax.dot_general(qb, k_all, across, preferred_element_type=jnp.float32) * scale
        s = jnp.where(cols[None, :], s, -jnp.inf)
        m = jnp.max(s, axis=1, keepdims=True)
        total = jnp.sum(jnp.exp(s - m), axis=1, keepdims=True)
        lse = m + jnp.log(total)
        w = jnp.exp(s - lse).astype(jnp.bfloat16)
        o = jnp.dot(w, v_all, preferred_element_type=jnp.float32)
        delta = jnp.sum(o * dob.astype(jnp.float32), axis=1, keepdims=True)
        dw = lax.dot_general(dob, v_all, across, preferred_element_type=jnp.float32)
        ds = (w.astype(jnp.float32) * (dw - delta)).astype(jnp.bfloat16)
        dq = jnp.dot(ds, k_all, preferred_element_type=jnp.float32) * scale
        outs.append(o)
        dqs.append(dq)
        stats.append(jnp.concatenate([lse[:, 0], delta[:, 0]], axis=0))
        self_dk.append(
            lax.dot_general(ds[:, :rows], qb, over_rows, preferred_element_type=jnp.float32)
        )
        self_dv.append(
            lax.dot_general(w[:, :rows], dob, over_rows, preferred_element_type=jnp.float32)
        )

    attention_out = jnp.concatenate(outs, axis=0)
    query_grad = jnp.concatenate(dqs, axis=0)
    stat_pack = jnp.concatenate(stats, axis=0).reshape(2 * blocks, BLK)
    stat_pack = jnp.concatenate(
        [stat_pack, jnp.zeros((8 - 2 * blocks, BLK), jnp.float32)], axis=0
    )

    got_near_stats = [receive(stat_pack, "seq", s, w) for s, w in near]
    got_far_stats = [receive(stat_pack, "seq", s, w) for s, w in far]

    dk_total = jnp.stack(self_dk, axis=0).sum(axis=0) * scale
    dv_total = jnp.stack(self_dv, axis=0).sum(axis=0)

    def key_terms(q_v, do_v, lse_v, delta_v, k_g, v_g, seen):
        s = lax.dot_general(q_v, k_g, across, preferred_element_type=jnp.float32) * scale
        s = jnp.where(seen, s, -jnp.inf)
        w = jnp.exp(s - lse_v[:, None]).astype(jnp.bfloat16)
        dw = lax.dot_general(do_v, v_g, across, preferred_element_type=jnp.float32)
        ds = (w.astype(jnp.float32) * (dw - delta_v[:, None])).astype(jnp.bfloat16)
        dk = lax.dot_general(ds, q_v, over_rows, preferred_element_type=jnp.float32)
        dv = lax.dot_general(w, do_v, over_rows, preferred_element_type=jnp.float32)
        return dk, dv

    def stat_rows(st):
        lse_v = jnp.concatenate([st[2 * b] for b in range(blocks)], axis=0)
        delta_v = jnp.concatenate([st[2 * b + 1] for b in range(blocks)], axis=0)
        return lse_v, delta_v

    for i in range(len(near)):
        p = got_near[i]
        lse_v, delta_v = stat_rows(got_near_stats[i])
        dk, dv = key_terms(
            p[:, 2 * HD : 3 * HD], p[:, 3 * HD :], lse_v, delta_v, key_tokens, value_tokens, near_ok[i]
        )
        dk_total = dk_total + dk * scale
        dv_total = dv_total + dv

    for i, (shift, wrap) in enumerate(far):
        p = got_far[i]
        st = got_far_stats[i]
        f = far_frames[i]
        inside = (f >= 0) & (f < count)
        entries = far_block[jnp.clip(f, 0, count - 1), device]
        dk_parts, dv_parts = [], []
        for b in range(blocks):
            rs = slice(b * BLK, (b + 1) * BLK)
            seen = inside & (entries[b] >= 0)
            dk, dv = key_terms(
                p[rs, 2 * HD : 3 * HD],
                p[rs, 3 * HD :],
                st[2 * b],
                st[2 * b + 1],
                key_tokens[rs],
                value_tokens[rs],
                seen,
            )
            dk_parts.append(dk)
            dv_parts.append(dv)
        dk_total = dk_total + jnp.concatenate(dk_parts, axis=0) * scale
        dv_total = dv_total + jnp.concatenate(dv_parts, axis=0)

    return (attention_out, query_grad, dk_total, dv_total)


def solution(mesh):
    return jax.shard_map(
        shards,
        mesh=mesh,
        in_specs=(P("seq", "head"), P("seq", "head"), P("seq", "head"), P("seq", "head"), P()),
        out_specs=(P("seq", "head"), P("seq", "head"), P("seq", "head"), P("seq", "head")),
        check_vma=False,
    )
```

time: 231 us -> 290 us (1.26)
  the two profiles are of different devices: /device:TPU:88 before, /device:TPU:1 now
where the time goes in v1:
time: 290 us; the launch traced here: 286 us
  starting transfers between devices  135 us (47%)
  matrix products  55.2 us (19%)
  between operations  34.6 us (12%)
  local copies, waits for them, and re-layouts  34 us (12%)
  waiting for transfers between devices  25 us (9%)
    ppermute x30, starting transfers between devices, receive(): return lax.ppermute(value, axis, pairs)  135 us
    ppermute x30, waiting for transfers between devices, receive(): return lax.ppermute(value, axis, pairs)  25 us
    dot_general x28, matrix products, key_terms(): dv = lax.dot_general(w, do_v, over_rows, preferred_element_type=jnp.float32)  22.5 us
    dot_general x28, matrix products, key_terms(): lax.dot_general(q_v, k_g, across, preferred_element_type=jnp.float32)  15.3 us
    dot_general x28, matrix products, key_terms(): dk = lax.dot_general(ds, q_v, over_rows, preferred_element_type=jnp.float32)  13.6 us
    unnamed x100, local copies, waits for them, and re-layouts  12.8 us
    sub x13, local copies, waits for them, and re-layouts, key_terms(): ds = (w.astype(jnp.float32) * (dw - delta_v[:, None])).astype(jnp.bfloat16)  10.1 us
  transfers between devices with their start and end apart: 30, of which 3 were waited for; matrix products, arithmetic and copies ran while one was open for 27% of the time, Pallas kernels for 0%

profile of v1, /device:TPU:1, one launch (start us, length us, event | category | flops | bytes accessed | tf_op | source)
XLA Modules:
  0.0 285.9 jit_solution(11286509994604781394)
XLA Ops:
  6.6 8.8 %collective-permute-start = (bf16[256,512]{1,0:T(8,128)(2,1)}, bf16[256,512]{1,0:T(8,128)(2,1)S(1)}, u32[]{:S(2)}, u32[]{:S(2)}) collective-permute-start(bf16[256,512]{1,0:T(8,128)(2,1)} %constant_dynamic-update-slice_fusion), channel_id=1, source_target_pairs={{4,0},{8,4},{12,8},{16,12},{20,16},{24,20},{28,24},{32,28},{36,32}... | collective-permute-start | bytes 786440 | tf_op jit(solution)/shard_map/ppermute | solution.py:38
  15.4 1.9 collective-permute-start.1
  18.6 4.0 %collective-permute-start.3 = (bf16[256,512]{1,0:T(8,128)(2,1)}, bf16[256,512]{1,0:T(8,128)(2,1)S(1)}, u32[]{:S(2)}, u32[]{:S(2)}) collective-permute-start(bf16[256,512]{1,0:T(8,128)(2,1)} %constant_dynamic-update-slice_fusion), channel_id=1, source_target_pairs={{0,8},{4,12},{8,16},{12,20},{16,24},{20,28},{24,32},{28,36},{32,40... | collective-permute-start | bytes 786440 | tf_op jit(solution)/shard_map/ppermute | solution.py:38
  73.2 5.2 %collective-permute-start.5 = (bf16[256,512]{1,0:T(8,128)(2,1)}, bf16[256,512]{1,0:T(8,128)(2,1)S(1)}, u32[]{:S(2)}, u32[]{:S(2)}) collective-permute-start(bf16[256,512]{1,0:T(8,128)(2,1)} %constant_dynamic-update-slice_fusion), channel_id=1, source_target_pairs={{0,12},{4,16},{8,20},{12,24},{16,28},{20,32},{24,36},{28,40},{32,4... | collective-permute-start | bytes 786440 | tf_op jit(solution)/shard_map/ppermute | solution.py:38
  79.9 6.1 %collective-permute-start.7 = (bf16[256,512]{1,0:T(8,128)(2,1)}, bf16[256,512]{1,0:T(8,128)(2,1)S(1)}, u32[]{:S(2)}, u32[]{:S(2)}) collective-permute-start(bf16[256,512]{1,0:T(8,128)(2,1)} %constant_dynamic-update-slice_fusion), channel_id=1, source_target_pairs={{0,16},{4,20},{8,24},{12,28},{16,32},{20,36},{24,40},{28,44},{32,4... | collective-permute-start | bytes 786440 | tf_op jit(solution)/shard_map/ppermute | solution.py:38
  87.4 9.4 %collective-permute-start.9 = (bf16[256,512]{1,0:T(8,128)(2,1)}, bf16[256,512]{1,0:T(8,128)(2,1)S(1)}, u32[]{:S(2)}, u32[]{:S(2)}) collective-permute-start(bf16[256,512]{1,0:T(8,128)(2,1)} %constant_dynamic-update-slice_fusion), channel_id=1, source_target_pairs={{0,32},{4,36},{8,40},{12,44},{16,48},{20,52},{24,56},{28,60},{32,6... | collective-permute-start | bytes 786440 | tf_op jit(solution)/shard_map/ppermute | solution.py:38
  99.8 5.5 %collective-permute-start.11 = (bf16[256,512]{1,0:T(8,128)(2,1)}, bf16[256,512]{1,0:T(8,128)(2,1)S(1)}, u32[]{:S(2)}, u32[]{:S(2)}) collective-permute-start(bf16[256,512]{1,0:T(8,128)(2,1)} %constant_dynamic-update-slice_fusion), channel_id=1, source_target_pairs={{0,64},{4,68},{8,72},{12,76},{16,80},{20,84},{24,88},{28,92},{32,9... | collective-permute-start | bytes 786440 | tf_op jit(solution)/shard_map/ppermute | solution.py:38
  106.7 9.1 %collective-permute-done.8 = bf16[256,512]{1,0:T(8,128)(2,1)S(1)} collective-permute-done((bf16[256,512]{1,0:T(8,128)(2,1)}, bf16[256,512]{1,0:T(8,128)(2,1)S(1)}, u32[]{:S(2)}, u32[]{:S(2)}) %collective-permute-start.8) | collective-permute-done | bytes 262176 | tf_op jit(solution)/shard_map/ppermute | solution.py:38
  115.8 16.0 %collective-permute-start.13 = (bf16[256,512]{1,0:T(8,128)(2,1)}, bf16[256,512]{1,0:T(8,128)(2,1)S(1)}, u32[]{:S(2)}, u32[]{:S(2)}) collective-permute-start(bf16[256,512]{1,0:T(8,128)(2,1)} %constant_dynamic-update-slice_fusion), channel_id=1, source_target_pairs={{0,128},{4,132},{8,136},{12,140},{16,144},{20,148},{24,152},{28,15... | collective-permute-start | bytes 786440 | tf_op jit(solution)/shard_map/ppermute | solution.py:38
  131.9 8.0 %collective-permute-start.14 = (bf16[256,512]{1,0:T(8,128)(2,1)}, bf16[256,512]{1,0:T(8,128)(2,1)S(1)}, u32[]{:S(2)}, u32[]{:S(2)}) collective-permute-start(bf16[256,512]{1,0:T(8,128)(2,1)} %constant_dynamic-update-slice_fusion), channel_id=1, source_target_pairs={{0,256},{4,260},{8,264},{12,268},{16,272},{20,276},{24,280},{28,28... | collective-permute-start | bytes 786440 | tf_op jit(solution)/shard_map/ppermute | solution.py:38
  140.1 14.3 %collective-permute-done.14 = bf16[256,512]{1,0:T(8,128)(2,1)S(1)} collective-permute-done((bf16[256,512]{1,0:T(8,128)(2,1)}, bf16[256,512]{1,0:T(8,128)(2,1)S(1)}, u32[]{:S(2)}, u32[]{:S(2)}) %collective-permute-start.14) | collective-permute-done | bytes 262176 | tf_op jit(solution)/shard_map/ppermute | solution.py:38
  159.0 1.9 collective-permute-start.16
  160.9 2.4 collective-permute-start.15
  164.6 9.3 %collective-permute-start.18 = (f32[8,128]{1,0:T(8,128)S(1)}, f32[8,128]{1,0:T(8,128)}, u32[]{:S(2)}, u32[]{:S(2)}) collective-permute-start(f32[8,128]{1,0:T(8,128)S(1)} %concatenate.142), channel_id=1, source_target_pairs={{0,8},{4,12},{8,16},{12,20},{16,24},{20,28},{24,32},{28,36},{32,40... | collective-permute-start | bytes 12296 | tf_op jit(solution)/shard_map/ppermute | solution.py:38
  177.7 5.8 %collective-permute-start.20 = (f32[8,128]{1,0:T(8,128)S(1)}, f32[8,128]{1,0:T(8,128)}, u32[]{:S(2)}, u32[]{:S(2)}) collective-permute-start(f32[8,128]{1,0:T(8,128)S(1)} %concatenate.142), channel_id=1, source_target_pairs={{0,12},{4,16},{8,20},{12,24},{16,28},{20,32},{24,36},{28,40},{32,4... | collective-permute-start | bytes 12296 | tf_op jit(solution)/shard_map/ppermute | solution.py:38
  186.0 5.5 %collective-permute-start.22 = (f32[8,128]{1,0:T(8,128)S(1)}, f32[8,128]{1,0:T(8,128)}, u32[]{:S(2)}, u32[]{:S(2)}) collective-permute-start(f32[8,128]{1,0:T(8,128)S(1)} %concatenate.142), channel_id=1, source_target_pairs={{0,16},{4,20},{8,24},{12,28},{16,32},{20,36},{24,40},{28,44},{32,4... | collective-permute-start | bytes 12296 | tf_op jit(solution)/shard_map/ppermute | solution.py:38
  198.9 8.5 %collective-permute-start.24 = (f32[8,128]{1,0:T(8,128)S(1)}, f32[8,128]{1,0:T(8,128)}, u32[]{:S(2)}, u32[]{:S(2)}) collective-permute-start(f32[8,128]{1,0:T(8,128)S(1)} %concatenate.142), channel_id=1, source_target_pairs={{0,32},{4,36},{8,40},{12,44},{16,48},{20,52},{24,56},{28,60},{32,6... | collective-permute-start | bytes 12296 | tf_op jit(solution)/shard_map/ppermute | solution.py:38
  215.6 6.2 %collective-permute-start.26 = (f32[8,128]{1,0:T(8,128)S(1)}, f32[8,128]{1,0:T(8,128)}, u32[]{:S(2)}, u32[]{:S(2)}) collective-permute-start(f32[8,128]{1,0:T(8,128)S(1)} %concatenate.142), channel_id=1, source_target_pairs={{0,64},{4,68},{8,72},{12,76},{16,80},{20,84},{24,88},{28,92},{32,9... | collective-permute-start | bytes 12296 | tf_op jit(solution)/shard_map/ppermute | solution.py:38
  230.7 1.6 fusion.176
  232.3 1.7 fusion.223
  235.6 8.3 %collective-permute-start.28 = (f32[8,128]{1,0:T(8,128)S(1)}, f32[8,128]{1,0:T(8,128)}, u32[]{:S(2)}, u32[]{:S(2)}) collective-permute-start(f32[8,128]{1,0:T(8,128)S(1)} %concatenate.142), channel_id=1, source_target_pairs={{0,128},{4,132},{8,136},{12,140},{16,144},{20,148},{24,152},{28,15... | collective-permute-start | bytes 12296 | tf_op jit(solution)/shard_map/ppermute | solution.py:38
  249.5 1.7 fusion.221
  252.7 6.6 %collective-permute-start.29 = (f32[8,128]{1,0:T(8,128)S(1)}, f32[8,128]{1,0:T(8,128)S(1)}, u32[]{:S(2)}, u32[]{:S(2)}) collective-permute-start(f32[8,128]{1,0:T(8,128)S(1)} %concatenate.142), channel_id=1, source_target_pairs={{0,256},{4,260},{8,264},{12,268},{16,272},{20,276},{24,280},{28,28... | collective-permute-start | bytes 12296 | tf_op jit(solution)/shard_map/ppermute | solution.py:38
  282.4 2.3 fusion.39
  (310 shorter events, 101.3 us)
Async XLA Ops:
  6.6 66.6 %collective-permute-start = (bf16[256,512]{1,0:T(8,128)(2,1)}, bf16[256,512]{1,0:T(8,128)(2,1)S(1)}, u32[]{:S(2)}, u32[]{:S(2)}) collective-permute-start(bf16[256,512]{1,0:T(8,128)(2,1)} %constant_dynamic-update-slice_fusion), channel_id=1, source_target_pairs={{4,0},{8,4},{12,8},{16,12},{20,16},{24,20},{28,24},{32,28},{36,32}... | collective-permute-start | bytes 786440 | tf_op jit(solution)/shard_map/ppermute | solution.py:38
  15.4 63.1 %collective-permute-start.1 = (bf16[256,512]{1,0:T(8,128)(2,1)}, bf16[256,512]{1,0:T(8,128)(2,1)S(1)}, u32[]{:S(2)}, u32[]{:S(2)}) collective-permute-start(bf16[256,512]{1,0:T(8,128)(2,1)} %constant_dynamic-update-slice_fusion), channel_id=1, source_target_pairs={{0,4},{4,8},{8,12},{12,16},{16,20},{20,24},{24,28},{28,32},{32,36}... | collective-permute-start | bytes 786440 | tf_op jit(solution)/shard_map/ppermute | solution.py:38
  17.3 62.6 %collective-permute-start.2 = (bf16[256,512]{1,0:T(8,128)(2,1)}, bf16[256,512]{1,0:T(8,128)(2,1)S(1)}, u32[]{:S(2)}, u32[]{:S(2)}) collective-permute-start(bf16[256,512]{1,0:T(8,128)(2,1)} %constant_dynamic-update-slice_fusion), channel_id=1, source_target_pairs={{8,0},{12,4},{16,8},{20,12},{24,16},{28,20},{32,24},{36,28},{40,32... | collective-permute-start | bytes 786440 | tf_op jit(solution)/shard_map/ppermute | solution.py:38
  18.6 67.4 %collective-permute-start.3 = (bf16[256,512]{1,0:T(8,128)(2,1)}, bf16[256,512]{1,0:T(8,128)(2,1)S(1)}, u32[]{:S(2)}, u32[]{:S(2)}) collective-permute-start(bf16[256,512]{1,0:T(8,128)(2,1)} %constant_dynamic-update-slice_fusion), channel_id=1, source_target_pairs={{0,8},{4,12},{8,16},{12,20},{16,24},{20,28},{24,32},{28,36},{32,40... | collective-permute-start | bytes 786440 | tf_op jit(solution)/shard_map/ppermute | solution.py:38
  22.6 64.8 %collective-permute-start.4 = (bf16[256,512]{1,0:T(8,128)(2,1)}, bf16[256,512]{1,0:T(8,128)(2,1)S(1)}, u32[]{:S(2)}, u32[]{:S(2)}) collective-permute-start(bf16[256,512]{1,0:T(8,128)(2,1)} %constant_dynamic-update-slice_fusion), channel_id=1, source_target_pairs={{12,0},{16,4},{20,8},{24,12},{28,16},{32,20},{36,24},{40,28},{44,3... | collective-permute-start | bytes 786440 | tf_op jit(solution)/shard_map/ppermute | solution.py:38
  79.9 25.5 %collective-permute-start.7 = (bf16[256,512]{1,0:T(8,128)(2,1)}, bf16[256,512]{1,0:T(8,128)(2,1)S(1)}, u32[]{:S(2)}, u32[]{:S(2)}) collective-permute-start(bf16[256,512]{1,0:T(8,128)(2,1)} %constant_dynamic-update-slice_fusion), channel_id=1, source_target_pairs={{0,16},{4,20},{8,24},{12,28},{16,32},{20,36},{24,40},{28,44},{32,4... | collective-permute-start | bytes 786440 | tf_op jit(solution)/shard_map/ppermute | solution.py:38
  86.0 29.8 %collective-permute-start.8 = (bf16[256,512]{1,0:T(8,128)(2,1)}, bf16[256,512]{1,0:T(8,128)(2,1)S(1)}, u32[]{:S(2)}, u32[]{:S(2)}) collective-permute-start(bf16[256,512]{1,0:T(8,128)(2,1)} %constant_dynamic-update-slice_fusion), channel_id=1, source_target_pairs={{32,0},{36,4},{40,8},{44,12},{48,16},{52,20},{56,24},{60,28},{64,3... | collective-permute-start | bytes 786440 | tf_op jit(solution)/shard_map/ppermute | solution.py:38
  87.4 44.5 %collective-permute-start.9 = (bf16[256,512]{1,0:T(8,128)(2,1)}, bf16[256,512]{1,0:T(8,128)(2,1)S(1)}, u32[]{:S(2)}, u32[]{:S(2)}) collective-permute-start(bf16[256,512]{1,0:T(8,128)(2,1)} %constant_dynamic-update-slice_fusion), channel_id=1, source_target_pairs={{0,32},{4,36},{8,40},{12,44},{16,48},{20,52},{24,56},{28,60},{32,6... | collective-permute-start | bytes 786440 | tf_op jit(solution)/shard_map/ppermute | solution.py:38
  96.9 43.0 %collective-permute-start.10 = (bf16[256,512]{1,0:T(8,128)(2,1)}, bf16[256,512]{1,0:T(8,128)(2,1)S(1)}, u32[]{:S(2)}, u32[]{:S(2)}) collective-permute-start(bf16[256,512]{1,0:T(8,128)(2,1)} %constant_dynamic-update-slice_fusion), channel_id=1, source_target_pairs={{64,0},{68,4},{72,8},{76,12},{80,16},{84,20},{88,24},{92,28},{96,3... | collective-permute-start | bytes 786440 | tf_op jit(solution)/shard_map/ppermute | solution.py:38
  99.8 40.2 %collective-permute-start.11 = (bf16[256,512]{1,0:T(8,128)(2,1)}, bf16[256,512]{1,0:T(8,128)(2,1)S(1)}, u32[]{:S(2)}, u32[]{:S(2)}) collective-permute-start(bf16[256,512]{1,0:T(8,128)(2,1)} %constant_dynamic-update-slice_fusion), channel_id=1, source_target_pairs={{0,64},{4,68},{8,72},{12,76},{16,80},{20,84},{24,88},{28,92},{32,9... | collective-permute-start | bytes 786440 | tf_op jit(solution)/shard_map/ppermute | solution.py:38
  105.3 34.7 %collective-permute-start.12 = (bf16[256,512]{1,0:T(8,128)(2,1)}, bf16[256,512]{1,0:T(8,128)(2,1)S(1)}, u32[]{:S(2)}, u32[]{:S(2)}) collective-permute-start(bf16[256,512]{1,0:T(8,128)(2,1)} %constant_dynamic-update-slice_fusion), channel_id=1, source_target_pairs={{128,0},{132,4},{136,8},{140,12},{144,16},{148,20},{152,24},{156,2... | collective-permute-start | bytes 786440 | tf_op jit(solution)/shard_map/ppermute | solution.py:38
  115.8 24.3 %collective-permute-start.13 = (bf16[256,512]{1,0:T(8,128)(2,1)}, bf16[256,512]{1,0:T(8,128)(2,1)S(1)}, u32[]{:S(2)}, u32[]{:S(2)}) collective-permute-start(bf16[256,512]{1,0:T(8,128)(2,1)} %constant_dynamic-update-slice_fusion), channel_id=1, source_target_pairs={{0,128},{4,132},{8,136},{12,140},{16,144},{20,148},{24,152},{28,15... | collective-permute-start | bytes 786440 | tf_op jit(solution)/shard_map/ppermute | solution.py:38
  164.6 29.5 %collective-permute-start.18 = (f32[8,128]{1,0:T(8,128)S(1)}, f32[8,128]{1,0:T(8,128)}, u32[]{:S(2)}, u32[]{:S(2)}) collective-permute-start(f32[8,128]{1,0:T(8,128)S(1)} %concatenate.142), channel_id=1, source_target_pairs={{0,8},{4,12},{8,16},{12,20},{16,24},{20,28},{24,32},{28,36},{32,40... | collective-permute-start | bytes 12296 | tf_op jit(solution)/shard_map/ppermute | solution.py:38
  173.9 24.9 %collective-permute-start.19 = (f32[8,128]{1,0:T(8,128)S(1)}, f32[8,128]{1,0:T(8,128)}, u32[]{:S(2)}, u32[]{:S(2)}) collective-permute-start(f32[8,128]{1,0:T(8,128)S(1)} %concatenate.142), channel_id=1, source_target_pairs={{12,0},{16,4},{20,8},{24,12},{28,16},{32,20},{36,24},{40,28},{44,3... | collective-permute-start | bytes 12296 | tf_op jit(solution)/shard_map/ppermute | solution.py:38
  177.7 33.1 %collective-permute-start.20 = (f32[8,128]{1,0:T(8,128)S(1)}, f32[8,128]{1,0:T(8,128)}, u32[]{:S(2)}, u32[]{:S(2)}) collective-permute-start(f32[8,128]{1,0:T(8,128)S(1)} %concatenate.142), channel_id=1, source_target_pairs={{0,12},{4,16},{8,20},{12,24},{16,28},{20,32},{24,36},{28,40},{32,4... | collective-permute-start | bytes 12296 | tf_op jit(solution)/shard_map/ppermute | solution.py:38
  183.5 32.1 %collective-permute-start.21 = (f32[8,128]{1,0:T(8,128)S(1)}, f32[8,128]{1,0:T(8,128)}, u32[]{:S(2)}, u32[]{:S(2)}) collective-permute-start(f32[8,128]{1,0:T(8,128)S(1)} %concatenate.142), channel_id=1, source_target_pairs={{16,0},{20,4},{24,8},{28,12},{32,16},{36,20},{40,24},{44,28},{48,3... | collective-permute-start | bytes 12296 | tf_op jit(solution)/shard_map/ppermute | solution.py:38
  186.0 40.1 %collective-permute-start.22 = (f32[8,128]{1,0:T(8,128)S(1)}, f32[8,128]{1,0:T(8,128)}, u32[]{:S(2)}, u32[]{:S(2)}) collective-permute-start(f32[8,128]{1,0:T(8,128)S(1)} %concatenate.142), channel_id=1, source_target_pairs={{0,16},{4,20},{8,24},{12,28},{16,32},{20,36},{24,40},{28,44},{32,4... | collective-permute-start | bytes 12296 | tf_op jit(solution)/shard_map/ppermute | solution.py:38
  194.1 41.5 %collective-permute-start.23 = (f32[8,128]{1,0:T(8,128)S(1)}, f32[8,128]{1,0:T(8,128)}, u32[]{:S(2)}, u32[]{:S(2)}) collective-permute-start(f32[8,128]{1,0:T(8,128)S(1)} %concatenate.142), channel_id=1, source_target_pairs={{32,0},{36,4},{40,8},{44,12},{48,16},{52,20},{56,24},{60,28},{64,3... | collective-permute-start | bytes 12296 | tf_op jit(solution)/shard_map/ppermute | solution.py:38
  198.9 53.9 %collective-permute-start.24 = (f32[8,128]{1,0:T(8,128)S(1)}, f32[8,128]{1,0:T(8,128)}, u32[]{:S(2)}, u32[]{:S(2)}) collective-permute-start(f32[8,128]{1,0:T(8,128)S(1)} %concatenate.142), channel_id=1, source_target_pairs={{0,32},{4,36},{8,40},{12,44},{16,48},{20,52},{24,56},{28,60},{32,6... | collective-permute-start | bytes 12296 | tf_op jit(solution)/shard_map/ppermute | solution.py:38
  210.8 53.5 %collective-permute-start.25 = (f32[8,128]{1,0:T(8,128)S(1)}, f32[8,128]{1,0:T(8,128)}, u32[]{:S(2)}, u32[]{:S(2)}) collective-permute-start(f32[8,128]{1,0:T(8,128)S(1)} %concatenate.142), channel_id=1, source_target_pairs={{64,0},{68,4},{72,8},{76,12},{80,16},{84,20},{88,24},{92,28},{96,3... | collective-permute-start | bytes 12296 | tf_op jit(solution)/shard_map/ppermute | solution.py:38
  215.6 53.8 %collective-permute-start.26 = (f32[8,128]{1,0:T(8,128)S(1)}, f32[8,128]{1,0:T(8,128)}, u32[]{:S(2)}, u32[]{:S(2)}) collective-permute-start(f32[8,128]{1,0:T(8,128)S(1)} %concatenate.142), channel_id=1, source_target_pairs={{0,64},{4,68},{8,72},{12,76},{16,80},{20,84},{24,88},{28,92},{32,9... | collective-permute-start | bytes 12296 | tf_op jit(solution)/shard_map/ppermute | solution.py:38
  226.0 48.3 %collective-permute-start.27 = (f32[8,128]{1,0:T(8,128)S(1)}, f32[8,128]{1,0:T(8,128)}, u32[]{:S(2)}, u32[]{:S(2)}) collective-permute-start(f32[8,128]{1,0:T(8,128)S(1)} %concatenate.142), channel_id=1, source_target_pairs={{128,0},{132,4},{136,8},{140,12},{144,16},{148,20},{152,24},{156,2... | collective-permute-start | bytes 12296 | tf_op jit(solution)/shard_map/ppermute | solution.py:38
  235.6 43.0 %collective-permute-start.28 = (f32[8,128]{1,0:T(8,128)S(1)}, f32[8,128]{1,0:T(8,128)}, u32[]{:S(2)}, u32[]{:S(2)}) collective-permute-start(f32[8,128]{1,0:T(8,128)S(1)} %concatenate.142), channel_id=1, source_target_pairs={{0,128},{4,132},{8,136},{12,140},{16,144},{20,148},{24,152},{28,15... | collective-permute-start | bytes 12296 | tf_op jit(solution)/shard_map/ppermute | solution.py:38
  252.7 28.1 %collective-permute-start.29 = (f32[8,128]{1,0:T(8,128)S(1)}, f32[8,128]{1,0:T(8,128)S(1)}, u32[]{:S(2)}, u32[]{:S(2)}) collective-permute-start(f32[8,128]{1,0:T(8,128)S(1)} %concatenate.142), channel_id=1, source_target_pairs={{0,256},{4,260},{8,264},{12,268},{16,272},{20,276},{24,280},{28,28... | collective-permute-start | bytes 12296 | tf_op jit(solution)/shard_map/ppermute | solution.py:38
  (31 other events, 556.9 us)

commit v2 on v1

--- a/solution.py
+++ b/solution.py
@@ -118,8 +118,13 @@
         [stat_pack, jnp.zeros((8 - 2 * blocks, BLK), jnp.float32)], axis=0
     )
 
-    got_near_stats = [receive(stat_pack, "seq", s, w) for s, w in near]
-    got_far_stats = [receive(stat_pack, "seq", s, w) for s, w in far]
+    all_stats = lax.all_gather(stat_pack, "seq")
+
+    def stats_of(frame):
+        return lax.dynamic_index_in_dim(all_stats, jnp.clip(frame, 0, count - 1), 0, keepdims=False)
+
+    got_near_stats = [stats_of(g) for g in near_frames]
+    got_far_stats = [stats_of(g) for g in far_frames]
 
     dk_total = jnp.stack(self_dk, axis=0).sum(axis=0) * scale
     dv_total = jnp.stack(self_dv, axis=0).sum(axis=0)

time: 290 us -> 273 us (0.941)
  starting transfers between devices: 135 us -> 72.6 us
  blocking collectives: 0 us -> 60.5 us
  local copies, waits for them, and re-layouts: 34 us -> 26.7 us
  matrix products: 55.2 us -> 48.7 us
    ppermute x30 -> x15, starting transfers between devices: 135 us -> 72.6 us  [receive(): return lax.ppermute(value, axis, pairs)]
    all_gather x0 -> x1, blocking collectives: none -> 60.5 us  [shards(): all_stats = lax.all_gather(stat_pack, 'seq')]
    sub x13, local copies, waits for them, and re-layouts: 10.1 us -> 2.83 us  [key_terms(): ds = (w.astype(jnp.float32) * (dw - delta_v[:, None])).astype(jnp.bfloat16)]
    dot_general x28, matrix products: 15.3 us -> 11.8 us  [key_terms(): lax.dot_general(q_v, k_g, across, preferred_element_type=jnp.float32)]
    ppermute x30 -> x15, waiting for transfers between devices: 25 us -> 24.9 us  [receive(): return lax.ppermute(value, axis, pairs)]
  transfers between devices with their start and end apart: 30 -> 15, of which waited for: 3 -> 3; matrix products, arithmetic and copies ran while one was open for 27% -> 6% of each run, Pallas kernels for 0% -> 0%
where the time goes in v2:
time: 273 us; the launch traced here: 271 us
  starting transfers between devices  72.6 us (27%)
  blocking collectives  60.5 us (22%)
  matrix products  48.7 us (18%)
  between operations  34.7 us (13%)
  local copies, waits for them, and re-layouts  26.7 us (10%)
  waiting for transfers between devices  24.9 us (9%)
    ppermute x15, starting transfers between devices, receive(): return lax.ppermute(value, axis, pairs)  72.6 us
    all_gather x1, blocking collectives, shards(): all_stats = lax.all_gather(stat_pack, 'seq')  60.5 us
    ppermute x15, waiting for transfers between devices, receive(): return lax.ppermute(value, axis, pairs)  24.9 us
    dot_general x28, matrix products, key_terms(): dv = lax.dot_general(w, do_v, over_rows, preferred_element_type=jnp.float32)  20.3 us
    dot_general x28, matrix products, key_terms(): dk = lax.dot_general(ds, q_v, over_rows, preferred_element_type=jnp.float32)  12.9 us
    unnamed x100, local copies, waits for them, and re-layouts  12.8 us
    dot_general x28, matrix products, key_terms(): lax.dot_general(q_v, k_g, across, preferred_element_type=jnp.float32)  11.8 us
  transfers between devices with their start and end apart: 15, of which 3 were waited for; matrix products, arithmetic and copies ran while one was open for 6% of the time, Pallas kernels for 0%

profile of v2, /device:TPU:1, one launch (start us, length us, event | category | flops | bytes accessed | tf_op | source)
XLA Modules:
  0.0 270.6 jit_solution(17276786291539761954)
XLA Ops:
  0.6 1.5 constant_dynamic-update-slice_fusion.51
  2.1 1.5 constant_dynamic-update-slice_fusion.2
  3.6 1.5 constant_dynamic-update-slice_fusion.1
  5.1 1.5 constant_dynamic-update-slice_fusion
  6.6 8.8 %collective-permute-start = (bf16[256,512]{1,0:T(8,128)(2,1)}, bf16[256,512]{1,0:T(8,128)(2,1)S(1)}, u32[]{:S(2)}, u32[]{:S(2)}) collective-permute-start(bf16[256,512]{1,0:T(8,128)(2,1)} %constant_dynamic-update-slice_fusion), channel_id=1, source_target_pairs={{4,0},{8,4},{12,8},{16,12},{20,16},{24,20},{28,24},{32,28},{36,32}... | collective-permute-start | bytes 786440 | tf_op jit(solution)/shard_map/ppermute | solution.py:38
  15.3 1.9 collective-permute-start.1
  17.3 1.3 collective-permute-start.2
  18.6 4.0 %collective-permute-start.3 = (bf16[256,512]{1,0:T(8,128)(2,1)}, bf16[256,512]{1,0:T(8,128)(2,1)S(1)}, u32[]{:S(2)}, u32[]{:S(2)}) collective-permute-start(bf16[256,512]{1,0:T(8,128)(2,1)} %constant_dynamic-update-slice_fusion), channel_id=1, source_target_pairs={{0,8},{4,12},{8,16},{12,20},{16,24},{20,28},{24,32},{28,36},{32,40... | collective-permute-start | bytes 786440 | tf_op jit(solution)/shard_map/ppermute | solution.py:38
  22.6 1.3 collective-permute-start.4
  24.0 1.4 constant_dynamic-slice_fusion.1
  73.3 5.2 %collective-permute-start.5 = (bf16[256,512]{1,0:T(8,128)(2,1)}, bf16[256,512]{1,0:T(8,128)(2,1)S(1)}, u32[]{:S(2)}, u32[]{:S(2)}) collective-permute-start(bf16[256,512]{1,0:T(8,128)(2,1)} %constant_dynamic-update-slice_fusion), channel_id=1, source_target_pairs={{0,12},{4,16},{8,20},{12,24},{16,28},{20,32},{24,36},{28,40},{32,4... | collective-permute-start | bytes 786440 | tf_op jit(solution)/shard_map/ppermute | solution.py:38
  78.5 1.3 collective-permute-start.6
  79.9 6.1 %collective-permute-start.7 = (bf16[256,512]{1,0:T(8,128)(2,1)}, bf16[256,512]{1,0:T(8,128)(2,1)S(1)}, u32[]{:S(2)}, u32[]{:S(2)}) collective-permute-start(bf16[256,512]{1,0:T(8,128)(2,1)} %constant_dynamic-update-slice_fusion), channel_id=1, source_target_pairs={{0,16},{4,20},{8,24},{12,28},{16,32},{20,36},{24,40},{28,44},{32,4... | collective-permute-start | bytes 786440 | tf_op jit(solution)/shard_map/ppermute | solution.py:38
  86.1 1.3 collective-permute-start.8
  87.4 9.4 %collective-permute-start.9 = (bf16[256,512]{1,0:T(8,128)(2,1)}, bf16[256,512]{1,0:T(8,128)(2,1)S(1)}, u32[]{:S(2)}, u32[]{:S(2)}) collective-permute-start(bf16[256,512]{1,0:T(8,128)(2,1)} %constant_dynamic-update-slice_fusion), channel_id=1, source_target_pairs={{0,32},{4,36},{8,40},{12,44},{16,48},{20,52},{24,56},{28,60},{32,6... | collective-permute-start | bytes 786440 | tf_op jit(solution)/shard_map/ppermute | solution.py:38
  97.0 1.3 collective-permute-start.10
  98.3 1.5 collective-permute-done.6
  99.8 5.5 %collective-permute-start.11 = (bf16[256,512]{1,0:T(8,128)(2,1)}, bf16[256,512]{1,0:T(8,128)(2,1)S(1)}, u32[]{:S(2)}, u32[]{:S(2)}) collective-permute-start(bf16[256,512]{1,0:T(8,128)(2,1)} %constant_dynamic-update-slice_fusion), channel_id=1, source_target_pairs={{0,64},{4,68},{8,72},{12,76},{16,80},{20,84},{24,88},{28,92},{32,9... | collective-permute-start | bytes 786440 | tf_op jit(solution)/shard_map/ppermute | solution.py:38
  106.7 9.1 %collective-permute-done.8 = bf16[256,512]{1,0:T(8,128)(2,1)S(1)} collective-permute-done((bf16[256,512]{1,0:T(8,128)(2,1)}, bf16[256,512]{1,0:T(8,128)(2,1)S(1)}, u32[]{:S(2)}, u32[]{:S(2)}) %collective-permute-start.8) | collective-permute-done | bytes 262176 | tf_op jit(solution)/shard_map/ppermute | solution.py:38
  115.9 16.0 %collective-permute-start.13 = (bf16[256,512]{1,0:T(8,128)(2,1)}, bf16[256,512]{1,0:T(8,128)(2,1)S(1)}, u32[]{:S(2)}, u32[]{:S(2)}) collective-permute-start(bf16[256,512]{1,0:T(8,128)(2,1)} %constant_dynamic-update-slice_fusion), channel_id=1, source_target_pairs={{0,128},{4,132},{8,136},{12,140},{16,144},{20,148},{24,152},{28,15... | collective-permute-start | bytes 786440 | tf_op jit(solution)/shard_map/ppermute | solution.py:38
  132.0 8.0 %collective-permute-start.14 = (bf16[256,512]{1,0:T(8,128)(2,1)}, bf16[256,512]{1,0:T(8,128)(2,1)S(1)}, u32[]{:S(2)}, u32[]{:S(2)}) collective-permute-start(bf16[256,512]{1,0:T(8,128)(2,1)} %constant_dynamic-update-slice_fusion), channel_id=1, source_target_pairs={{0,256},{4,260},{8,264},{12,268},{16,272},{20,276},{24,280},{28,28... | collective-permute-start | bytes 786440 | tf_op jit(solution)/shard_map/ppermute | solution.py:38
  140.2 14.2 %collective-permute-done.14 = bf16[256,512]{1,0:T(8,128)(2,1)S(1)} collective-permute-done((bf16[256,512]{1,0:T(8,128)(2,1)}, bf16[256,512]{1,0:T(8,128)(2,1)S(1)}, u32[]{:S(2)}, u32[]{:S(2)}) %collective-permute-start.14) | collective-permute-done | bytes 262176 | tf_op jit(solution)/shard_map/ppermute | solution.py:38
  160.5 60.5 %all-gather = f32[1024,128]{1,0:T(8,128)S(1)} all-gather(f32[8,128]{1,0:T(8,128)S(1)} %concatenate.142), channel_id=2, replica_groups=mesh['seq'=128,'head'=4] {'seq'}, dimensions={0}, use_global_device_ids=true | all-gather | bytes 528384 | tf_op jit(solution)/shard_map/all_gather | solution.py:121
  267.2 2.3 fusion.39
  (282 shorter events, 69.6 us)
Async XLA Ops:
  6.6 66.7 %collective-permute-start = (bf16[256,512]{1,0:T(8,128)(2,1)}, bf16[256,512]{1,0:T(8,128)(2,1)S(1)}, u32[]{:S(2)}, u32[]{:S(2)}) collective-permute-start(bf16[256,512]{1,0:T(8,128)(2,1)} %constant_dynamic-update-slice_fusion), channel_id=1, source_target_pairs={{4,0},{8,4},{12,8},{16,12},{20,16},{24,20},{28,24},{32,28},{36,32}... | collective-permute-start | bytes 786440 | tf_op jit(solution)/shard_map/ppermute | solution.py:38
  15.3 63.1 %collective-permute-start.1 = (bf16[256,512]{1,0:T(8,128)(2,1)}, bf16[256,512]{1,0:T(8,128)(2,1)S(1)}, u32[]{:S(2)}, u32[]{:S(2)}) collective-permute-start(bf16[256,512]{1,0:T(8,128)(2,1)} %constant_dynamic-update-slice_fusion), channel_id=1, source_target_pairs={{0,4},{4,8},{8,12},{12,16},{16,20},{20,24},{24,28},{28,32},{32,36}... | collective-permute-start | bytes 786440 | tf_op jit(solution)/shard_map/ppermute | solution.py:38
  17.3 62.6 %collective-permute-start.2 = (bf16[256,512]{1,0:T(8,128)(2,1)}, bf16[256,512]{1,0:T(8,128)(2,1)S(1)}, u32[]{:S(2)}, u32[]{:S(2)}) collective-permute-start(bf16[256,512]{1,0:T(8,128)(2,1)} %constant_dynamic-update-slice_fusion), channel_id=1, source_target_pairs={{8,0},{12,4},{16,8},{20,12},{24,16},{28,20},{32,24},{36,28},{40,32... | collective-permute-start | bytes 786440 | tf_op jit(solution)/shard_map/ppermute | solution.py:38
  18.6 67.5 %collective-permute-start.3 = (bf16[256,512]{1,0:T(8,128)(2,1)}, bf16[256,512]{1,0:T(8,128)(2,1)S(1)}, u32[]{:S(2)}, u32[]{:S(2)}) collective-permute-start(bf16[256,512]{1,0:T(8,128)(2,1)} %constant_dynamic-update-slice_fusion), channel_id=1, source_target_pairs={{0,8},{4,12},{8,16},{12,20},{16,24},{20,28},{24,32},{28,36},{32,40... | collective-permute-start | bytes 786440 | tf_op jit(solution)/shard_map/ppermute | solution.py:38
  22.6 64.8 %collective-permute-start.4 = (bf16[256,512]{1,0:T(8,128)(2,1)}, bf16[256,512]{1,0:T(8,128)(2,1)S(1)}, u32[]{:S(2)}, u32[]{:S(2)}) collective-permute-start(bf16[256,512]{1,0:T(8,128)(2,1)} %constant_dynamic-update-slice_fusion), channel_id=1, source_target_pairs={{12,0},{16,4},{20,8},{24,12},{28,16},{32,20},{36,24},{40,28},{44,3... | collective-permute-start | bytes 786440 | tf_op jit(solution)/shard_map/ppermute | solution.py:38
  73.3 23.7 %collective-permute-start.5 = (bf16[256,512]{1,0:T(8,128)(2,1)}, bf16[256,512]{1,0:T(8,128)(2,1)S(1)}, u32[]{:S(2)}, u32[]{:S(2)}) collective-permute-start(bf16[256,512]{1,0:T(8,128)(2,1)} %constant_dynamic-update-slice_fusion), channel_id=1, source_target_pairs={{0,12},{4,16},{8,20},{12,24},{16,28},{20,32},{24,36},{28,40},{32,4... | collective-permute-start | bytes 786440 | tf_op jit(solution)/shard_map/ppermute | solution.py:38
  78.5 21.3 %collective-permute-start.6 = (bf16[256,512]{1,0:T(8,128)(2,1)}, bf16[256,512]{1,0:T(8,128)(2,1)S(1)}, u32[]{:S(2)}, u32[]{:S(2)}) collective-permute-start(bf16[256,512]{1,0:T(8,128)(2,1)} %constant_dynamic-update-slice_fusion), channel_id=1, source_target_pairs={{16,0},{20,4},{24,8},{28,12},{32,16},{36,20},{40,24},{44,28},{48,3... | collective-permute-start | bytes 786440 | tf_op jit(solution)/shard_map/ppermute | solution.py:38
  79.9 25.4 %collective-permute-start.7 = (bf16[256,512]{1,0:T(8,128)(2,1)}, bf16[256,512]{1,0:T(8,128)(2,1)S(1)}, u32[]{:S(2)}, u32[]{:S(2)}) collective-permute-start(bf16[256,512]{1,0:T(8,128)(2,1)} %constant_dynamic-update-slice_fusion), channel_id=1, source_target_pairs={{0,16},{4,20},{8,24},{12,28},{16,32},{20,36},{24,40},{28,44},{32,4... | collective-permute-start | bytes 786440 | tf_op jit(solution)/shard_map/ppermute | solution.py:38
  86.1 29.8 %collective-permute-start.8 = (bf16[256,512]{1,0:T(8,128)(2,1)}, bf16[256,512]{1,0:T(8,128)(2,1)S(1)}, u32[]{:S(2)}, u32[]{:S(2)}) collective-permute-start(bf16[256,512]{1,0:T(8,128)(2,1)} %constant_dynamic-update-slice_fusion), channel_id=1, source_target_pairs={{32,0},{36,4},{40,8},{44,12},{48,16},{52,20},{56,24},{60,28},{64,3... | collective-permute-start | bytes 786440 | tf_op jit(solution)/shard_map/ppermute | solution.py:38
  87.4 44.5 %collective-permute-start.9 = (bf16[256,512]{1,0:T(8,128)(2,1)}, bf16[256,512]{1,0:T(8,128)(2,1)S(1)}, u32[]{:S(2)}, u32[]{:S(2)}) collective-permute-start(bf16[256,512]{1,0:T(8,128)(2,1)} %constant_dynamic-update-slice_fusion), channel_id=1, source_target_pairs={{0,32},{4,36},{8,40},{12,44},{16,48},{20,52},{24,56},{28,60},{32,6... | collective-permute-start | bytes 786440 | tf_op jit(solution)/shard_map/ppermute | solution.py:38
  96.9 57.6 %copy-start.3 = (bf16[256,512]{1,0:T(8,128)(2,1)}, bf16[256,512]{1,0:T(8,128)(2,1)S(1)}, u32[]{:S(2)}) copy-start(bf16[256,512]{1,0:T(8,128)(2,1)S(1)} %collective-permute-done.5) | copy-start | bytes 786436
  97.0 43.0 %collective-permute-start.10 = (bf16[256,512]{1,0:T(8,128)(2,1)}, bf16[256,512]{1,0:T(8,128)(2,1)S(1)}, u32[]{:S(2)}, u32[]{:S(2)}) collective-permute-start(bf16[256,512]{1,0:T(8,128)(2,1)} %constant_dynamic-update-slice_fusion), channel_id=1, source_target_pairs={{64,0},{68,4},{72,8},{76,12},{80,16},{84,20},{88,24},{92,28},{96,3... | collective-permute-start | bytes 786440 | tf_op jit(solution)/shard_map/ppermute | solution.py:38
  98.3 56.2 %copy-start.2 = (bf16[256,128]{1,0:T(8,128)(2,1)S(1)}, bf16[256,128]{1,0:T(8,128)(2,1)}, u32[]{:S(2)}) copy-start(bf16[256,128]{1,0:T(8,128)(2,1)} %param.5) | copy-start | bytes 196612
  99.8 40.2 %collective-permute-start.11 = (bf16[256,512]{1,0:T(8,128)(2,1)}, bf16[256,512]{1,0:T(8,128)(2,1)S(1)}, u32[]{:S(2)}, u32[]{:S(2)}) collective-permute-start(bf16[256,512]{1,0:T(8,128)(2,1)} %constant_dynamic-update-slice_fusion), channel_id=1, source_target_pairs={{0,64},{4,68},{8,72},{12,76},{16,80},{20,84},{24,88},{28,92},{32,9... | collective-permute-start | bytes 786440 | tf_op jit(solution)/shard_map/ppermute | solution.py:38
  105.4 34.7 %collective-permute-start.12 = (bf16[256,512]{1,0:T(8,128)(2,1)}, bf16[256,512]{1,0:T(8,128)(2,1)S(1)}, u32[]{:S(2)}, u32[]{:S(2)}) collective-permute-start(bf16[256,512]{1,0:T(8,128)(2,1)} %constant_dynamic-update-slice_fusion), channel_id=1, source_target_pairs={{128,0},{132,4},{136,8},{140,12},{144,16},{148,20},{152,24},{156,2... | collective-permute-start | bytes 786440 | tf_op jit(solution)/shard_map/ppermute | solution.py:38
  115.9 24.3 %collective-permute-start.13 = (bf16[256,512]{1,0:T(8,128)(2,1)}, bf16[256,512]{1,0:T(8,128)(2,1)S(1)}, u32[]{:S(2)}, u32[]{:S(2)}) collective-permute-start(bf16[256,512]{1,0:T(8,128)(2,1)} %constant_dynamic-update-slice_fusion), channel_id=1, source_target_pairs={{0,128},{4,132},{8,136},{12,140},{16,144},{20,148},{24,152},{28,15... | collective-permute-start | bytes 786440 | tf_op jit(solution)/shard_map/ppermute | solution.py:38
  131.9 23.1 %copy-start.5 = (bf16[256,512]{1,0:T(8,128)(2,1)}, bf16[256,512]{1,0:T(8,128)(2,1)S(1)}, u32[]{:S(2)}) copy-start(bf16[256,512]{1,0:T(8,128)(2,1)S(1)} %collective-permute-done.9) | copy-start | bytes 786436
  132.0 22.5 %collective-permute-start.14 = (bf16[256,512]{1,0:T(8,128)(2,1)}, bf16[256,512]{1,0:T(8,128)(2,1)S(1)}, u32[]{:S(2)}, u32[]{:S(2)}) collective-permute-start(bf16[256,512]{1,0:T(8,128)(2,1)} %constant_dynamic-update-slice_fusion), channel_id=1, source_target_pairs={{0,256},{4,260},{8,264},{12,268},{16,272},{20,276},{24,280},{28,28... | collective-permute-start | bytes 786440 | tf_op jit(solution)/shard_map/ppermute | solution.py:38
  140.0 15.0 %copy-start.7 = (bf16[256,512]{1,0:T(8,128)(2,1)}, bf16[256,512]{1,0:T(8,128)(2,1)S(1)}, u32[]{:S(2)}) copy-start(bf16[256,512]{1,0:T(8,128)(2,1)S(1)} %collective-permute-done.10) | copy-start | bytes 786436
  140.0 15.0 %copy-start.9 = (bf16[256,512]{1,0:T(8,128)(2,1)}, bf16[256,512]{1,0:T(8,128)(2,1)S(1)}, u32[]{:S(2)}) copy-start(bf16[256,512]{1,0:T(8,128)(2,1)S(1)} %collective-permute-done.11) | copy-start | bytes 786436
  140.1 14.9 %copy-start.11 = (bf16[256,512]{1,0:T(8,128)(2,1)}, bf16[256,512]{1,0:T(8,128)(2,1)S(1)}, u32[]{:S(2)}) copy-start(bf16[256,512]{1,0:T(8,128)(2,1)S(1)} %collective-permute-done.12) | copy-start | bytes 786436
  140.2 15.2 %copy-start.13 = (bf16[256,512]{1,0:T(8,128)(2,1)}, bf16[256,512]{1,0:T(8,128)(2,1)S(1)}, u32[]{:S(2)}) copy-start(bf16[256,512]{1,0:T(8,128)(2,1)S(1)} %collective-permute-done.13) | copy-start | bytes 786436
  160.1 64.9 %copy-start.21 = (bf16[256,128]{1,0:T(8,128)(2,1)S(1)}, bf16[256,128]{1,0:T(8,128)(2,1)}, u32[]{:S(2)}) copy-start(bf16[256,128]{1,0:T(8,128)(2,1)} %param.6) | copy-start | bytes 196612
  160.5 65.0 %copy-start = (bf16[256,128]{1,0:T(8,128)(2,1)S(1)}, bf16[256,128]{1,0:T(8,128)(2,1)}, u32[]{:S(2)}) copy-start(bf16[256,128]{1,0:T(8,128)(2,1)} %param.7) | copy-start | bytes 196612
  (16 other events, 108.8 us)

commit v3 on v0

--- a/solution.py
+++ b/solution.py
@@ -88,19 +88,23 @@
     near_ok = jnp.repeat((neighbour >= 0) & (neighbour < frame_count), tok_rows)
     pieces = [near_keys]
     mask_list = [jnp.broadcast_to(near_ok[None, :], (tok_rows, 3 * tok_rows))]
-    sent_starts = []
+    half = frame_count // 2
+    offsets = [o for o in offsets if o != -half]
     for offset in offsets:
-        viewer = jnp.clip(device - offset, 0, frame_count - 1)
-        sent_start = jnp.maximum(far_block[viewer, device, 0], 0)
-        arrived = from_behind(joined, "seq", -offset)
-        other_frame = device + offset
+        if offset == half:
+            arrived = lax.ppermute(
+                joined, "seq", [(src, (src + half) % frame_count) for src in range(frame_count)]
+            )
+            other_frame = (device + half) % frame_count
+        else:
+            arrived = from_behind(joined, "seq", -offset)
+            other_frame = device + offset
         is_valid = (other_frame >= 0) & (other_frame < frame_count)
         safe_frame = jnp.clip(other_frame, 0, frame_count - 1)
         entries = far_block[device, safe_frame]
         pair_start, far_hit = far_window(entries, is_valid)
         pieces.append(arrived)
         mask_list.append(far_hit)
-        sent_starts.append(sent_start)
     keys_all = jnp.concatenate(pieces, axis=0)
     visible = jnp.concatenate(mask_list, axis=1)
     attention_out, query_grad, weights, dscores, log_total, row_delta = attend_parts(
@@ -109,16 +113,23 @@
     near_terms = key_terms(
         weights[:, : 3 * tok_rows], dscores[:, : 3 * tok_rows], query_tokens, grad_out
     )
-    from_after = from_behind(near_terms[:tok_rows], "seq", -1)
-    from_before = from_behind(near_terms[2 * tok_rows :], "seq", 1)
+    sent = near_terms.astype(jnp.bfloat16)
+    from_after = from_behind(sent[:tok_rows], "seq", -1).astype(jnp.float32)
+    from_before = from_behind(sent[2 * tok_rows :], "seq", 1).astype(jnp.float32)
     grad_total = near_terms[tok_rows : 2 * tok_rows] + from_after + from_before
     far_terms = key_terms(
         weights[:, 3 * tok_rows :], dscores[:, 3 * tok_rows :], query_tokens, grad_out
     )
     for slot_index in range(len(offsets)):
         first_row = slot_index * 2 * BLK
-        grad_piece = far_terms[first_row : first_row + 2 * BLK]
-        returned = from_behind(grad_piece, "seq", offsets[slot_index])
+        grad_piece = far_terms[first_row : first_row + 2 * BLK].astype(jnp.bfloat16)
+        if offsets[slot_index] == half:
+            returned = lax.ppermute(
+                grad_piece, "seq", [(src, (src + half) % frame_count) for src in range(frame_count)]
+            )
+        else:
+            returned = from_behind(grad_piece, "seq", offsets[slot_index])
+        returned = returned.astype(jnp.float32)
         current = grad_total
         grad_total = current + returned
     key_grad = grad_total[:, :HD]

time: 231 us -> 195 us (0.84)
  the two profiles are of different devices: /device:TPU:88 before, /device:TPU:36 now
where the time goes in v3:
time: 195 us; the launch traced here: 194 us
  starting transfers between devices  117 us (60%)
  waiting for transfers between devices  41.1 us (21%)
  local copies, waits for them, and re-layouts  14.1 us (7%)
  between operations  10 us (5%)
  matrix products  5.68 us (3%)
  other arithmetic  5.16 us (3%)
    ppermute x26, starting transfers between devices, from_behind(): lax.ppermute(value, axis, [(source, source + steps) for source in range(l...  105 us
    ppermute x26, waiting for transfers between devices, from_behind(): lax.ppermute(value, axis, [(source, source + steps) for source in range(l...  38.7 us
    ppermute x1, starting transfers between devices, extended(): after = lax.ppermute(leading, axis, down)  6.96 us
    slice x13, local copies, waits for them, and re-layouts, far_window(): pair_start = jnp.maximum(entries[0], 0)  6.88 us
    unnamed x68, local copies, waits for them, and re-layouts  5.11 us
  transfers between devices with their start and end apart: 30, of which 8 were waited for; matrix products, arithmetic and copies ran while one was open for 8% of the time, Pallas kernels for 0%

profile of v3, /device:TPU:36, one launch (start us, length us, event | category | flops | bytes accessed | tf_op | source)
XLA Modules:
  0.0 193.5 jit_solution(9448292385226002100)
XLA Ops:
  2.5 2.0 %collective-permute-start.14 = (bf16[256,256]{1,0:T(8,128)(2,1)S(1)}, bf16[256,256]{1,0:T(8,128)(2,1)S(1)}, u32[]{:S(2)}, u32[]{:S(2)}) collective-permute-start(bf16[256,256]{1,0:T(8,128)(2,1)S(1)} %constant_dynamic-update-slice_fusion.13), channel_id=1, source_target_pairs={{0,256},{4,260},{8,264},{12,268},{16,272},{20,276},{24,280},{28,28... | collective-permute-start | bytes 393224 | tf_op jit(solution)/shard_map/ppermute | solution.py:95
  4.5 4.5 %collective-permute-start.13 = (bf16[256,256]{1,0:T(8,128)(2,1)S(1)}, bf16[256,256]{1,0:T(8,128)(2,1)S(1)}, u32[]{:S(2)}, u32[]{:S(2)}) collective-permute-start(bf16[256,256]{1,0:T(8,128)(2,1)S(1)} %constant_dynamic-update-slice_fusion.13), channel_id=1, source_target_pairs={{0,128},{4,132},{8,136},{12,140},{16,144},{20,148},{24,152},{28,15... | collective-permute-start | bytes 393224 | tf_op jit(solution)/shard_map/ppermute | solution.py:26
  9.0 3.6 %collective-permute-start.12 = (bf16[256,256]{1,0:T(8,128)(2,1)S(1)}, bf16[256,256]{1,0:T(8,128)(2,1)S(1)}, u32[]{:S(2)}, u32[]{:S(2)}) collective-permute-start(bf16[256,256]{1,0:T(8,128)(2,1)S(1)} %constant_dynamic-update-slice_fusion.13), channel_id=1, source_target_pairs={{128,0},{132,4},{136,8},{140,12},{144,16},{148,20},{152,24},{156,2... | collective-permute-start | bytes 393224 | tf_op jit(solution)/shard_map/ppermute | solution.py:26
  12.6 12.5 %collective-permute-start.2 = (bf16[256,256]{1,0:T(8,128)(2,1)S(1)}, bf16[256,256]{1,0:T(8,128)(2,1)S(1)}, u32[]{:S(2)}, u32[]{:S(2)}) collective-permute-start(bf16[256,256]{1,0:T(8,128)(2,1)S(1)} %constant_dynamic-update-slice_fusion.13), channel_id=1, source_target_pairs={{8,0},{12,4},{16,8},{20,12},{24,16},{28,20},{32,24},{36,28},{40,32... | collective-permute-start | bytes 393224 | tf_op jit(solution)/shard_map/ppermute | solution.py:26
  48.3 7.0 %collective-permute-start.1 = (bf16[256,256]{1,0:T(8,128)(2,1)S(1)}, bf16[256,256]{1,0:T(8,128)(2,1)S(1)}, u32[]{:S(2)}, u32[]{:S(2)}) collective-permute-start(bf16[256,256]{1,0:T(8,128)(2,1)S(1)} %constant_dynamic-update-slice_fusion.13), channel_id=1, source_target_pairs={{4,0},{8,4},{12,8},{16,12},{20,16},{24,20},{28,24},{32,28},{36,32}... | collective-permute-start | bytes 393224 | tf_op jit(solution)/shard_map/ppermute | solution.py:18
  55.4 2.4 %collective-permute-done.1 = bf16[256,256]{1,0:T(8,128)(2,1)S(1)} collective-permute-done((bf16[256,256]{1,0:T(8,128)(2,1)S(1)}, bf16[256,256]{1,0:T(8,128)(2,1)S(1)}, u32[]{:S(2)}, u32[]{:S(2)}) %collective-permute-start.1) | collective-permute-done | bytes 131104 | tf_op jit(solution)/shard_map/ppermute | solution.py:18
  59.8 8.3 %collective-permute-start.4 = (bf16[256,256]{1,0:T(8,128)(2,1)S(1)}, bf16[256,256]{1,0:T(8,128)(2,1)S(1)}, u32[]{:S(2)}, u32[]{:S(2)}) collective-permute-start(bf16[256,256]{1,0:T(8,128)(2,1)S(1)} %constant_dynamic-update-slice_fusion.13), channel_id=1, source_target_pairs={{12,0},{16,4},{20,8},{24,12},{28,16},{32,20},{36,24},{40,28},{44,3... | collective-permute-start | bytes 393224 | tf_op jit(solution)/shard_map/ppermute | solution.py:26
  70.9 3.1 %collective-permute-start.6 = (bf16[256,256]{1,0:T(8,128)(2,1)S(1)}, bf16[256,256]{1,0:T(8,128)(2,1)S(1)}, u32[]{:S(2)}, u32[]{:S(2)}) collective-permute-start(bf16[256,256]{1,0:T(8,128)(2,1)S(1)} %constant_dynamic-update-slice_fusion.13), channel_id=1, source_target_pairs={{16,0},{20,4},{24,8},{28,12},{32,16},{36,20},{40,24},{44,28},{48,3... | collective-permute-start | bytes 393224 | tf_op jit(solution)/shard_map/ppermute | solution.py:26
  74.0 6.2 %collective-permute-done.5 = bf16[256,256]{1,0:T(8,128)(2,1)S(1)} collective-permute-done((bf16[256,256]{1,0:T(8,128)(2,1)S(1)}, bf16[256,256]{1,0:T(8,128)(2,1)S(1)}, u32[]{:S(2)}, u32[]{:S(2)}) %collective-permute-start.5) | collective-permute-done | bytes 131104 | tf_op jit(solution)/shard_map/ppermute | solution.py:26
  84.1 10.7 %collective-permute-done.7 = bf16[256,256]{1,0:T(8,128)(2,1)S(1)} collective-permute-done((bf16[256,256]{1,0:T(8,128)(2,1)S(1)}, bf16[256,256]{1,0:T(8,128)(2,1)S(1)}, u32[]{:S(2)}, u32[]{:S(2)}) %collective-permute-start.7) | collective-permute-done | bytes 131104 | tf_op jit(solution)/shard_map/ppermute | solution.py:26
  98.8 9.6 %collective-permute-done.9 = bf16[256,256]{1,0:T(8,128)(2,1)S(1)} collective-permute-done((bf16[256,256]{1,0:T(8,128)(2,1)S(1)}, bf16[256,256]{1,0:T(8,128)(2,1)S(1)}, u32[]{:S(2)}, u32[]{:S(2)}) %collective-permute-start.9) | collective-permute-done | bytes 131104 | tf_op jit(solution)/shard_map/ppermute | solution.py:26
  110.4 6.1 %collective-permute-done.11 = bf16[256,256]{1,0:T(8,128)(2,1)S(1)} collective-permute-done((bf16[256,256]{1,0:T(8,128)(2,1)S(1)}, bf16[256,256]{1,0:T(8,128)(2,1)S(1)}, u32[]{:S(2)}, u32[]{:S(2)}) %collective-permute-start.11) | collective-permute-done | bytes 131104 | tf_op jit(solution)/shard_map/ppermute | solution.py:26
  124.7 1.9 collective-permute-start.29
  126.6 1.9 collective-permute-start.28
  128.5 4.8 %collective-permute-start.27 = (bf16[256,256]{0,1:T(8,128)(2,1)S(1)}, bf16[256,256]{0,1:T(8,128)(2,1)S(1)}, u32[]{:S(2)}, u32[]{:S(2)}) collective-permute-start(bf16[256,256]{0,1:T(8,128)(2,1)S(1)} %get-tuple-element.37), channel_id=1, source_target_pairs={{0,128},{4,132},{8,136},{12,140},{16,144},{20,148},{24,152},{28,15... | collective-permute-start | bytes 393224 | tf_op jit(solution)/shard_map/ppermute | solution.py:26
  133.3 2.8 %collective-permute-start.26 = (bf16[256,256]{0,1:T(8,128)(2,1)S(1)}, bf16[256,256]{0,1:T(8,128)(2,1)S(1)}, u32[]{:S(2)}, u32[]{:S(2)}) collective-permute-start(bf16[256,256]{0,1:T(8,128)(2,1)S(1)} %get-tuple-element.38), channel_id=1, source_target_pairs={{64,0},{68,4},{72,8},{76,12},{80,16},{84,20},{88,24},{92,28},{96,3... | collective-permute-start | bytes 393224 | tf_op jit(solution)/shard_map/ppermute | solution.py:26
  136.5 3.0 %collective-permute-start.25 = (bf16[256,256]{0,1:T(8,128)(2,1)S(1)}, bf16[256,256]{0,1:T(8,128)(2,1)S(1)}, u32[]{:S(2)}, u32[]{:S(2)}) collective-permute-start(bf16[256,256]{0,1:T(8,128)(2,1)S(1)} %get-tuple-element.39), channel_id=1, source_target_pairs={{0,64},{4,68},{8,72},{12,76},{16,80},{20,84},{24,88},{28,92},{32,9... | collective-permute-start | bytes 393224 | tf_op jit(solution)/shard_map/ppermute | solution.py:26
  139.6 3.6 %collective-permute-start.24 = (bf16[256,256]{0,1:T(8,128)(2,1)S(1)}, bf16[256,256]{0,1:T(8,128)(2,1)S(1)}, u32[]{:S(2)}, u32[]{:S(2)}) collective-permute-start(bf16[256,256]{0,1:T(8,128)(2,1)S(1)} %get-tuple-element.40), channel_id=1, source_target_pairs={{32,0},{36,4},{40,8},{44,12},{48,16},{52,20},{56,24},{60,28},{64,3... | collective-permute-start | bytes 393224 | tf_op jit(solution)/shard_map/ppermute | solution.py:26
  143.2 6.2 %collective-permute-start.23 = (bf16[256,256]{0,1:T(8,128)(2,1)S(1)}, bf16[256,256]{0,1:T(8,128)(2,1)S(1)}, u32[]{:S(2)}, u32[]{:S(2)}) collective-permute-start(bf16[256,256]{0,1:T(8,128)(2,1)S(1)} %get-tuple-element.41), channel_id=1, source_target_pairs={{0,32},{4,36},{8,40},{12,44},{16,48},{20,52},{24,56},{28,60},{32,6... | collective-permute-start | bytes 393224 | tf_op jit(solution)/shard_map/ppermute | solution.py:26
  149.4 6.9 %collective-permute-start.22 = (bf16[256,256]{0,1:T(8,128)(2,1)S(1)}, bf16[256,256]{0,1:T(8,128)(2,1)S(1)}, u32[]{:S(2)}, u32[]{:S(2)}) collective-permute-start(bf16[256,256]{0,1:T(8,128)(2,1)S(1)} %get-tuple-element.42), channel_id=1, source_target_pairs={{16,0},{20,4},{24,8},{28,12},{32,16},{36,20},{40,24},{44,28},{48,3... | collective-permute-start | bytes 393224 | tf_op jit(solution)/shard_map/ppermute | solution.py:26
  158.2 4.4 %collective-permute-start.20 = (bf16[256,256]{0,1:T(8,128)(2,1)}, bf16[256,256]{0,1:T(8,128)(2,1)S(1)}, u32[]{:S(2)}, u32[]{:S(2)}) collective-permute-start(bf16[256,256]{0,1:T(8,128)(2,1)} %get-tuple-element.44), channel_id=1, source_target_pairs={{12,0},{16,4},{20,8},{24,12},{28,16},{32,20},{36,24},{40,28},{44,3... | collective-permute-start | bytes 393224 | tf_op jit(solution)/shard_map/ppermute | solution.py:26
  164.6 15.6 %collective-permute-start.18 = (bf16[256,256]{0,1:T(8,128)(2,1)S(1)}, bf16[256,256]{0,1:T(8,128)(2,1)S(1)}, u32[]{:S(2)}, u32[]{:S(2)}) collective-permute-start(bf16[256,256]{0,1:T(8,128)(2,1)S(1)} %get-tuple-element.46), channel_id=1, source_target_pairs={{8,0},{12,4},{16,8},{20,12},{24,16},{28,20},{32,24},{36,28},{40,32... | collective-permute-start | bytes 393224 | tf_op jit(solution)/shard_map/ppermute | solution.py:26
  182.1 2.4 %collective-permute-start.16 = (bf16[256,256]{0,1:T(8,128)(2,1)S(1)}, bf16[256,256]{0,1:T(8,128)(2,1)S(1)}, u32[]{:S(2)}, u32[]{:S(2)}) collective-permute-start(bf16[256,256]{0,1:T(8,128)(2,1)S(1)} %get-tuple-element.48), channel_id=1, source_target_pairs={{0,4},{4,8},{8,12},{12,16},{16,20},{20,24},{24,28},{28,32},{32,36}... | collective-permute-start | bytes 393224 | tf_op jit(solution)/shard_map/ppermute | solution.py:26
  186.8 5.0 %collective-permute-done.16 = bf16[256,256]{0,1:T(8,128)(2,1)S(1)} collective-permute-done((bf16[256,256]{0,1:T(8,128)(2,1)S(1)}, bf16[256,256]{0,1:T(8,128)(2,1)S(1)}, u32[]{:S(2)}, u32[]{:S(2)}) %collective-permute-start.16) | collective-permute-done | bytes 131104 | tf_op jit(solution)/shard_map/ppermute | solution.py:26
  (175 shorter events, 49.1 us)
Async XLA Ops:
  2.5 114.1 %collective-permute-start.14 = (bf16[256,256]{1,0:T(8,128)(2,1)S(1)}, bf16[256,256]{1,0:T(8,128)(2,1)S(1)}, u32[]{:S(2)}, u32[]{:S(2)}) collective-permute-start(bf16[256,256]{1,0:T(8,128)(2,1)S(1)} %constant_dynamic-update-slice_fusion.13), channel_id=1, source_target_pairs={{0,256},{4,260},{8,264},{12,268},{16,272},{20,276},{24,280},{28,28... | collective-permute-start | bytes 393224 | tf_op jit(solution)/shard_map/ppermute | solution.py:95
  4.5 112.1 %collective-permute-start.13 = (bf16[256,256]{1,0:T(8,128)(2,1)S(1)}, bf16[256,256]{1,0:T(8,128)(2,1)S(1)}, u32[]{:S(2)}, u32[]{:S(2)}) collective-permute-start(bf16[256,256]{1,0:T(8,128)(2,1)S(1)} %constant_dynamic-update-slice_fusion.13), channel_id=1, source_target_pairs={{0,128},{4,132},{8,136},{12,140},{16,144},{20,148},{24,152},{28,15... | collective-permute-start | bytes 393224 | tf_op jit(solution)/shard_map/ppermute | solution.py:26
  9.0 107.6 %collective-permute-start.12 = (bf16[256,256]{1,0:T(8,128)(2,1)S(1)}, bf16[256,256]{1,0:T(8,128)(2,1)S(1)}, u32[]{:S(2)}, u32[]{:S(2)}) collective-permute-start(bf16[256,256]{1,0:T(8,128)(2,1)S(1)} %constant_dynamic-update-slice_fusion.13), channel_id=1, source_target_pairs={{128,0},{132,4},{136,8},{140,12},{144,16},{148,20},{152,24},{156,2... | collective-permute-start | bytes 393224 | tf_op jit(solution)/shard_map/ppermute | solution.py:26
  12.6 47.2 %collective-permute-start.2 = (bf16[256,256]{1,0:T(8,128)(2,1)S(1)}, bf16[256,256]{1,0:T(8,128)(2,1)S(1)}, u32[]{:S(2)}, u32[]{:S(2)}) collective-permute-start(bf16[256,256]{1,0:T(8,128)(2,1)S(1)} %constant_dynamic-update-slice_fusion.13), channel_id=1, source_target_pairs={{8,0},{12,4},{16,8},{20,12},{24,16},{28,20},{32,24},{36,28},{40,32... | collective-permute-start | bytes 393224 | tf_op jit(solution)/shard_map/ppermute | solution.py:26
  25.1 23.2 %collective-permute-start = (bf16[256,256]{1,0:T(8,128)(2,1)S(1)}, bf16[256,256]{1,0:T(8,128)(2,1)S(1)}, u32[]{:S(2)}, u32[]{:S(2)}) collective-permute-start(bf16[256,256]{1,0:T(8,128)(2,1)S(1)} %constant_dynamic-update-slice_fusion.13), channel_id=1, source_target_pairs={{0,4},{4,8},{8,12},{12,16},{16,20},{20,24},{24,28},{28,32},{32,36}... | collective-permute-start | bytes 393224 | tf_op jit(solution)/shard_map/ppermute | solution.py:17
  68.9 11.3 %collective-permute-start.5 = (bf16[256,256]{1,0:T(8,128)(2,1)S(1)}, bf16[256,256]{1,0:T(8,128)(2,1)S(1)}, u32[]{:S(2)}, u32[]{:S(2)}) collective-permute-start(bf16[256,256]{1,0:T(8,128)(2,1)S(1)} %constant_dynamic-update-slice_fusion.13), channel_id=1, source_target_pairs={{0,12},{4,16},{8,20},{12,24},{16,28},{20,32},{24,36},{28,40},{32,4... | collective-permute-start | bytes 393224 | tf_op jit(solution)/shard_map/ppermute | solution.py:26
  70.9 11.3 %collective-permute-start.6 = (bf16[256,256]{1,0:T(8,128)(2,1)S(1)}, bf16[256,256]{1,0:T(8,128)(2,1)S(1)}, u32[]{:S(2)}, u32[]{:S(2)}) collective-permute-start(bf16[256,256]{1,0:T(8,128)(2,1)S(1)} %constant_dynamic-update-slice_fusion.13), channel_id=1, source_target_pairs={{16,0},{20,4},{24,8},{28,12},{32,16},{36,20},{40,24},{44,28},{48,3... | collective-permute-start | bytes 393224 | tf_op jit(solution)/shard_map/ppermute | solution.py:26
  80.2 14.6 %collective-permute-start.7 = (bf16[256,256]{1,0:T(8,128)(2,1)S(1)}, bf16[256,256]{1,0:T(8,128)(2,1)S(1)}, u32[]{:S(2)}, u32[]{:S(2)}) collective-permute-start(bf16[256,256]{1,0:T(8,128)(2,1)S(1)} %constant_dynamic-update-slice_fusion.13), channel_id=1, source_target_pairs={{0,16},{4,20},{8,24},{12,28},{16,32},{20,36},{24,40},{28,44},{32,4... | collective-permute-start | bytes 393224 | tf_op jit(solution)/shard_map/ppermute | solution.py:26
  82.2 14.8 %collective-permute-start.8 = (bf16[256,256]{1,0:T(8,128)(2,1)S(1)}, bf16[256,256]{1,0:T(8,128)(2,1)S(1)}, u32[]{:S(2)}, u32[]{:S(2)}) collective-permute-start(bf16[256,256]{1,0:T(8,128)(2,1)S(1)} %constant_dynamic-update-slice_fusion.13), channel_id=1, source_target_pairs={{32,0},{36,4},{40,8},{44,12},{48,16},{52,20},{56,24},{60,28},{64,3... | collective-permute-start | bytes 393224 | tf_op jit(solution)/shard_map/ppermute | solution.py:26
  94.8 13.7 %collective-permute-start.9 = (bf16[256,256]{1,0:T(8,128)(2,1)S(1)}, bf16[256,256]{1,0:T(8,128)(2,1)S(1)}, u32[]{:S(2)}, u32[]{:S(2)}) collective-permute-start(bf16[256,256]{1,0:T(8,128)(2,1)S(1)} %constant_dynamic-update-slice_fusion.13), channel_id=1, source_target_pairs={{0,32},{4,36},{8,40},{12,44},{16,48},{20,52},{24,56},{28,60},{32,6... | collective-permute-start | bytes 393224 | tf_op jit(solution)/shard_map/ppermute | solution.py:26
  96.9 13.5 %collective-permute-start.10 = (bf16[256,256]{1,0:T(8,128)(2,1)S(1)}, bf16[256,256]{1,0:T(8,128)(2,1)S(1)}, u32[]{:S(2)}, u32[]{:S(2)}) collective-permute-start(bf16[256,256]{1,0:T(8,128)(2,1)S(1)} %constant_dynamic-update-slice_fusion.13), channel_id=1, source_target_pairs={{64,0},{68,4},{72,8},{76,12},{80,16},{84,20},{88,24},{92,28},{96,3... | collective-permute-start | bytes 393224 | tf_op jit(solution)/shard_map/ppermute | solution.py:26
  122.7 13.8 %collective-permute-start.17 = (bf16[256,256]{0,1:T(8,128)(2,1)S(1)}, bf16[256,256]{0,1:T(8,128)(2,1)S(1)}, u32[]{:S(2)}, u32[]{:S(2)}) collective-permute-start(bf16[256,256]{0,1:T(8,128)(2,1)S(1)} %get-tuple-element.34), channel_id=1, source_target_pairs={{0,8},{4,12},{8,16},{12,20},{16,24},{20,28},{24,32},{28,36},{32,40... | collective-permute-start | bytes 393224 | tf_op jit(solution)/shard_map/ppermute | solution.py:26
  124.7 14.9 %collective-permute-start.29 = (bf16[256,256]{0,1:T(8,128)(2,1)S(1)}, bf16[256,256]{0,1:T(8,128)(2,1)S(1)}, u32[]{:S(2)}, u32[]{:S(2)}) collective-permute-start(bf16[256,256]{0,1:T(8,128)(2,1)S(1)} %get-tuple-element.35), channel_id=1, source_target_pairs={{0,256},{4,260},{8,264},{12,268},{16,272},{20,276},{24,280},{28,28... | collective-permute-start | bytes 393224 | tf_op jit(solution)/shard_map/ppermute | solution.py:127
  126.6 16.6 %collective-permute-start.28 = (bf16[256,256]{0,1:T(8,128)(2,1)S(1)}, bf16[256,256]{0,1:T(8,128)(2,1)S(1)}, u32[]{:S(2)}, u32[]{:S(2)}) collective-permute-start(bf16[256,256]{0,1:T(8,128)(2,1)S(1)} %get-tuple-element.36), channel_id=1, source_target_pairs={{128,0},{132,4},{136,8},{140,12},{144,16},{148,20},{152,24},{156,2... | collective-permute-start | bytes 393224 | tf_op jit(solution)/shard_map/ppermute | solution.py:26
  128.5 20.8 %collective-permute-start.27 = (bf16[256,256]{0,1:T(8,128)(2,1)S(1)}, bf16[256,256]{0,1:T(8,128)(2,1)S(1)}, u32[]{:S(2)}, u32[]{:S(2)}) collective-permute-start(bf16[256,256]{0,1:T(8,128)(2,1)S(1)} %get-tuple-element.37), channel_id=1, source_target_pairs={{0,128},{4,132},{8,136},{12,140},{16,144},{20,148},{24,152},{28,15... | collective-permute-start | bytes 393224 | tf_op jit(solution)/shard_map/ppermute | solution.py:26
  133.3 22.9 %collective-permute-start.26 = (bf16[256,256]{0,1:T(8,128)(2,1)S(1)}, bf16[256,256]{0,1:T(8,128)(2,1)S(1)}, u32[]{:S(2)}, u32[]{:S(2)}) collective-permute-start(bf16[256,256]{0,1:T(8,128)(2,1)S(1)} %get-tuple-element.38), channel_id=1, source_target_pairs={{64,0},{68,4},{72,8},{76,12},{80,16},{84,20},{88,24},{92,28},{96,3... | collective-permute-start | bytes 393224 | tf_op jit(solution)/shard_map/ppermute | solution.py:26
  136.5 21.7 %collective-permute-start.25 = (bf16[256,256]{0,1:T(8,128)(2,1)S(1)}, bf16[256,256]{0,1:T(8,128)(2,1)S(1)}, u32[]{:S(2)}, u32[]{:S(2)}) collective-permute-start(bf16[256,256]{0,1:T(8,128)(2,1)S(1)} %get-tuple-element.39), channel_id=1, source_target_pairs={{0,64},{4,68},{8,72},{12,76},{16,80},{20,84},{24,88},{28,92},{32,9... | collective-permute-start | bytes 393224 | tf_op jit(solution)/shard_map/ppermute | solution.py:26
  139.6 23.0 %collective-permute-start.24 = (bf16[256,256]{0,1:T(8,128)(2,1)S(1)}, bf16[256,256]{0,1:T(8,128)(2,1)S(1)}, u32[]{:S(2)}, u32[]{:S(2)}) collective-permute-start(bf16[256,256]{0,1:T(8,128)(2,1)S(1)} %get-tuple-element.40), channel_id=1, source_target_pairs={{32,0},{36,4},{40,8},{44,12},{48,16},{52,20},{56,24},{60,28},{64,3... | collective-permute-start | bytes 393224 | tf_op jit(solution)/shard_map/ppermute | solution.py:26
  143.2 21.4 %collective-permute-start.23 = (bf16[256,256]{0,1:T(8,128)(2,1)S(1)}, bf16[256,256]{0,1:T(8,128)(2,1)S(1)}, u32[]{:S(2)}, u32[]{:S(2)}) collective-permute-start(bf16[256,256]{0,1:T(8,128)(2,1)S(1)} %get-tuple-element.41), channel_id=1, source_target_pairs={{0,32},{4,36},{8,40},{12,44},{16,48},{20,52},{24,56},{28,60},{32,6... | collective-permute-start | bytes 393224 | tf_op jit(solution)/shard_map/ppermute | solution.py:26
  149.4 30.8 %collective-permute-start.22 = (bf16[256,256]{0,1:T(8,128)(2,1)S(1)}, bf16[256,256]{0,1:T(8,128)(2,1)S(1)}, u32[]{:S(2)}, u32[]{:S(2)}) collective-permute-start(bf16[256,256]{0,1:T(8,128)(2,1)S(1)} %get-tuple-element.42), channel_id=1, source_target_pairs={{16,0},{20,4},{24,8},{28,12},{32,16},{36,20},{40,24},{44,28},{48,3... | collective-permute-start | bytes 393224 | tf_op jit(solution)/shard_map/ppermute | solution.py:26
  156.2 25.9 %collective-permute-start.21 = (bf16[256,256]{0,1:T(8,128)(2,1)S(1)}, bf16[256,256]{0,1:T(8,128)(2,1)S(1)}, u32[]{:S(2)}, u32[]{:S(2)}) collective-permute-start(bf16[256,256]{0,1:T(8,128)(2,1)S(1)} %get-tuple-element.43), channel_id=1, source_target_pairs={{0,16},{4,20},{8,24},{12,28},{16,32},{20,36},{24,40},{28,44},{32,4... | collective-permute-start | bytes 393224 | tf_op jit(solution)/shard_map/ppermute | solution.py:26
  158.2 28.5 %collective-permute-start.20 = (bf16[256,256]{0,1:T(8,128)(2,1)}, bf16[256,256]{0,1:T(8,128)(2,1)S(1)}, u32[]{:S(2)}, u32[]{:S(2)}) collective-permute-start(bf16[256,256]{0,1:T(8,128)(2,1)} %get-tuple-element.44), channel_id=1, source_target_pairs={{12,0},{16,4},{20,8},{24,12},{28,16},{32,20},{36,24},{40,28},{44,3... | collective-permute-start | bytes 393224 | tf_op jit(solution)/shard_map/ppermute | solution.py:26
  162.6 24.1 %collective-permute-start.19 = (bf16[256,256]{0,1:T(8,128)(2,1)S(1)}, bf16[256,256]{0,1:T(8,128)(2,1)S(1)}, u32[]{:S(2)}, u32[]{:S(2)}) collective-permute-start(bf16[256,256]{0,1:T(8,128)(2,1)S(1)} %get-tuple-element.45), channel_id=1, source_target_pairs={{0,12},{4,16},{8,20},{12,24},{16,28},{20,32},{24,36},{28,40},{32,4... | collective-permute-start | bytes 393224 | tf_op jit(solution)/shard_map/ppermute | solution.py:26
  164.6 22.2 %collective-permute-start.18 = (bf16[256,256]{0,1:T(8,128)(2,1)S(1)}, bf16[256,256]{0,1:T(8,128)(2,1)S(1)}, u32[]{:S(2)}, u32[]{:S(2)}) collective-permute-start(bf16[256,256]{0,1:T(8,128)(2,1)S(1)} %get-tuple-element.46), channel_id=1, source_target_pairs={{8,0},{12,4},{16,8},{20,12},{24,16},{28,20},{32,24},{36,28},{40,32... | collective-permute-start | bytes 393224 | tf_op jit(solution)/shard_map/ppermute | solution.py:26
  (10 other events, 328.8 us)

commit v4 on v0

v4 whole, which is shorter than its diff:
```python
import jax
import jax.numpy as jnp
import numpy as np
from jax import lax
from jax.sharding import Mesh
from jax.sharding import PartitionSpec as P

HD = 128
BLK = 128
ROW = 16
ROW_AXES = ("z", "c")


def offsets_for(frame_count):
    distances = [2, 3]
    power_step = 4
    while power_step < frame_count:
        distances.append(power_step)
        power_step = power_step * 2
    return [sign_value * distance_step for distance_step in distances for sign_value in (1, -1)]


def far_window(entries, is_valid):
    pair_start = jnp.maximum(entries[0], 0)
    pair_index = jnp.arange(2, dtype=jnp.int32)
    far_hit = (
        is_valid & (entries[:, None] >= 0) & (entries[:, None] - pair_start == pair_index[None, :])
    )
    far_hit = jnp.repeat(jnp.repeat(far_hit, BLK, axis=0), BLK, axis=1)
    return (pair_start, far_hit)


def attend_parts(queries, grads_out, keys_all, visible):
    score_scale = HD ** (-0.5)
    across = (((1,), (1,)), ((), ()))
    key_part = keys_all[:, :HD]
    value_part = keys_all[:, HD:]
    scores = (
        lax.dot_general(queries, key_part, across, preferred_element_type=jnp.float32) * score_scale
    )
    scores = jnp.where(visible, scores, -jnp.inf)
    row_max = jnp.max(scores, axis=1, keepdims=True)
    row_total = jnp.sum(jnp.exp(scores - row_max), axis=1, keepdims=True)
    log_total = row_max + jnp.log(row_total)
    weights = jnp.exp(scores - log_total).astype(jnp.bfloat16)
    out_rows = jnp.dot(weights, value_part, preferred_element_type=jnp.float32)
    row_delta = jnp.sum(out_rows * grads_out.astype(jnp.float32), axis=1, keepdims=True)
    dweights = lax.dot_general(grads_out, value_part, across, preferred_element_type=jnp.float32)
    dscores = (weights.astype(jnp.float32) * (dweights - row_delta)).astype(jnp.bfloat16)
    query_rows_grad = jnp.dot(dscores, key_part, preferred_element_type=jnp.float32) * score_scale
    return (out_rows, query_rows_grad, weights, dscores)


def key_terms(weights, dscores, queries, grads_out):
    score_scale = HD ** (-0.5)
    over_rows = (((0,), (0,)), ((), ()))
    key_side = (
        lax.dot_general(dscores, queries, over_rows, preferred_element_type=jnp.float32)
        * score_scale
    )
    value_side = lax.dot_general(weights, grads_out, over_rows, preferred_element_type=jnp.float32)
    return jnp.concatenate([key_side, value_side], axis=1)


def swap_pairs(frame_count):
    half = ROW // 2
    pairs = []
    for source in range(frame_count):
        target = source - half if source % ROW < half else source + half
        if 0 <= target < frame_count:
            pairs.append((source, target))
    return pairs


def shards(query_tokens, key_tokens, value_tokens, grad_out, far_block):
    tok_rows = query_tokens.shape[0]
    cols = lax.axis_size("y")
    frame_count = cols * ROW
    half = ROW // 2
    y = lax.axis_index("y")
    w = lax.axis_index("z") * lax.axis_size("c") + lax.axis_index("c")
    device = y * ROW + w
    offsets = offsets_for(frame_count)
    seq_axes = ("y",) + ROW_AXES

    joined = jnp.concatenate([key_tokens, value_tokens], axis=1)
    own_row = lax.all_gather(joined, ROW_AXES)
    swapped = lax.ppermute(joined, seq_axes, swap_pairs(frame_count))
    near_rows = lax.all_gather(swapped, ROW_AXES)
    column = lax.all_gather(joined, "y")
    table = jnp.concatenate([near_rows[:half], own_row, near_rows[half:]], axis=0)

    def row_frame(offset):
        index = jnp.clip(w + offset + half, 0, 2 * ROW - 1)
        return lax.dynamic_index_in_dim(table, index, 0, keepdims=False)

    def column_frame(offset):
        index = jnp.clip(y + offset // ROW, 0, cols - 1)
        return lax.dynamic_index_in_dim(column, index, 0, keepdims=False)

    def fetch(offset):
        return row_frame(offset) if abs(offset) <= half else column_frame(offset)

    near_keys = jnp.concatenate([row_frame(-1), joined, row_frame(1)], axis=0)
    neighbour = device + jnp.arange(3, dtype=jnp.int32) - 1
    near_ok = jnp.repeat((neighbour >= 0) & (neighbour < frame_count), tok_rows)
    pieces = [near_keys]
    mask_list = [jnp.broadcast_to(near_ok[None, :], (tok_rows, 3 * tok_rows))]
    for offset in offsets:
        arrived = fetch(offset)
        other_frame = device + offset
        is_valid = (other_frame >= 0) & (other_frame < frame_count)
        safe_frame = jnp.clip(other_frame, 0, frame_count - 1)
        entries = far_block[device, safe_frame]
        pair_start, far_hit = far_window(entries, is_valid)
        pieces.append(arrived)
        mask_list.append(far_hit)
    keys_all = jnp.concatenate(pieces, axis=0)
    visible = jnp.concatenate(mask_list, axis=1)
    attention_out, query_grad, weights, dscores = attend_parts(
        query_tokens, grad_out, keys_all, visible
    )
    terms = key_terms(weights, dscores, query_tokens, grad_out)

    near_table = jnp.zeros((2 * ROW,) + joined.shape, jnp.float32)
    far_column = jnp.zeros((cols,) + joined.shape, jnp.float32)
    term_offsets = [-1, 1] + offsets
    term_rows = [0, 2 * tok_rows] + [(3 + i) * tok_rows for i in range(len(offsets))]
    for offset, first in zip(term_offsets, term_rows):
        piece = terms[first : first + tok_rows]
        if abs(offset) <= half:
            index = jnp.clip(w + offset + half, 0, 2 * ROW - 1)
            current = lax.dynamic_index_in_dim(near_table, index, 0, keepdims=True)
            near_table = lax.dynamic_update_index_in_dim(near_table, current + piece[None], index, 0)
        else:
            index = jnp.clip(y + offset // ROW, 0, cols - 1)
            current = lax.dynamic_index_in_dim(far_column, index, 0, keepdims=True)
            far_column = lax.dynamic_update_index_in_dim(far_column, current + piece[None], index, 0)
    own_sum = lax.psum_scatter(near_table[half : half + ROW], ROW_AXES, scatter_dimension=0)
    side = jnp.concatenate([near_table[:half], near_table[half + ROW :]], axis=0)
    side_sum = lax.psum_scatter(side, ROW_AXES, scatter_dimension=0)
    side_back = lax.ppermute(side_sum, seq_axes, swap_pairs(frame_count))
    column_sum = lax.psum_scatter(far_column, "y", scatter_dimension=0)
    grad_total = terms[tok_rows : 2 * tok_rows] + own_sum + side_back + column_sum
    key_grad = grad_total[:, :HD]
    value_grad = grad_total[:, HD:]
    return (attention_out, query_grad, key_grad, value_grad)


def solution(mesh):
    seq_count, head_count = mesh.devices.shape
    cols = seq_count // ROW
    devices = np.asarray(mesh.devices).reshape(cols, ROW // 2, 2, head_count)
    grid = Mesh(devices, ("y",) + ROW_AXES + ("head",))
    seq = ("y",) + ROW_AXES
    return jax.shard_map(
        shards,
        mesh=grid,
        in_specs=(P(seq, "head"), P(seq, "head"), P(seq, "head"), P(seq, "head"), P()),
        out_specs=(P(seq, "head"), P(seq, "head"), P(seq, "head"), P(seq, "head")),
        check_vma=False,
    )
```

time: 231 us -> 371 us (1.61)
  the two profiles are of different devices: /device:TPU:88 before, /device:TPU:1 now
where the time goes in v4:
time: 371 us; the launch traced here: 368 us
  waiting for transfers between devices  269 us (73%)
  local copies, waits for them, and re-layouts  44.4 us (12%)
  between operations  23.7 us (6%)
  other arithmetic  19.4 us (5%)
  matrix products  9.56 us (3%)
    reduce_scatter x1, waiting for transfers between devices, shards(): lax.psum_scatter(near_table[half:half + ROW], ROW_AXES, scatter_dimension=0)  69 us
    reduce_scatter x1, waiting for transfers between devices, shards(): side_sum = lax.psum_scatter(side, ROW_AXES, scatter_dimension=0)  52.7 us
    all_gather x1, waiting for transfers between devices, shards(): own_row = lax.all_gather(joined, ROW_AXES)  42.3 us
    reduce_scatter x1, waiting for transfers between devices, shards(): column_sum = lax.psum_scatter(far_column, 'y', scatter_dimension=0)  40.2 us
    all_gather x1, waiting for transfers between devices, shards(): column = lax.all_gather(joined, 'y')  34.3 us
    all_gather x1, waiting for transfers between devices, shards(): near_rows = lax.all_gather(swapped, ROW_AXES)  29.3 us
    unnamed x90, local copies, waits for them, and re-layouts  26.4 us
    dynamic_update_slice x5, other arithmetic, shards(): lax.dynamic_update_index_in_dim(far_column, current + piece[None], index, 0)  8.64 us
  transfers between devices with their start and end apart: 8, of which 6 were waited for; matrix products, arithmetic and copies ran while one was open for 12% of the time, Pallas kernels for 0%

profile of v4, /device:TPU:1, one launch (start us, length us, event | category | flops | bytes accessed | tf_op | source)
XLA Modules:
  0.0 367.9 jit_solution(15289953752193415001)
XLA Ops:
  12.1 1.2 and_reduce_fusion.1
  21.0 1.3 and_reduce_fusion
  33.3 0.9 copy.9
  44.4 29.3 %all-gather.7.cloned.1.call-done = bf16[4096,256]{1,0:T(8,128)(2,1)} async-done(((bf16[256,256]{1,0:T(8,128)(2,1)}), bf16[4096,256]{1,0:T(8,128)(2,1)}) %all-gather.7.cloned.1.call-update) | async-done | bytes 2097168 | tf_op jit(solution)/shard_map/all_gather | solution.py:89
  73.6 1.7 fusion.44
  75.3 42.3 %all-gather.9.cloned.1.call-done = bf16[4096,256]{1,0:T(8,128)(2,1)} async-done(((bf16[256,256]{1,0:T(8,128)(2,1)}), bf16[4096,256]{1,0:T(8,128)(2,1)}) %all-gather.9.cloned.1.call-update) | async-done | bytes 2097168 | tf_op jit(solution)/shard_map/all_gather | solution.py:87
  117.6 1.8 pad_maximum_fusion
  119.8 34.3 %all-gather.11.cloned.1.call-done = bf16[2048,256]{1,0:T(8,128)(2,1)} async-done(((bf16[256,256]{1,0:T(8,128)(2,1)}), bf16[2048,256]{1,0:T(8,128)(2,1)}) %all-gather.11.cloned.1.call-update) | async-done | bytes 1048592 | tf_op jit(solution)/shard_map/all_gather | solution.py:90
  159.7 3.0 fusion.46
  167.3 1.4 copy-done.5
  171.3 1.4 copy-done.4
  173.0 2.8 copy-done.3
  175.9 2.4 pad_maximum_fusion.1
  178.4 1.9 fusion.33
  180.2 1.7 fusion.32
  181.9 1.7 fusion.31
  183.6 1.7 fusion.30
  185.3 1.7 fusion.29
  187.1 4.5 %slice.202 = f32[16,256,256]{1,2,0:T(8,128)} slice(f32[32,256,256]{1,2,0:T(8,128)} %copy-done.3), slice={[8:24], [0:256], [0:256]} | slice | bytes 8388608 | tf_op jit(solution)/shard_map/slice | solution.py:139
  192.4 52.7 %reduce-scatter.6.cloned.1.call-done = f32[1,256,256]{1,2,0:T(8,128)} async-done(((f32[16,256,256]{1,2,0:T(8,128)}), f32[1,256,256]{1,2,0:T(8,128)}) %reduce-scatter.6.cloned.1.call-update) | async-done | bytes 262160 | tf_op jit(solution)/shard_map/reduce_scatter | solution.py:141
  245.8 3.4 convolution_multiply_fusion.2
  249.1 40.2 %reduce-scatter.8.cloned.1.call-done = f32[1,256,256]{1,2,0:T(8,128)} async-done(((f32[8,256,256]{1,2,0:T(8,128)}), f32[1,256,256]{1,2,0:T(8,128)}) %reduce-scatter.8.cloned.1.call-update) | async-done | bytes 262160 | tf_op jit(solution)/shard_map/reduce_scatter | solution.py:143
  289.4 69.0 %reduce-scatter.4.cloned.1.call-done = f32[1,256,256]{1,2,0:T(8,128)} async-done(((f32[16,256,256]{1,2,0:T(8,128)}), f32[1,256,256]{1,2,0:T(8,128)}) %reduce-scatter.4.cloned.1.call-update) | async-done | bytes 262160 | tf_op jit(solution)/shard_map/reduce_scatter | solution.py:139
  358.4 1.1 bitcast_add_fusion
  (178 shorter events, 40.8 us)
Async XLA Ops:
  7.2 152.5 %copy-start = (bf16[256,128]{1,0:T(8,128)(2,1)S(1)}, bf16[256,128]{1,0:T(8,128)(2,1)}, u32[]{:S(2)}) copy-start(bf16[256,128]{1,0:T(8,128)(2,1)} %param.5) | copy-start | bytes 196612
  7.2 66.4 %all-gather.7.cloned.1.call-start = ((), (), s32[]{:S(2)}) async-start(), calls=%async_computation.6 | async-start | bytes 2228224 | tf_op jit(solution)/shard_map/all_gather | solution.py:89
  8.9 1.4 copy-start.6
  9.0 0.7 collective-permute-start
  9.6 0.7 copy-start.12
  10.3 107.3 %all-gather.9.cloned.1.call-start = ((), (), s32[]{:S(2)}) async-start(), calls=%async_computation.7 | async-start | bytes 2228224 | tf_op jit(solution)/shard_map/all_gather | solution.py:87
  11.1 143.0 %all-gather.11.cloned.1.call-start = ((), (), s32[]{:S(2)}) async-start(), calls=%async_computation.8 | async-start | bytes 1179648 | tf_op jit(solution)/shard_map/all_gather | solution.py:90
  11.8 233.3 %reduce-scatter.6.cloned.1.call-start = ((), (), s32[]{:S(2)}) async-start(), calls=%async_computation.4 | async-start | bytes 4456448 | tf_op jit(solution)/shard_map/reduce_scatter | solution.py:141
  117.6 1.9 copy-start.10
  117.6 1.9 copy-start.11
  159.7 3.1 copy-start.7
  163.4 0.8 copy-start.9
  164.2 1.6 copy-start.8
  167.3 1.4 copy-start.5
  169.5 1.6 copy-start.1
  171.3 1.4 copy-start.4
  172.6 3.2 copy-start.3
  178.3 111.1 %reduce-scatter.8.cloned.1.call-start = ((), (), s32[]{:S(2)}) async-start(), calls=%async_computation.5 | async-start | bytes 2359296 | tf_op jit(solution)/shard_map/reduce_scatter | solution.py:143
  178.3 1.9 copy-start.2
  187.0 171.4 %reduce-scatter.4.cloned.1.call-start = ((), (), s32[]{:S(2)}) async-start(), calls=%async_computation.3 | async-start | bytes 4456448 | tf_op jit(solution)/shard_map/reduce_scatter | solution.py:139
  245.1 113.3 %collective-permute-start.1 = (f32[256,256]{0,1:T(8,128)}, f32[256,256]{0,1:T(8,128)S(1)}, u32[]{:S(2)}, u32[]{:S(2)}) collective-permute-start(f32[256,256]{0,1:T(8,128)} %bitcast.286), channel_id=1, source_target_pairs={{32,64},{36,68},{40,72},{44,76},{48,80},{52,84},{56,88},{60,92},{6... | collective-permute-start | bytes 786440 | tf_op jit(solution)/shard_map/ppermute | solution.py:142
Sparse Core Ops, SparseCore 0:
  10.7 62.8 all-gather.6
  76.3 41.2 all-gather.8
  120.3 33.8 all-gather.10
  178.4 66.6 reduce-scatter.5
  247.8 41.5 reduce-scatter.7
  292.1 66.2 reduce-scatter.3

commit v5 on v3

--- a/solution.py
+++ b/solution.py
@@ -77,13 +77,53 @@
     return jnp.concatenate([key_side, value_side], axis=1)
 
 
+RELAY = (
+    (1, (0,)),
+    (-8, (0,)),
+    (16, (0,)),
+    (2, (0, 1)),
+    (-32, (0, 16)),
+    (-4, (0, 1, 2, 3)),
+    (64, (0, -32)),
+    (8, (0, -4)),
+)
+
+
+def cyclic(value, axis, shift):
+    count = lax.axis_size(axis)
+    return lax.ppermute(value, axis, [(source, (source - shift) % count) for source in range(count)])
+
+
+def relay_gather(own, axis):
+    rows = own.shape[0]
+    held = {0: own}
+    for shift, sent in RELAY:
+        got = cyclic(jnp.concatenate([held[e] for e in sent], axis=0), axis, shift)
+        for j, e in enumerate(sent):
+            held[e + shift] = got[j * rows : (j + 1) * rows]
+    return held
+
+
+def relay_return(terms, axis):
+    acc = dict(terms)
+    rows = acc[0].shape[0]
+    for shift, sent in reversed(RELAY):
+        buf = jnp.concatenate([acc.pop(e + shift).astype(jnp.bfloat16) for e in sent], axis=0)
+        got = cyclic(buf, axis, -shift).astype(jnp.float32)
+        for j, e in enumerate(sent):
+            part = got[j * rows : (j + 1) * rows]
+            acc[e] = acc[e] + part if e in acc else part
+    return acc[0]
+
+
 def shards(query_tokens, key_tokens, value_tokens, grad_out, far_block):
     tok_rows = query_tokens.shape[0]
     frame_count = lax.axis_size("seq")
     device = lax.axis_index("seq")
     offsets = offsets_for(frame_count)
     joined = jnp.concatenate([key_tokens, value_tokens], axis=1)
-    near_keys = extended(joined, (("seq", 0),), tok_rows)
+    held = relay_gather(joined, "seq")
+    near_keys = jnp.concatenate([held[-1], joined, held[1]], axis=0)
     neighbour = device + jnp.arange(3, dtype=jnp.int32) - 1
     near_ok = jnp.repeat((neighbour >= 0) & (neighbour < frame_count), tok_rows)
     pieces = [near_keys]
@@ -91,13 +131,10 @@
     half = frame_count // 2
     offsets = [o for o in offsets if o != -half]
     for offset in offsets:
+        arrived = held[offset]
         if offset == half:
-            arrived = lax.ppermute(
-                joined, "seq", [(src, (src + half) % frame_count) for src in range(frame_count)]
-            )
             other_frame = (device + half) % frame_count
         else:
-            arrived = from_behind(joined, "seq", -offset)
             other_frame = device + offset
         is_valid = (other_frame >= 0) & (other_frame < frame_count)
         safe_frame = jnp.clip(other_frame, 0, frame_count - 1)
@@ -110,28 +147,16 @@
     attention_out, query_grad, weights, dscores, log_total, row_delta = attend_parts(
         query_tokens, grad_out, keys_all, visible
     )
-    near_terms = key_terms(
-        weights[:, : 3 * tok_rows], dscores[:, : 3 * tok_rows], query_tokens, grad_out
-    )
-    sent = near_terms.astype(jnp.bfloat16)
-    from_after = from_behind(sent[:tok_rows], "seq", -1).astype(jnp.float32)
-    from_before = from_behind(sent[2 * tok_rows :], "seq", 1).astype(jnp.float32)
-    grad_total = near_terms[tok_rows : 2 * tok_rows] + from_after + from_before
-    far_terms = key_terms(
-        weights[:, 3 * tok_rows :], dscores[:, 3 * tok_rows :], query_tokens, grad_out
-    )
-    for slot_index in range(len(offsets)):
-        first_row = slot_index * 2 * BLK
-        grad_piece = far_terms[first_row : first_row + 2 * BLK].astype(jnp.bfloat16)
-        if offsets[slot_index] == half:
-            returned = lax.ppermute(
-                grad_piece, "seq", [(src, (src + half) % frame_count) for src in range(frame_count)]
-            )
-        else:
-            returned = from_behind(grad_piece, "seq", offsets[slot_index])
-        returned = returned.astype(jnp.float32)
-        current = grad_total
-        grad_total = current + returned
+    terms = key_terms(weights, dscores, query_tokens, grad_out)
+    by_offset = {
+        -1: terms[:tok_rows],
+        0: terms[tok_rows : 2 * tok_rows],
+        1: terms[2 * tok_rows : 3 * tok_rows],
+    }
+    for slot_index, offset in enumerate(offsets):
+        first_row = (3 + slot_index) * tok_rows
+        by_offset[offset] = terms[first_row : first_row + tok_rows]
+    grad_total = relay_return(by_offset, "seq")
     key_grad = grad_total[:, :HD]
     value_grad = grad_total[:, HD:]
     return (attention_out, query_grad, key_grad, value_grad)

time: 195 us -> 207 us (1.062)
  the two profiles are of different devices: /device:TPU:36 before, /device:TPU:1 now
where the time goes in v5:
time: 207 us; the launch traced here: 204 us
  waiting for transfers between devices  83.4 us (40%)
  starting transfers between devices  75.4 us (36%)
  local copies, waits for them, and re-layouts  18.6 us (9%)
  between operations  10.1 us (5%)
  other arithmetic  8.25 us (4%)
  matrix products  7.89 us (4%)
    ppermute x16, waiting for transfers between devices, cyclic(): lax.ppermute(value, axis, [(source, (source - shift) % count) for source...  83.4 us
    ppermute x16, starting transfers between devices, cyclic(): lax.ppermute(value, axis, [(source, (source - shift) % count) for source...  75.4 us
    unnamed x82, local copies, waits for them, and re-layouts  9.71 us
    slice x13, local copies, waits for them, and re-layouts, far_window(): pair_start = jnp.maximum(entries[0], 0)  6.84 us
  transfers between devices with their start and end apart: 16, of which 9 were waited for; matrix products, arithmetic and copies ran while one was open for 9% of the time, Pallas kernels for 0%

profile of v5, /device:TPU:1, one launch (start us, length us, event | category | flops | bytes accessed | tf_op | source)
XLA Modules:
  0.0 203.6 jit_solution(15667988909325552478)
XLA Ops:
  2.4 11.5 %collective-permute-start.4 = (bf16[256,256]{1,0:T(8,128)(2,1)S(1)}, bf16[256,256]{1,0:T(8,128)(2,1)S(1)}, u32[]{:S(2)}, u32[]{:S(2)}) collective-permute-start(bf16[256,256]{1,0:T(8,128)(2,1)S(1)} %constant_dynamic-update-slice_fusion.13), channel_id=1, source_target_pairs={{0,32},{4,36},{8,40},{12,44},{16,48},{20,52},{24,56},{28,60},{32,6... | collective-permute-start | bytes 393224 | tf_op jit(solution)/shard_map/ppermute | solution.py:94
  13.9 5.1 %collective-permute-start.5 = (bf16[256,256]{1,0:T(8,128)(2,1)S(1)}, bf16[256,256]{1,0:T(8,128)(2,1)S(1)}, u32[]{:S(2)}, u32[]{:S(2)}) collective-permute-start(bf16[256,256]{1,0:T(8,128)(2,1)S(1)} %constant_dynamic-update-slice_fusion.13), channel_id=1, source_target_pairs={{0,448},{4,452},{8,456},{12,460},{16,464},{20,468},{24,472},{28,47... | collective-permute-start | bytes 393224 | tf_op jit(solution)/shard_map/ppermute | solution.py:94
  19.0 3.1 %collective-permute-start = (bf16[256,256]{1,0:T(8,128)(2,1)S(1)}, bf16[256,256]{1,0:T(8,128)(2,1)S(1)}, u32[]{:S(2)}, u32[]{:S(2)}) collective-permute-start(bf16[256,256]{1,0:T(8,128)(2,1)S(1)} %constant_dynamic-update-slice_fusion.13), channel_id=1, source_target_pairs={{0,508},{4,0},{8,4},{12,8},{16,12},{20,16},{24,20},{28,24},{32,28}... | collective-permute-start | bytes 393224 | tf_op jit(solution)/shard_map/ppermute | solution.py:94
  42.7 2.5 %collective-permute-start.1 = (bf16[512,256]{1,0:T(8,128)(2,1)S(1)}, bf16[512,256]{1,0:T(8,128)(2,1)S(1)}, u32[]{:S(2)}, u32[]{:S(2)}) collective-permute-start(bf16[512,256]{1,0:T(8,128)(2,1)S(1)} %pad_maximum_fusion.6), channel_id=1, source_target_pairs={{0,504},{4,508},{8,0},{12,4},{16,8},{20,12},{24,16},{28,20},{32,24... | collective-permute-start | bytes 786440 | tf_op jit(solution)/shard_map/ppermute | solution.py:94
  45.4 7.2 %collective-permute-done.1 = bf16[512,256]{1,0:T(8,128)(2,1)S(1)} collective-permute-done((bf16[512,256]{1,0:T(8,128)(2,1)S(1)}, bf16[512,256]{1,0:T(8,128)(2,1)S(1)}, u32[]{:S(2)}, u32[]{:S(2)}) %collective-permute-start.1) | collective-permute-done | bytes 262176 | tf_op jit(solution)/shard_map/ppermute | solution.py:94
  52.6 4.0 %collective-permute-start.2 = (bf16[1024,256]{1,0:T(8,128)(2,1)S(1)}, bf16[1024,256]{1,0:T(8,128)(2,1)S(1)}, u32[]{:S(2)}, u32[]{:S(2)}) collective-permute-start(bf16[1024,256]{1,0:T(8,128)(2,1)S(1)} %pad_maximum_fusion.1), channel_id=1, source_target_pairs={{0,16},{4,20},{8,24},{12,28},{16,32},{20,36},{24,40},{28,44},{32,4... | collective-permute-start | bytes 1572872 | tf_op jit(solution)/shard_map/ppermute | solution.py:94
  56.7 24.7 %collective-permute-done.2 = bf16[1024,256]{1,0:T(8,128)(2,1)S(1)} collective-permute-done((bf16[1024,256]{1,0:T(8,128)(2,1)S(1)}, bf16[1024,256]{1,0:T(8,128)(2,1)S(1)}, u32[]{:S(2)}, u32[]{:S(2)}) %collective-permute-start.2) | collective-permute-done | bytes 524320 | tf_op jit(solution)/shard_map/ppermute | solution.py:94
  81.7 1.9 collective-permute-start.3
  85.7 9.9 %collective-permute-done.3 = bf16[512,256]{1,0:T(8,128)(2,1)S(1)} collective-permute-done((bf16[512,256]{1,0:T(8,128)(2,1)S(1)}, bf16[512,256]{1,0:T(8,128)(2,1)S(1)}, u32[]{:S(2)}, u32[]{:S(2)}) %collective-permute-start.3) | collective-permute-done | bytes 262176 | tf_op jit(solution)/shard_map/ppermute | solution.py:94
  95.6 4.0 %collective-permute-done.6 = bf16[512,256]{1,0:T(8,128)(2,1)S(1)} collective-permute-done((bf16[512,256]{1,0:T(8,128)(2,1)S(1)}, bf16[512,256]{1,0:T(8,128)(2,1)S(1)}, u32[]{:S(2)}, u32[]{:S(2)}) %collective-permute-start.6) | collective-permute-done | bytes 262176 | tf_op jit(solution)/shard_map/ppermute | solution.py:94
  99.7 2.2 %collective-permute-start.7 = (bf16[512,256]{1,0:T(8,128)(2,1)S(1)}, bf16[512,256]{1,0:T(8,128)(2,1)S(1)}, u32[]{:S(2)}, u32[]{:S(2)}) collective-permute-start(bf16[512,256]{1,0:T(8,128)(2,1)S(1)} %pad_maximum_fusion.3), channel_id=1, source_target_pairs={{0,256},{4,260},{8,264},{12,268},{16,272},{20,276},{24,280},{28,28... | collective-permute-start | bytes 786440 | tf_op jit(solution)/shard_map/ppermute | solution.py:94
  104.4 10.0 %collective-permute-done.7 = bf16[512,256]{1,0:T(8,128)(2,1)S(1)} collective-permute-done((bf16[512,256]{1,0:T(8,128)(2,1)S(1)}, bf16[512,256]{1,0:T(8,128)(2,1)S(1)}, u32[]{:S(2)}, u32[]{:S(2)}) %collective-permute-start.7) | collective-permute-done | bytes 262176 | tf_op jit(solution)/shard_map/ppermute | solution.py:94
  114.5 2.9 %fusion.38 = (f32[256]{0:T(256)S(1)}, f32[256,4096]{0,1:T(8,128)S(1)}) fusion(pred[256,4096]{0,1:T(8,128)(4,1)} %constant_dynamic-update-slice_fusion, bf16[256,128]{1,0:T(8,128)(2,1)S(1)} %copy-done, bf16[4096,256]{1,0:T(8,128)(2,1)S(1)} %slice_dynamic-update-slice_fusion), kind=kOutput, calls=%fused_computation.188 | convolution fusion | flops 271580928 | bytes 6358016 | tf_op jit(solution)/shard_map/dot_general | solution.py:54
  123.5 2.0 collective-permute-start.9
  127.4 10.2 %collective-permute-done.9 = bf16[512,256]{0,1:T(8,128)(2,1)S(1)} collective-permute-done((bf16[512,256]{0,1:T(8,128)(2,1)S(1)}, bf16[512,256]{0,1:T(8,128)(2,1)S(1)}, u32[]{:S(2)}, u32[]{:S(2)}) %collective-permute-start.9) | collective-permute-done | bytes 262176 | tf_op jit(solution)/shard_map/ppermute | solution.py:94
  138.5 4.9 %collective-permute-start.11 = (bf16[512,256]{0,1:T(8,128)(2,1)S(1)}, bf16[512,256]{0,1:T(8,128)(2,1)S(1)}, u32[]{:S(2)}, u32[]{:S(2)}) collective-permute-start(bf16[512,256]{0,1:T(8,128)(2,1)S(1)} %pad_maximum_fusion.9), channel_id=1, source_target_pairs={{0,384},{4,388},{8,392},{12,396},{16,400},{20,404},{24,408},{28,41... | collective-permute-start | bytes 786440 | tf_op jit(solution)/shard_map/ppermute | solution.py:94
  143.4 3.3 %collective-permute-done.8 = bf16[512,256]{0,1:T(8,128)(2,1)S(1)} collective-permute-done((bf16[512,256]{0,1:T(8,128)(2,1)S(1)}, bf16[512,256]{0,1:T(8,128)(2,1)S(1)}, u32[]{:S(2)}, u32[]{:S(2)}) %collective-permute-start.8) | collective-permute-done | bytes 262176 | tf_op jit(solution)/shard_map/ppermute | solution.py:94
  146.8 3.4 %collective-permute-done.11 = bf16[512,256]{0,1:T(8,128)(2,1)S(1)} collective-permute-done((bf16[512,256]{0,1:T(8,128)(2,1)S(1)}, bf16[512,256]{0,1:T(8,128)(2,1)S(1)}, u32[]{:S(2)}, u32[]{:S(2)}) %collective-permute-start.11) | collective-permute-done | bytes 262176 | tf_op jit(solution)/shard_map/ppermute | solution.py:94
  151.1 1.9 collective-permute-start.10
  153.1 10.7 %collective-permute-done.10 = bf16[1024,256]{0,1:T(8,128)(2,1)S(1)} collective-permute-done((bf16[1024,256]{0,1:T(8,128)(2,1)S(1)}, bf16[1024,256]{0,1:T(8,128)(2,1)S(1)}, u32[]{:S(2)}, u32[]{:S(2)}) %collective-permute-start.10) | collective-permute-done | bytes 524320 | tf_op jit(solution)/shard_map/ppermute | solution.py:94
  164.0 19.4 %collective-permute-start.12 = (bf16[512,256]{0,1:T(8,128)(2,1)S(1)}, bf16[512,256]{0,1:T(8,128)(2,1)S(1)}, u32[]{:S(2)}, u32[]{:S(2)}) collective-permute-start(bf16[512,256]{0,1:T(8,128)(2,1)S(1)} %pad_maximum_fusion.10), channel_id=1, source_target_pairs={{0,8},{4,12},{8,16},{12,20},{16,24},{20,28},{24,32},{28,36},{32,40... | collective-permute-start | bytes 786440 | tf_op jit(solution)/shard_map/ppermute | solution.py:94
  183.4 3.0 %collective-permute-start.14 = (bf16[256,256]{0,1:T(8,128)(2,1)S(1)}, bf16[256,256]{0,1:T(8,128)(2,1)}, u32[]{:S(2)}, u32[]{:S(2)}) collective-permute-start(bf16[256,256]{0,1:T(8,128)(2,1)S(1)} %get-tuple-element.38), channel_id=1, source_target_pairs={{0,480},{4,484},{8,488},{12,492},{16,496},{20,500},{24,504},{28,50... | collective-permute-start | bytes 393224 | tf_op jit(solution)/shard_map/ppermute | solution.py:94
  186.4 4.3 %collective-permute-start.13 = (bf16[256,256]{0,1:T(8,128)(2,1)S(1)}, bf16[256,256]{0,1:T(8,128)(2,1)}, u32[]{:S(2)}, u32[]{:S(2)}) collective-permute-start(bf16[256,256]{0,1:T(8,128)(2,1)S(1)} %get-tuple-element.36), channel_id=1, source_target_pairs={{0,64},{4,68},{8,72},{12,76},{16,80},{20,84},{24,88},{28,92},{32,9... | collective-permute-start | bytes 393224 | tf_op jit(solution)/shard_map/ppermute | solution.py:94
  191.7 5.8 %collective-permute-start.15 = (bf16[256,256]{0,1:T(8,128)(2,1)}, bf16[256,256]{0,1:T(8,128)(2,1)}, u32[]{:S(2)}, u32[]{:S(2)}) collective-permute-start(bf16[256,256]{0,1:T(8,128)(2,1)} %fusion.25), channel_id=1, source_target_pairs={{0,4},{4,8},{8,12},{12,16},{16,20},{20,24},{24,28},{28,32},{32,36}... | collective-permute-start | bytes 393224 | tf_op jit(solution)/shard_map/ppermute | solution.py:94
  (177 shorter events, 35.7 us)
Async XLA Ops:
  0.6 113.8 %copy-start = (bf16[256,128]{1,0:T(8,128)(2,1)S(1)}, bf16[256,128]{1,0:T(8,128)(2,1)}, u32[]{:S(2)}) copy-start(bf16[256,128]{1,0:T(8,128)(2,1)} %param.5) | copy-start | bytes 196612
  2.4 93.2 %collective-permute-start.4 = (bf16[256,256]{1,0:T(8,128)(2,1)S(1)}, bf16[256,256]{1,0:T(8,128)(2,1)S(1)}, u32[]{:S(2)}, u32[]{:S(2)}) collective-permute-start(bf16[256,256]{1,0:T(8,128)(2,1)S(1)} %constant_dynamic-update-slice_fusion.13), channel_id=1, source_target_pairs={{0,32},{4,36},{8,40},{12,44},{16,48},{20,52},{24,56},{28,60},{32,6... | collective-permute-start | bytes 393224 | tf_op jit(solution)/shard_map/ppermute | solution.py:94
  13.9 67.8 %collective-permute-start.5 = (bf16[256,256]{1,0:T(8,128)(2,1)S(1)}, bf16[256,256]{1,0:T(8,128)(2,1)S(1)}, u32[]{:S(2)}, u32[]{:S(2)}) collective-permute-start(bf16[256,256]{1,0:T(8,128)(2,1)S(1)} %constant_dynamic-update-slice_fusion.13), channel_id=1, source_target_pairs={{0,448},{4,452},{8,456},{12,460},{16,464},{20,468},{24,472},{28,47... | collective-permute-start | bytes 393224 | tf_op jit(solution)/shard_map/ppermute | solution.py:94
  19.0 23.7 %collective-permute-start = (bf16[256,256]{1,0:T(8,128)(2,1)S(1)}, bf16[256,256]{1,0:T(8,128)(2,1)S(1)}, u32[]{:S(2)}, u32[]{:S(2)}) collective-permute-start(bf16[256,256]{1,0:T(8,128)(2,1)S(1)} %constant_dynamic-update-slice_fusion.13), channel_id=1, source_target_pairs={{0,508},{4,0},{8,4},{12,8},{16,12},{20,16},{24,20},{28,24},{32,28}... | collective-permute-start | bytes 393224 | tf_op jit(solution)/shard_map/ppermute | solution.py:94
  22.2 59.2 %copy-start.9 = (bf16[256,128]{1,0:T(8,128)(2,1)S(1)}, bf16[256,128]{1,0:T(8,128)(2,1)}, u32[]{:S(2)}) copy-start(bf16[256,128]{1,0:T(8,128)(2,1)} %param.6) | copy-start | bytes 196612
  28.7 52.8 %copy-start.10 = (bf16[256,128]{1,0:T(8,128)(2,1)S(1)}, bf16[256,128]{1,0:T(8,128)(2,1)}, u32[]{:S(2)}) copy-start(bf16[256,128]{1,0:T(8,128)(2,1)} %param.7) | copy-start | bytes 196612
  42.7 9.8 %collective-permute-start.1 = (bf16[512,256]{1,0:T(8,128)(2,1)S(1)}, bf16[512,256]{1,0:T(8,128)(2,1)S(1)}, u32[]{:S(2)}, u32[]{:S(2)}) collective-permute-start(bf16[512,256]{1,0:T(8,128)(2,1)S(1)} %pad_maximum_fusion.6), channel_id=1, source_target_pairs={{0,504},{4,508},{8,0},{12,4},{16,8},{20,12},{24,16},{28,20},{32,24... | collective-permute-start | bytes 786440 | tf_op jit(solution)/shard_map/ppermute | solution.py:94
  52.6 28.9 %collective-permute-start.2 = (bf16[1024,256]{1,0:T(8,128)(2,1)S(1)}, bf16[1024,256]{1,0:T(8,128)(2,1)S(1)}, u32[]{:S(2)}, u32[]{:S(2)}) collective-permute-start(bf16[1024,256]{1,0:T(8,128)(2,1)S(1)} %pad_maximum_fusion.1), channel_id=1, source_target_pairs={{0,16},{4,20},{8,24},{12,28},{16,32},{20,36},{24,40},{28,44},{32,4... | collective-permute-start | bytes 1572872 | tf_op jit(solution)/shard_map/ppermute | solution.py:94
  81.6 21.4 %copy-start.8 = (bf16[256,128]{1,0:T(8,128)(2,1)S(1)}, bf16[256,128]{1,0:T(8,128)(2,1)}, u32[]{:S(2)}) copy-start(bf16[256,128]{1,0:T(8,128)(2,1)} %param.8) | copy-start | bytes 196612
  81.7 13.9 %collective-permute-start.3 = (bf16[512,256]{1,0:T(8,128)(2,1)S(1)}, bf16[512,256]{1,0:T(8,128)(2,1)S(1)}, u32[]{:S(2)}, u32[]{:S(2)}) collective-permute-start(bf16[512,256]{1,0:T(8,128)(2,1)S(1)} %get-tuple-element.54), channel_id=1, source_target_pairs={{0,480},{4,484},{8,488},{12,492},{16,496},{20,500},{24,504},{28,50... | collective-permute-start | bytes 786440 | tf_op jit(solution)/shard_map/ppermute | solution.py:94
  83.8 15.9 %collective-permute-start.6 = (bf16[512,256]{1,0:T(8,128)(2,1)S(1)}, bf16[512,256]{1,0:T(8,128)(2,1)S(1)}, u32[]{:S(2)}, u32[]{:S(2)}) collective-permute-start(bf16[512,256]{1,0:T(8,128)(2,1)S(1)} %get-tuple-element.53), channel_id=1, source_target_pairs={{0,128},{4,132},{8,136},{12,140},{16,144},{20,148},{24,152},{28,15... | collective-permute-start | bytes 786440 | tf_op jit(solution)/shard_map/ppermute | solution.py:94
  99.7 14.7 %collective-permute-start.7 = (bf16[512,256]{1,0:T(8,128)(2,1)S(1)}, bf16[512,256]{1,0:T(8,128)(2,1)S(1)}, u32[]{:S(2)}, u32[]{:S(2)}) collective-permute-start(bf16[512,256]{1,0:T(8,128)(2,1)S(1)} %pad_maximum_fusion.3), channel_id=1, source_target_pairs={{0,256},{4,260},{8,264},{12,268},{16,272},{20,276},{24,280},{28,28... | collective-permute-start | bytes 786440 | tf_op jit(solution)/shard_map/ppermute | solution.py:94
  114.5 2.9 %copy-start.6 = (bf16[4096,256]{1,0:T(8,128)(2,1)}, bf16[4096,256]{1,0:T(8,128)(2,1)S(1)}, u32[]{:S(2)}) copy-start(bf16[4096,256]{1,0:T(8,128)(2,1)S(1)} %slice_dynamic-update-slice_fusion) | copy-start | bytes 6291460
  118.6 1.6 copy-start.7
  123.0 67.9 %copy-start.1 = (f32[4096,128]{0,1:T(8,128)}, f32[4096,128]{0,1:T(8,128)S(1)}, u32[]{:S(2)}) copy-start(f32[4096,128]{0,1:T(8,128)S(1)} %convolution_multiply_fusion.1) | copy-start | bytes 6291460
  123.5 14.2 %collective-permute-start.9 = (bf16[512,256]{0,1:T(8,128)(2,1)S(1)}, bf16[512,256]{0,1:T(8,128)(2,1)S(1)}, u32[]{:S(2)}, u32[]{:S(2)}) collective-permute-start(bf16[512,256]{0,1:T(8,128)(2,1)S(1)} %pad_maximum_fusion.8), channel_id=1, source_target_pairs={{0,256},{4,260},{8,264},{12,268},{16,272},{20,276},{24,280},{28,28... | collective-permute-start | bytes 786440 | tf_op jit(solution)/shard_map/ppermute | solution.py:94
  125.5 21.2 %collective-permute-start.8 = (bf16[512,256]{0,1:T(8,128)(2,1)S(1)}, bf16[512,256]{0,1:T(8,128)(2,1)S(1)}, u32[]{:S(2)}, u32[]{:S(2)}) collective-permute-start(bf16[512,256]{0,1:T(8,128)(2,1)S(1)} %pad_maximum_fusion.7), channel_id=1, source_target_pairs={{0,32},{4,36},{8,40},{12,44},{16,48},{20,52},{24,56},{28,60},{32,6... | collective-permute-start | bytes 786440 | tf_op jit(solution)/shard_map/ppermute | solution.py:94
  138.5 11.7 %collective-permute-start.11 = (bf16[512,256]{0,1:T(8,128)(2,1)S(1)}, bf16[512,256]{0,1:T(8,128)(2,1)S(1)}, u32[]{:S(2)}, u32[]{:S(2)}) collective-permute-start(bf16[512,256]{0,1:T(8,128)(2,1)S(1)} %pad_maximum_fusion.9), channel_id=1, source_target_pairs={{0,384},{4,388},{8,392},{12,396},{16,400},{20,404},{24,408},{28,41... | collective-permute-start | bytes 786440 | tf_op jit(solution)/shard_map/ppermute | solution.py:94
  146.8 3.6 %copy-start.3 = (f32[512,256]{0,1:T(8,128)}, f32[512,256]{0,1:T(8,128)S(1)}, u32[]{:S(2)}) copy-start(f32[512,256]{0,1:T(8,128)S(1)} %convert_element_type.67) | copy-start | bytes 1572868
  151.1 12.6 %collective-permute-start.10 = (bf16[1024,256]{0,1:T(8,128)(2,1)S(1)}, bf16[1024,256]{0,1:T(8,128)(2,1)S(1)}, u32[]{:S(2)}, u32[]{:S(2)}) collective-permute-start(bf16[1024,256]{0,1:T(8,128)(2,1)S(1)} %pad_maximum_fusion.2), channel_id=1, source_target_pairs={{0,496},{4,500},{8,504},{12,508},{16,0},{20,4},{24,8},{28,12},{32,... | collective-permute-start | bytes 1572872 | tf_op jit(solution)/shard_map/ppermute | solution.py:94
  164.0 26.7 %collective-permute-start.12 = (bf16[512,256]{0,1:T(8,128)(2,1)S(1)}, bf16[512,256]{0,1:T(8,128)(2,1)S(1)}, u32[]{:S(2)}, u32[]{:S(2)}) collective-permute-start(bf16[512,256]{0,1:T(8,128)(2,1)S(1)} %pad_maximum_fusion.10), channel_id=1, source_target_pairs={{0,8},{4,12},{8,16},{12,20},{16,24},{20,28},{24,32},{28,36},{32,40... | collective-permute-start | bytes 786440 | tf_op jit(solution)/shard_map/ppermute | solution.py:94
  183.4 17.2 %collective-permute-start.14 = (bf16[256,256]{0,1:T(8,128)(2,1)S(1)}, bf16[256,256]{0,1:T(8,128)(2,1)}, u32[]{:S(2)}, u32[]{:S(2)}) collective-permute-start(bf16[256,256]{0,1:T(8,128)(2,1)S(1)} %get-tuple-element.38), channel_id=1, source_target_pairs={{0,480},{4,484},{8,488},{12,492},{16,496},{20,500},{24,504},{28,50... | collective-permute-start | bytes 393224 | tf_op jit(solution)/shard_map/ppermute | solution.py:94
  186.4 14.2 %collective-permute-start.13 = (bf16[256,256]{0,1:T(8,128)(2,1)S(1)}, bf16[256,256]{0,1:T(8,128)(2,1)}, u32[]{:S(2)}, u32[]{:S(2)}) collective-permute-start(bf16[256,256]{0,1:T(8,128)(2,1)S(1)} %get-tuple-element.36), channel_id=1, source_target_pairs={{0,64},{4,68},{8,72},{12,76},{16,80},{20,84},{24,88},{28,92},{32,9... | collective-permute-start | bytes 393224 | tf_op jit(solution)/shard_map/ppermute | solution.py:94
  191.7 8.9 %collective-permute-start.15 = (bf16[256,256]{0,1:T(8,128)(2,1)}, bf16[256,256]{0,1:T(8,128)(2,1)}, u32[]{:S(2)}, u32[]{:S(2)}) collective-permute-start(bf16[256,256]{0,1:T(8,128)(2,1)} %fusion.25), channel_id=1, source_target_pairs={{0,4},{4,8},{8,12},{12,16},{16,20},{20,24},{24,28},{28,32},{32,36}... | collective-permute-start | bytes 393224 | tf_op jit(solution)/shard_map/ppermute | solution.py:94
  (4 other events, 3.4 us)

commit v6 on v3

--- a/solution.py
+++ b/solution.py
@@ -85,9 +85,8 @@
     joined = jnp.concatenate([key_tokens, value_tokens], axis=1)
     near_keys = extended(joined, (("seq", 0),), tok_rows)
     neighbour = device + jnp.arange(3, dtype=jnp.int32) - 1
-    near_ok = jnp.repeat((neighbour >= 0) & (neighbour < frame_count), tok_rows)
+    near_ok = (neighbour >= 0) & (neighbour < frame_count)
     pieces = [near_keys]
-    mask_list = [jnp.broadcast_to(near_ok[None, :], (tok_rows, 3 * tok_rows))]
     half = frame_count // 2
     offsets = [o for o in offsets if o != -half]
     for offset in offsets:
@@ -95,18 +94,27 @@
             arrived = lax.ppermute(
                 joined, "seq", [(src, (src + half) % frame_count) for src in range(frame_count)]
             )
-            other_frame = (device + half) % frame_count
         else:
             arrived = from_behind(joined, "seq", -offset)
-            other_frame = device + offset
-        is_valid = (other_frame >= 0) & (other_frame < frame_count)
-        safe_frame = jnp.clip(other_frame, 0, frame_count - 1)
-        entries = far_block[device, safe_frame]
-        pair_start, far_hit = far_window(entries, is_valid)
         pieces.append(arrived)
-        mask_list.append(far_hit)
+    shifts = jnp.asarray(offsets, jnp.int32)
+    other_frame = jnp.where(shifts == half, (device + half) % frame_count, device + shifts)
+    is_valid = (other_frame >= 0) & (other_frame < frame_count)
+    frame_rows = lax.dynamic_index_in_dim(far_block, device, 0, keepdims=False)
+    entries = jnp.take(frame_rows, jnp.clip(other_frame, 0, frame_count - 1), axis=0)
+    seen = is_valid[:, None] & (entries >= 0)
+    blocks = tok_rows // BLK
+    row_block = jnp.arange(tok_rows, dtype=jnp.int32) // BLK
+    near_mask = jnp.broadcast_to(
+        near_ok[None, :, None], (tok_rows, 3, tok_rows)
+    ).reshape(tok_rows, 3 * tok_rows)
+    seen_rows = jnp.take(seen, row_block, axis=1)
+    diag = row_block[:, None] == row_block[None, :]
+    far_mask = (diag[:, None, :] & seen_rows.T[:, :, None]).reshape(
+        tok_rows, len(offsets) * tok_rows
+    )
     keys_all = jnp.concatenate(pieces, axis=0)
-    visible = jnp.concatenate(mask_list, axis=1)
+    visible = jnp.concatenate([near_mask, far_mask], axis=1)
     attention_out, query_grad, weights, dscores, log_total, row_delta = attend_parts(
         query_tokens, grad_out, keys_all, visible
     )

time: 195 us -> 180 us (0.923)
  the two profiles are of different devices: /device:TPU:36 before, /device:TPU:34 now
where the time goes in v6:
time: 180 us; the launch traced here: 179 us
  starting transfers between devices  114 us (63%)
  waiting for transfers between devices  43.7 us (24%)
  local copies, waits for them, and re-layouts  8.93 us (5%)
  matrix products  8 us (4%)
  other arithmetic  3.01 us (2%)
    ppermute x26, starting transfers between devices, from_behind(): lax.ppermute(value, axis, [(source, source + steps) for source in range(l...  105 us
    ppermute x26, waiting for transfers between devices, from_behind(): lax.ppermute(value, axis, [(source, source + steps) for source in range(l...  38.7 us
    unnamed x29, local copies, waits for them, and re-layouts  5.43 us
  transfers between devices with their start and end apart: 30, of which 9 were waited for; matrix products, arithmetic and copies ran while one was open for 4% of the time, Pallas kernels for 0%

profile of v6, /device:TPU:34, one launch (start us, length us, event | category | flops | bytes accessed | tf_op | source)
XLA Modules:
  0.0 179.0 jit_solution(15902811361088285508)
XLA Ops:
  2.4 2.0 %collective-permute-start.14 = (bf16[256,256]{1,0:T(8,128)(2,1)S(1)}, bf16[256,256]{1,0:T(8,128)(2,1)S(1)}, u32[]{:S(2)}, u32[]{:S(2)}) collective-permute-start(bf16[256,256]{1,0:T(8,128)(2,1)S(1)} %constant_dynamic-update-slice_fusion), channel_id=1, source_target_pairs={{0,256},{4,260},{8,264},{12,268},{16,272},{20,276},{24,280},{28,28... | collective-permute-start | bytes 393224 | tf_op jit(solution)/shard_map/ppermute | solution.py:94
  4.4 4.5 %collective-permute-start.13 = (bf16[256,256]{1,0:T(8,128)(2,1)S(1)}, bf16[256,256]{1,0:T(8,128)(2,1)S(1)}, u32[]{:S(2)}, u32[]{:S(2)}) collective-permute-start(bf16[256,256]{1,0:T(8,128)(2,1)S(1)} %constant_dynamic-update-slice_fusion), channel_id=1, source_target_pairs={{0,128},{4,132},{8,136},{12,140},{16,144},{20,148},{24,152},{28,15... | collective-permute-start | bytes 393224 | tf_op jit(solution)/shard_map/ppermute | solution.py:26
  8.9 3.6 %collective-permute-start.12 = (bf16[256,256]{1,0:T(8,128)(2,1)S(1)}, bf16[256,256]{1,0:T(8,128)(2,1)S(1)}, u32[]{:S(2)}, u32[]{:S(2)}) collective-permute-start(bf16[256,256]{1,0:T(8,128)(2,1)S(1)} %constant_dynamic-update-slice_fusion), channel_id=1, source_target_pairs={{128,0},{132,4},{136,8},{140,12},{144,16},{148,20},{152,24},{156,2... | collective-permute-start | bytes 393224 | tf_op jit(solution)/shard_map/ppermute | solution.py:26
  12.5 12.5 %collective-permute-start.2 = (bf16[256,256]{1,0:T(8,128)(2,1)S(1)}, bf16[256,256]{1,0:T(8,128)(2,1)S(1)}, u32[]{:S(2)}, u32[]{:S(2)}) collective-permute-start(bf16[256,256]{1,0:T(8,128)(2,1)S(1)} %constant_dynamic-update-slice_fusion), channel_id=1, source_target_pairs={{8,0},{12,4},{16,8},{20,12},{24,16},{28,20},{32,24},{36,28},{40,32... | collective-permute-start | bytes 393224 | tf_op jit(solution)/shard_map/ppermute | solution.py:26
  25.1 1.9 %collective-permute-start = (bf16[256,256]{1,0:T(8,128)(2,1)S(1)}, bf16[256,256]{1,0:T(8,128)(2,1)S(1)}, u32[]{:S(2)}, u32[]{:S(2)}) collective-permute-start(bf16[256,256]{1,0:T(8,128)(2,1)S(1)} %constant_dynamic-update-slice_fusion), channel_id=1, source_target_pairs={{0,4},{4,8},{8,12},{12,16},{16,20},{20,24},{24,28},{28,32},{32,36}... | collective-permute-start | bytes 393224 | tf_op jit(solution)/shard_map/ppermute | solution.py:17
  31.2 3.4 %collective-permute-done = bf16[256,256]{1,0:T(8,128)(2,1)S(1)} collective-permute-done((bf16[256,256]{1,0:T(8,128)(2,1)S(1)}, bf16[256,256]{1,0:T(8,128)(2,1)S(1)}, u32[]{:S(2)}, u32[]{:S(2)}) %collective-permute-start) | collective-permute-done | bytes 131104 | tf_op jit(solution)/shard_map/ppermute | solution.py:17
  34.7 3.5 %collective-permute-start.1 = (bf16[256,256]{1,0:T(8,128)(2,1)S(1)}, bf16[256,256]{1,0:T(8,128)(2,1)S(1)}, u32[]{:S(2)}, u32[]{:S(2)}) collective-permute-start(bf16[256,256]{1,0:T(8,128)(2,1)S(1)} %constant_dynamic-update-slice_fusion), channel_id=1, source_target_pairs={{4,0},{8,4},{12,8},{16,12},{20,16},{24,20},{28,24},{32,28},{36,32}... | collective-permute-start | bytes 393224 | tf_op jit(solution)/shard_map/ppermute | solution.py:18
  42.6 8.3 %collective-permute-start.4 = (bf16[256,256]{1,0:T(8,128)(2,1)S(1)}, bf16[256,256]{1,0:T(8,128)(2,1)S(1)}, u32[]{:S(2)}, u32[]{:S(2)}) collective-permute-start(bf16[256,256]{1,0:T(8,128)(2,1)S(1)} %constant_dynamic-update-slice_fusion), channel_id=1, source_target_pairs={{12,0},{16,4},{20,8},{24,12},{28,16},{32,20},{36,24},{40,28},{44,3... | collective-permute-start | bytes 393224 | tf_op jit(solution)/shard_map/ppermute | solution.py:26
  53.8 3.1 %collective-permute-start.6 = (bf16[256,256]{1,0:T(8,128)(2,1)S(1)}, bf16[256,256]{1,0:T(8,128)(2,1)S(1)}, u32[]{:S(2)}, u32[]{:S(2)}) collective-permute-start(bf16[256,256]{1,0:T(8,128)(2,1)S(1)} %constant_dynamic-update-slice_fusion), channel_id=1, source_target_pairs={{16,0},{20,4},{24,8},{28,12},{32,16},{36,20},{40,24},{44,28},{48,3... | collective-permute-start | bytes 393224 | tf_op jit(solution)/shard_map/ppermute | solution.py:26
  56.9 6.2 %collective-permute-done.5 = bf16[256,256]{1,0:T(8,128)(2,1)S(1)} collective-permute-done((bf16[256,256]{1,0:T(8,128)(2,1)S(1)}, bf16[256,256]{1,0:T(8,128)(2,1)S(1)}, u32[]{:S(2)}, u32[]{:S(2)}) %collective-permute-start.5) | collective-permute-done | bytes 131104 | tf_op jit(solution)/shard_map/ppermute | solution.py:26
  67.0 10.7 %collective-permute-done.7 = bf16[256,256]{1,0:T(8,128)(2,1)S(1)} collective-permute-done((bf16[256,256]{1,0:T(8,128)(2,1)S(1)}, bf16[256,256]{1,0:T(8,128)(2,1)S(1)}, u32[]{:S(2)}, u32[]{:S(2)}) %collective-permute-start.7) | collective-permute-done | bytes 131104 | tf_op jit(solution)/shard_map/ppermute | solution.py:26
  81.7 9.6 %collective-permute-done.9 = bf16[256,256]{1,0:T(8,128)(2,1)S(1)} collective-permute-done((bf16[256,256]{1,0:T(8,128)(2,1)S(1)}, bf16[256,256]{1,0:T(8,128)(2,1)S(1)}, u32[]{:S(2)}, u32[]{:S(2)}) %collective-permute-start.9) | collective-permute-done | bytes 131104 | tf_op jit(solution)/shard_map/ppermute | solution.py:26
  93.3 6.1 %collective-permute-done.11 = bf16[256,256]{1,0:T(8,128)(2,1)S(1)} collective-permute-done((bf16[256,256]{1,0:T(8,128)(2,1)S(1)}, bf16[256,256]{1,0:T(8,128)(2,1)S(1)}, u32[]{:S(2)}, u32[]{:S(2)}) %collective-permute-start.11) | collective-permute-done | bytes 131104 | tf_op jit(solution)/shard_map/ppermute | solution.py:26
  99.5 3.3 %fusion.36 = (f32[256]{0:T(256)S(1)}, f32[256,4096]{0,1:T(8,128)S(1)}) fusion(bf16[256,128]{1,0:T(8,128)(2,1)S(1)} %copy-done.3, bf16[4096,256]{1,0:T(8,128)(2,1)S(1)} %constant_dynamic-update-slice_fusion.2, pred[256,3328]{0,1:T(32,128)(4,1)S(1)} %bitcast.21, pred[4096]{0:T(1024)(128)(4,1)S(1)} %pad.4.clone), kind=kOutput, calls=%fused_computation.93 | convolution fusion | flops 272629504 | bytes 6165504 | tf_op jit(solution)/shard_map/dot_general | solution.py:54
  114.0 4.8 %collective-permute-start.27 = (bf16[256,256]{0,1:T(8,128)(2,1)S(1)}, bf16[256,256]{0,1:T(8,128)(2,1)S(1)}, u32[]{:S(2)}, u32[]{:S(2)}) collective-permute-start(bf16[256,256]{0,1:T(8,128)(2,1)S(1)} %get-tuple-element.21), channel_id=1, source_target_pairs={{0,128},{4,132},{8,136},{12,140},{16,144},{20,148},{24,152},{28,15... | collective-permute-start | bytes 393224 | tf_op jit(solution)/shard_map/ppermute | solution.py:26
  118.8 2.8 %collective-permute-start.26 = (bf16[256,256]{0,1:T(8,128)(2,1)S(1)}, bf16[256,256]{0,1:T(8,128)(2,1)S(1)}, u32[]{:S(2)}, u32[]{:S(2)}) collective-permute-start(bf16[256,256]{0,1:T(8,128)(2,1)S(1)} %get-tuple-element.22), channel_id=1, source_target_pairs={{64,0},{68,4},{72,8},{76,12},{80,16},{84,20},{88,24},{92,28},{96,3... | collective-permute-start | bytes 393224 | tf_op jit(solution)/shard_map/ppermute | solution.py:26
  122.0 3.0 %collective-permute-start.25 = (bf16[256,256]{0,1:T(8,128)(2,1)S(1)}, bf16[256,256]{0,1:T(8,128)(2,1)S(1)}, u32[]{:S(2)}, u32[]{:S(2)}) collective-permute-start(bf16[256,256]{0,1:T(8,128)(2,1)S(1)} %get-tuple-element.23), channel_id=1, source_target_pairs={{0,64},{4,68},{8,72},{12,76},{16,80},{20,84},{24,88},{28,92},{32,9... | collective-permute-start | bytes 393224 | tf_op jit(solution)/shard_map/ppermute | solution.py:26
  125.1 3.6 %collective-permute-start.24 = (bf16[256,256]{0,1:T(8,128)(2,1)S(1)}, bf16[256,256]{0,1:T(8,128)(2,1)S(1)}, u32[]{:S(2)}, u32[]{:S(2)}) collective-permute-start(bf16[256,256]{0,1:T(8,128)(2,1)S(1)} %get-tuple-element.24), channel_id=1, source_target_pairs={{32,0},{36,4},{40,8},{44,12},{48,16},{52,20},{56,24},{60,28},{64,3... | collective-permute-start | bytes 393224 | tf_op jit(solution)/shard_map/ppermute | solution.py:26
  128.7 6.2 %collective-permute-start.23 = (bf16[256,256]{0,1:T(8,128)(2,1)S(1)}, bf16[256,256]{0,1:T(8,128)(2,1)S(1)}, u32[]{:S(2)}, u32[]{:S(2)}) collective-permute-start(bf16[256,256]{0,1:T(8,128)(2,1)S(1)} %get-tuple-element.25), channel_id=1, source_target_pairs={{0,32},{4,36},{8,40},{12,44},{16,48},{20,52},{24,56},{28,60},{32,6... | collective-permute-start | bytes 393224 | tf_op jit(solution)/shard_map/ppermute | solution.py:26
  134.9 6.9 %collective-permute-start.22 = (bf16[256,256]{0,1:T(8,128)(2,1)S(1)}, bf16[256,256]{0,1:T(8,128)(2,1)S(1)}, u32[]{:S(2)}, u32[]{:S(2)}) collective-permute-start(bf16[256,256]{0,1:T(8,128)(2,1)S(1)} %get-tuple-element.26), channel_id=1, source_target_pairs={{16,0},{20,4},{24,8},{28,12},{32,16},{36,20},{40,24},{44,28},{48,3... | collective-permute-start | bytes 393224 | tf_op jit(solution)/shard_map/ppermute | solution.py:26
  143.7 4.4 %collective-permute-start.20 = (bf16[256,256]{0,1:T(8,128)(2,1)}, bf16[256,256]{0,1:T(8,128)(2,1)S(1)}, u32[]{:S(2)}, u32[]{:S(2)}) collective-permute-start(bf16[256,256]{0,1:T(8,128)(2,1)} %get-tuple-element.28), channel_id=1, source_target_pairs={{12,0},{16,4},{20,8},{24,12},{28,16},{32,20},{36,24},{40,28},{44,3... | collective-permute-start | bytes 393224 | tf_op jit(solution)/shard_map/ppermute | solution.py:26
  150.1 15.6 %collective-permute-start.18 = (bf16[256,256]{0,1:T(8,128)(2,1)S(1)}, bf16[256,256]{0,1:T(8,128)(2,1)S(1)}, u32[]{:S(2)}, u32[]{:S(2)}) collective-permute-start(bf16[256,256]{0,1:T(8,128)(2,1)S(1)} %get-tuple-element.30), channel_id=1, source_target_pairs={{8,0},{12,4},{16,8},{20,12},{24,16},{28,20},{32,24},{36,28},{40,32... | collective-permute-start | bytes 393224 | tf_op jit(solution)/shard_map/ppermute | solution.py:26
  167.6 2.4 %collective-permute-start.16 = (bf16[256,256]{0,1:T(8,128)(2,1)S(1)}, bf16[256,256]{0,1:T(8,128)(2,1)S(1)}, u32[]{:S(2)}, u32[]{:S(2)}) collective-permute-start(bf16[256,256]{0,1:T(8,128)(2,1)S(1)} %get-tuple-element.32), channel_id=1, source_target_pairs={{0,4},{4,8},{8,12},{12,16},{16,20},{20,24},{24,28},{28,32},{32,36}... | collective-permute-start | bytes 393224 | tf_op jit(solution)/shard_map/ppermute | solution.py:26
  172.3 5.0 %collective-permute-done.16 = bf16[256,256]{0,1:T(8,128)(2,1)S(1)} collective-permute-done((bf16[256,256]{0,1:T(8,128)(2,1)S(1)}, bf16[256,256]{0,1:T(8,128)(2,1)S(1)}, u32[]{:S(2)}, u32[]{:S(2)}) %collective-permute-start.16) | collective-permute-done | bytes 131104 | tf_op jit(solution)/shard_map/ppermute | solution.py:26
  (103 shorter events, 44.3 us)
Async XLA Ops:
  2.4 97.1 %collective-permute-start.14 = (bf16[256,256]{1,0:T(8,128)(2,1)S(1)}, bf16[256,256]{1,0:T(8,128)(2,1)S(1)}, u32[]{:S(2)}, u32[]{:S(2)}) collective-permute-start(bf16[256,256]{1,0:T(8,128)(2,1)S(1)} %constant_dynamic-update-slice_fusion), channel_id=1, source_target_pairs={{0,256},{4,260},{8,264},{12,268},{16,272},{20,276},{24,280},{28,28... | collective-permute-start | bytes 393224 | tf_op jit(solution)/shard_map/ppermute | solution.py:94
  4.4 95.0 %collective-permute-start.13 = (bf16[256,256]{1,0:T(8,128)(2,1)S(1)}, bf16[256,256]{1,0:T(8,128)(2,1)S(1)}, u32[]{:S(2)}, u32[]{:S(2)}) collective-permute-start(bf16[256,256]{1,0:T(8,128)(2,1)S(1)} %constant_dynamic-update-slice_fusion), channel_id=1, source_target_pairs={{0,128},{4,132},{8,136},{12,140},{16,144},{20,148},{24,152},{28,15... | collective-permute-start | bytes 393224 | tf_op jit(solution)/shard_map/ppermute | solution.py:26
  8.9 90.5 %collective-permute-start.12 = (bf16[256,256]{1,0:T(8,128)(2,1)S(1)}, bf16[256,256]{1,0:T(8,128)(2,1)S(1)}, u32[]{:S(2)}, u32[]{:S(2)}) collective-permute-start(bf16[256,256]{1,0:T(8,128)(2,1)S(1)} %constant_dynamic-update-slice_fusion), channel_id=1, source_target_pairs={{128,0},{132,4},{136,8},{140,12},{144,16},{148,20},{152,24},{156,2... | collective-permute-start | bytes 393224 | tf_op jit(solution)/shard_map/ppermute | solution.py:26
  12.5 30.1 %collective-permute-start.2 = (bf16[256,256]{1,0:T(8,128)(2,1)S(1)}, bf16[256,256]{1,0:T(8,128)(2,1)S(1)}, u32[]{:S(2)}, u32[]{:S(2)}) collective-permute-start(bf16[256,256]{1,0:T(8,128)(2,1)S(1)} %constant_dynamic-update-slice_fusion), channel_id=1, source_target_pairs={{8,0},{12,4},{16,8},{20,12},{24,16},{28,20},{32,24},{36,28},{40,32... | collective-permute-start | bytes 393224 | tf_op jit(solution)/shard_map/ppermute | solution.py:26
  40.7 11.1 %collective-permute-start.3 = (bf16[256,256]{1,0:T(8,128)(2,1)S(1)}, bf16[256,256]{1,0:T(8,128)(2,1)S(1)}, u32[]{:S(2)}, u32[]{:S(2)}) collective-permute-start(bf16[256,256]{1,0:T(8,128)(2,1)S(1)} %constant_dynamic-update-slice_fusion), channel_id=1, source_target_pairs={{0,8},{4,12},{8,16},{12,20},{16,24},{20,28},{24,32},{28,36},{32,40... | collective-permute-start | bytes 393224 | tf_op jit(solution)/shard_map/ppermute | solution.py:26
  51.8 11.3 %collective-permute-start.5 = (bf16[256,256]{1,0:T(8,128)(2,1)S(1)}, bf16[256,256]{1,0:T(8,128)(2,1)S(1)}, u32[]{:S(2)}, u32[]{:S(2)}) collective-permute-start(bf16[256,256]{1,0:T(8,128)(2,1)S(1)} %constant_dynamic-update-slice_fusion), channel_id=1, source_target_pairs={{0,12},{4,16},{8,20},{12,24},{16,28},{20,32},{24,36},{28,40},{32,4... | collective-permute-start | bytes 393224 | tf_op jit(solution)/shard_map/ppermute | solution.py:26
  53.8 11.3 %collective-permute-start.6 = (bf16[256,256]{1,0:T(8,128)(2,1)S(1)}, bf16[256,256]{1,0:T(8,128)(2,1)S(1)}, u32[]{:S(2)}, u32[]{:S(2)}) collective-permute-start(bf16[256,256]{1,0:T(8,128)(2,1)S(1)} %constant_dynamic-update-slice_fusion), channel_id=1, source_target_pairs={{16,0},{20,4},{24,8},{28,12},{32,16},{36,20},{40,24},{44,28},{48,3... | collective-permute-start | bytes 393224 | tf_op jit(solution)/shard_map/ppermute | solution.py:26
  63.1 14.6 %collective-permute-start.7 = (bf16[256,256]{1,0:T(8,128)(2,1)S(1)}, bf16[256,256]{1,0:T(8,128)(2,1)S(1)}, u32[]{:S(2)}, u32[]{:S(2)}) collective-permute-start(bf16[256,256]{1,0:T(8,128)(2,1)S(1)} %constant_dynamic-update-slice_fusion), channel_id=1, source_target_pairs={{0,16},{4,20},{8,24},{12,28},{16,32},{20,36},{24,40},{28,44},{32,4... | collective-permute-start | bytes 393224 | tf_op jit(solution)/shard_map/ppermute | solution.py:26
  65.0 14.8 %collective-permute-start.8 = (bf16[256,256]{1,0:T(8,128)(2,1)S(1)}, bf16[256,256]{1,0:T(8,128)(2,1)S(1)}, u32[]{:S(2)}, u32[]{:S(2)}) collective-permute-start(bf16[256,256]{1,0:T(8,128)(2,1)S(1)} %constant_dynamic-update-slice_fusion), channel_id=1, source_target_pairs={{32,0},{36,4},{40,8},{44,12},{48,16},{52,20},{56,24},{60,28},{64,3... | collective-permute-start | bytes 393224 | tf_op jit(solution)/shard_map/ppermute | solution.py:26
  77.7 13.7 %collective-permute-start.9 = (bf16[256,256]{1,0:T(8,128)(2,1)S(1)}, bf16[256,256]{1,0:T(8,128)(2,1)S(1)}, u32[]{:S(2)}, u32[]{:S(2)}) collective-permute-start(bf16[256,256]{1,0:T(8,128)(2,1)S(1)} %constant_dynamic-update-slice_fusion), channel_id=1, source_target_pairs={{0,32},{4,36},{8,40},{12,44},{16,48},{20,52},{24,56},{28,60},{32,6... | collective-permute-start | bytes 393224 | tf_op jit(solution)/shard_map/ppermute | solution.py:26
  79.8 13.5 %collective-permute-start.10 = (bf16[256,256]{1,0:T(8,128)(2,1)S(1)}, bf16[256,256]{1,0:T(8,128)(2,1)S(1)}, u32[]{:S(2)}, u32[]{:S(2)}) collective-permute-start(bf16[256,256]{1,0:T(8,128)(2,1)S(1)} %constant_dynamic-update-slice_fusion), channel_id=1, source_target_pairs={{64,0},{68,4},{72,8},{76,12},{80,16},{84,20},{88,24},{92,28},{96,3... | collective-permute-start | bytes 393224 | tf_op jit(solution)/shard_map/ppermute | solution.py:26
  108.2 13.8 %collective-permute-start.17 = (bf16[256,256]{0,1:T(8,128)(2,1)S(1)}, bf16[256,256]{0,1:T(8,128)(2,1)S(1)}, u32[]{:S(2)}, u32[]{:S(2)}) collective-permute-start(bf16[256,256]{0,1:T(8,128)(2,1)S(1)} %get-tuple-element.18), channel_id=1, source_target_pairs={{0,8},{4,12},{8,16},{12,20},{16,24},{20,28},{24,32},{28,36},{32,40... | collective-permute-start | bytes 393224 | tf_op jit(solution)/shard_map/ppermute | solution.py:26
  110.2 14.9 %collective-permute-start.29 = (bf16[256,256]{0,1:T(8,128)(2,1)S(1)}, bf16[256,256]{0,1:T(8,128)(2,1)S(1)}, u32[]{:S(2)}, u32[]{:S(2)}) collective-permute-start(bf16[256,256]{0,1:T(8,128)(2,1)S(1)} %get-tuple-element.19), channel_id=1, source_target_pairs={{0,256},{4,260},{8,264},{12,268},{16,272},{20,276},{24,280},{28,28... | collective-permute-start | bytes 393224 | tf_op jit(solution)/shard_map/ppermute | solution.py:135
  112.1 16.6 %collective-permute-start.28 = (bf16[256,256]{0,1:T(8,128)(2,1)S(1)}, bf16[256,256]{0,1:T(8,128)(2,1)S(1)}, u32[]{:S(2)}, u32[]{:S(2)}) collective-permute-start(bf16[256,256]{0,1:T(8,128)(2,1)S(1)} %get-tuple-element.20), channel_id=1, source_target_pairs={{128,0},{132,4},{136,8},{140,12},{144,16},{148,20},{152,24},{156,2... | collective-permute-start | bytes 393224 | tf_op jit(solution)/shard_map/ppermute | solution.py:26
  114.0 20.8 %collective-permute-start.27 = (bf16[256,256]{0,1:T(8,128)(2,1)S(1)}, bf16[256,256]{0,1:T(8,128)(2,1)S(1)}, u32[]{:S(2)}, u32[]{:S(2)}) collective-permute-start(bf16[256,256]{0,1:T(8,128)(2,1)S(1)} %get-tuple-element.21), channel_id=1, source_target_pairs={{0,128},{4,132},{8,136},{12,140},{16,144},{20,148},{24,152},{28,15... | collective-permute-start | bytes 393224 | tf_op jit(solution)/shard_map/ppermute | solution.py:26
  118.8 22.9 %collective-permute-start.26 = (bf16[256,256]{0,1:T(8,128)(2,1)S(1)}, bf16[256,256]{0,1:T(8,128)(2,1)S(1)}, u32[]{:S(2)}, u32[]{:S(2)}) collective-permute-start(bf16[256,256]{0,1:T(8,128)(2,1)S(1)} %get-tuple-element.22), channel_id=1, source_target_pairs={{64,0},{68,4},{72,8},{76,12},{80,16},{84,20},{88,24},{92,28},{96,3... | collective-permute-start | bytes 393224 | tf_op jit(solution)/shard_map/ppermute | solution.py:26
  122.0 21.7 %collective-permute-start.25 = (bf16[256,256]{0,1:T(8,128)(2,1)S(1)}, bf16[256,256]{0,1:T(8,128)(2,1)S(1)}, u32[]{:S(2)}, u32[]{:S(2)}) collective-permute-start(bf16[256,256]{0,1:T(8,128)(2,1)S(1)} %get-tuple-element.23), channel_id=1, source_target_pairs={{0,64},{4,68},{8,72},{12,76},{16,80},{20,84},{24,88},{28,92},{32,9... | collective-permute-start | bytes 393224 | tf_op jit(solution)/shard_map/ppermute | solution.py:26
  125.1 23.0 %collective-permute-start.24 = (bf16[256,256]{0,1:T(8,128)(2,1)S(1)}, bf16[256,256]{0,1:T(8,128)(2,1)S(1)}, u32[]{:S(2)}, u32[]{:S(2)}) collective-permute-start(bf16[256,256]{0,1:T(8,128)(2,1)S(1)} %get-tuple-element.24), channel_id=1, source_target_pairs={{32,0},{36,4},{40,8},{44,12},{48,16},{52,20},{56,24},{60,28},{64,3... | collective-permute-start | bytes 393224 | tf_op jit(solution)/shard_map/ppermute | solution.py:26
  128.7 21.4 %collective-permute-start.23 = (bf16[256,256]{0,1:T(8,128)(2,1)S(1)}, bf16[256,256]{0,1:T(8,128)(2,1)S(1)}, u32[]{:S(2)}, u32[]{:S(2)}) collective-permute-start(bf16[256,256]{0,1:T(8,128)(2,1)S(1)} %get-tuple-element.25), channel_id=1, source_target_pairs={{0,32},{4,36},{8,40},{12,44},{16,48},{20,52},{24,56},{28,60},{32,6... | collective-permute-start | bytes 393224 | tf_op jit(solution)/shard_map/ppermute | solution.py:26
  134.9 30.8 %collective-permute-start.22 = (bf16[256,256]{0,1:T(8,128)(2,1)S(1)}, bf16[256,256]{0,1:T(8,128)(2,1)S(1)}, u32[]{:S(2)}, u32[]{:S(2)}) collective-permute-start(bf16[256,256]{0,1:T(8,128)(2,1)S(1)} %get-tuple-element.26), channel_id=1, source_target_pairs={{16,0},{20,4},{24,8},{28,12},{32,16},{36,20},{40,24},{44,28},{48,3... | collective-permute-start | bytes 393224 | tf_op jit(solution)/shard_map/ppermute | solution.py:26
  141.8 25.9 %collective-permute-start.21 = (bf16[256,256]{0,1:T(8,128)(2,1)S(1)}, bf16[256,256]{0,1:T(8,128)(2,1)S(1)}, u32[]{:S(2)}, u32[]{:S(2)}) collective-permute-start(bf16[256,256]{0,1:T(8,128)(2,1)S(1)} %get-tuple-element.27), channel_id=1, source_target_pairs={{0,16},{4,20},{8,24},{12,28},{16,32},{20,36},{24,40},{28,44},{32,4... | collective-permute-start | bytes 393224 | tf_op jit(solution)/shard_map/ppermute | solution.py:26
  143.7 28.5 %collective-permute-start.20 = (bf16[256,256]{0,1:T(8,128)(2,1)}, bf16[256,256]{0,1:T(8,128)(2,1)S(1)}, u32[]{:S(2)}, u32[]{:S(2)}) collective-permute-start(bf16[256,256]{0,1:T(8,128)(2,1)} %get-tuple-element.28), channel_id=1, source_target_pairs={{12,0},{16,4},{20,8},{24,12},{28,16},{32,20},{36,24},{40,28},{44,3... | collective-permute-start | bytes 393224 | tf_op jit(solution)/shard_map/ppermute | solution.py:26
  148.1 24.1 %collective-permute-start.19 = (bf16[256,256]{0,1:T(8,128)(2,1)S(1)}, bf16[256,256]{0,1:T(8,128)(2,1)S(1)}, u32[]{:S(2)}, u32[]{:S(2)}) collective-permute-start(bf16[256,256]{0,1:T(8,128)(2,1)S(1)} %get-tuple-element.29), channel_id=1, source_target_pairs={{0,12},{4,16},{8,20},{12,24},{16,28},{20,32},{24,36},{28,40},{32,4... | collective-permute-start | bytes 393224 | tf_op jit(solution)/shard_map/ppermute | solution.py:26
  150.1 22.2 %collective-permute-start.18 = (bf16[256,256]{0,1:T(8,128)(2,1)S(1)}, bf16[256,256]{0,1:T(8,128)(2,1)S(1)}, u32[]{:S(2)}, u32[]{:S(2)}) collective-permute-start(bf16[256,256]{0,1:T(8,128)(2,1)S(1)} %get-tuple-element.30), channel_id=1, source_target_pairs={{8,0},{12,4},{16,8},{20,12},{24,16},{28,20},{32,24},{36,28},{40,32... | collective-permute-start | bytes 393224 | tf_op jit(solution)/shard_map/ppermute | solution.py:26
  (10 other events, 185.1 us)

commit v7 on v6

--- a/solution.py
+++ b/solution.py
@@ -104,30 +104,41 @@
     entries = jnp.take(frame_rows, jnp.clip(other_frame, 0, frame_count - 1), axis=0)
     seen = is_valid[:, None] & (entries >= 0)
     blocks = tok_rows // BLK
-    row_block = jnp.arange(tok_rows, dtype=jnp.int32) // BLK
     near_mask = jnp.broadcast_to(
         near_ok[None, :, None], (tok_rows, 3, tok_rows)
     ).reshape(tok_rows, 3 * tok_rows)
-    seen_rows = jnp.take(seen, row_block, axis=1)
-    diag = row_block[:, None] == row_block[None, :]
-    far_mask = (diag[:, None, :] & seen_rows.T[:, :, None]).reshape(
-        tok_rows, len(offsets) * tok_rows
-    )
-    keys_all = jnp.concatenate(pieces, axis=0)
-    visible = jnp.concatenate([near_mask, far_mask], axis=1)
-    attention_out, query_grad, weights, dscores, log_total, row_delta = attend_parts(
-        query_tokens, grad_out, keys_all, visible
-    )
-    near_terms = key_terms(
-        weights[:, : 3 * tok_rows], dscores[:, : 3 * tok_rows], query_tokens, grad_out
+    near_keys_all = pieces[0]
+    far_pieces = pieces[1:]
+    outs, dqs, near_parts, far_parts = [], [], [], []
+    for blk in range(blocks):
+        rs = slice(blk * BLK, (blk + 1) * BLK)
+        kv = jnp.concatenate([near_keys_all] + [p[rs] for p in far_pieces], axis=0)
+        far_cols = jnp.broadcast_to(seen[:, blk][None, :, None], (BLK, len(offsets), BLK))
+        visible = jnp.concatenate(
+            [near_mask[rs], far_cols.reshape(BLK, len(offsets) * BLK)], axis=1
+        )
+        out_b, dq_b, weights, dscores, log_total, row_delta = attend_parts(
+            query_tokens[rs], grad_out[rs], kv, visible
+        )
+        terms_b = key_terms(weights, dscores, query_tokens[rs], grad_out[rs])
+        outs.append(out_b)
+        dqs.append(dq_b)
+        near_parts.append(terms_b[: 3 * tok_rows])
+        far_parts.append(terms_b[3 * tok_rows :])
+    attention_out = jnp.concatenate(outs, axis=0)
+    query_grad = jnp.concatenate(dqs, axis=0)
+    near_terms = sum(near_parts[1:], near_parts[0])
+    far_terms = jnp.concatenate(
+        [
+            jnp.concatenate([part[i * BLK : (i + 1) * BLK] for part in far_parts], axis=0)
+            for i in range(len(offsets))
+        ],
+        axis=0,
     )
     sent = near_terms.astype(jnp.bfloat16)
     from_after = from_behind(sent[:tok_rows], "seq", -1).astype(jnp.float32)
     from_before = from_behind(sent[2 * tok_rows :], "seq", 1).astype(jnp.float32)
     grad_total = near_terms[tok_rows : 2 * tok_rows] + from_after + from_before
-    far_terms = key_terms(
-        weights[:, 3 * tok_rows :], dscores[:, 3 * tok_rows :], query_tokens, grad_out
-    )
     for slot_index in range(len(offsets)):
         first_row = slot_index * 2 * BLK
         grad_piece = far_terms[first_row : first_row + 2 * BLK].astype(jnp.bfloat16)

time: 180 us -> 205 us (1.14)
  the two profiles are of different devices: /device:TPU:34 before, /device:TPU:1 now
where the time goes in v7:
time: 205 us; the launch traced here: 202 us
  starting transfers between devices  137 us (67%)
  waiting for transfers between devices  50.1 us (24%)
  local copies, waits for them, and re-layouts  5.95 us (3%)
  matrix products  4.38 us (2%)
  other arithmetic  3.93 us (2%)
    ppermute x26, starting transfers between devices, from_behind(): lax.ppermute(value, axis, [(source, source + steps) for source in range(l...  106 us
    ppermute x26, waiting for transfers between devices, from_behind(): lax.ppermute(value, axis, [(source, source + steps) for source in range(l...  46.7 us
    ppermute x1, starting transfers between devices, shards(): lax.ppermute(grad_piece, 'seq', [(src, (src + half) % frame_count) for sr...  14.2 us
    ppermute x1, starting transfers between devices, shards(): lax.ppermute(joined, 'seq', [(src, (src + half) % frame_count) for src in...  8.28 us
    ppermute x1, starting transfers between devices, extended(): before = lax.ppermute(last, axis, up)  5.75 us
  transfers between devices with their start and end apart: 30, of which 10 were waited for; matrix products, arithmetic and copies ran while one was open for 3% of the time, Pallas kernels for 0%

profile of v7, /device:TPU:1, one launch (start us, length us, event | category | flops | bytes accessed | tf_op | source)
XLA Modules:
  0.0 202.3 jit_solution(2058903354789481892)
XLA Ops:
  2.4 8.3 %collective-permute-start.14 = (bf16[256,256]{1,0:T(8,128)(2,1)S(1)}, bf16[256,256]{1,0:T(8,128)(2,1)S(1)}, u32[]{:S(2)}, u32[]{:S(2)}) collective-permute-start(bf16[256,256]{1,0:T(8,128)(2,1)S(1)} %constant_dynamic-update-slice_fusion), channel_id=1, source_target_pairs={{0,256},{4,260},{8,264},{12,268},{16,272},{20,276},{24,280},{28,28... | collective-permute-start | bytes 393224 | tf_op jit(solution)/shard_map/ppermute | solution.py:94
  10.7 2.4 %collective-permute-start.13 = (bf16[256,256]{1,0:T(8,128)(2,1)S(1)}, bf16[256,256]{1,0:T(8,128)(2,1)S(1)}, u32[]{:S(2)}, u32[]{:S(2)}) collective-permute-start(bf16[256,256]{1,0:T(8,128)(2,1)S(1)} %constant_dynamic-update-slice_fusion), channel_id=1, source_target_pairs={{0,128},{4,132},{8,136},{12,140},{16,144},{20,148},{24,152},{28,15... | collective-permute-start | bytes 393224 | tf_op jit(solution)/shard_map/ppermute | solution.py:26
  15.7 5.7 %collective-permute-start = (bf16[256,256]{1,0:T(8,128)(2,1)S(1)}, bf16[256,256]{1,0:T(8,128)(2,1)S(1)}, u32[]{:S(2)}, u32[]{:S(2)}) collective-permute-start(bf16[256,256]{1,0:T(8,128)(2,1)S(1)} %constant_dynamic-update-slice_fusion), channel_id=1, source_target_pairs={{0,4},{4,8},{8,12},{12,16},{16,20},{20,24},{24,28},{28,32},{32,36}... | collective-permute-start | bytes 393224 | tf_op jit(solution)/shard_map/ppermute | solution.py:17
  23.4 1.9 collective-permute-start.1
  27.1 3.3 %collective-permute-done.1 = bf16[256,256]{1,0:T(8,128)(2,1)S(1)} collective-permute-done((bf16[256,256]{1,0:T(8,128)(2,1)S(1)}, bf16[256,256]{1,0:T(8,128)(2,1)S(1)}, u32[]{:S(2)}, u32[]{:S(2)}) %collective-permute-start.1) | collective-permute-done | bytes 131104 | tf_op jit(solution)/shard_map/ppermute | solution.py:18
  30.4 11.4 %collective-permute-start.11 = (bf16[256,256]{1,0:T(8,128)(2,1)S(1)}, bf16[256,256]{1,0:T(8,128)(2,1)S(1)}, u32[]{:S(2)}, u32[]{:S(2)}) collective-permute-start(bf16[256,256]{1,0:T(8,128)(2,1)S(1)} %constant_dynamic-update-slice_fusion), channel_id=1, source_target_pairs={{0,64},{4,68},{8,72},{12,76},{16,80},{20,84},{24,88},{28,92},{32,9... | collective-permute-start | bytes 393224 | tf_op jit(solution)/shard_map/ppermute | solution.py:26
  43.2 1.9 collective-permute-done.3
  46.4 6.0 %collective-permute-done.4 = bf16[256,256]{1,0:T(8,128)(2,1)S(1)} collective-permute-done((bf16[256,256]{1,0:T(8,128)(2,1)S(1)}, bf16[256,256]{1,0:T(8,128)(2,1)S(1)}, u32[]{:S(2)}, u32[]{:S(2)}) %collective-permute-start.4) | collective-permute-done | bytes 131104 | tf_op jit(solution)/shard_map/ppermute | solution.py:26
  54.1 1.9 collective-permute-done.5
  57.3 11.0 %collective-permute-done.6 = bf16[256,256]{1,0:T(8,128)(2,1)S(1)} collective-permute-done((bf16[256,256]{1,0:T(8,128)(2,1)S(1)}, bf16[256,256]{1,0:T(8,128)(2,1)S(1)}, u32[]{:S(2)}, u32[]{:S(2)}) %collective-permute-start.6) | collective-permute-done | bytes 131104 | tf_op jit(solution)/shard_map/ppermute | solution.py:26
  68.3 10.0 %collective-permute-start.7 = (bf16[256,256]{1,0:T(8,128)(2,1)S(1)}, bf16[256,256]{1,0:T(8,128)(2,1)S(1)}, u32[]{:S(2)}, u32[]{:S(2)}) collective-permute-start(bf16[256,256]{1,0:T(8,128)(2,1)S(1)} %constant_dynamic-update-slice_fusion), channel_id=1, source_target_pairs={{0,16},{4,20},{8,24},{12,28},{16,32},{20,36},{24,40},{28,44},{32,4... | collective-permute-start | bytes 393224 | tf_op jit(solution)/shard_map/ppermute | solution.py:26
  78.3 1.9 collective-permute-done.7
  81.6 14.0 %collective-permute-done.8 = bf16[256,256]{1,0:T(8,128)(2,1)S(1)} collective-permute-done((bf16[256,256]{1,0:T(8,128)(2,1)S(1)}, bf16[256,256]{1,0:T(8,128)(2,1)S(1)}, u32[]{:S(2)}, u32[]{:S(2)}) %collective-permute-start.8) | collective-permute-done | bytes 131104 | tf_op jit(solution)/shard_map/ppermute | solution.py:26
  95.6 8.7 %collective-permute-start.9 = (bf16[256,256]{1,0:T(8,128)(2,1)S(1)}, bf16[256,256]{1,0:T(8,128)(2,1)S(1)}, u32[]{:S(2)}, u32[]{:S(2)}) collective-permute-start(bf16[256,256]{1,0:T(8,128)(2,1)S(1)} %constant_dynamic-update-slice_fusion), channel_id=1, source_target_pairs={{0,32},{4,36},{8,40},{12,44},{16,48},{20,52},{24,56},{28,60},{32,6... | collective-permute-start | bytes 393224 | tf_op jit(solution)/shard_map/ppermute | solution.py:26
  104.3 1.9 collective-permute-done.9
  107.5 6.7 %collective-permute-done.10 = bf16[256,256]{1,0:T(8,128)(2,1)S(1)} collective-permute-done((bf16[256,256]{1,0:T(8,128)(2,1)S(1)}, bf16[256,256]{1,0:T(8,128)(2,1)S(1)}, u32[]{:S(2)}, u32[]{:S(2)}) %collective-permute-start.10) | collective-permute-done | bytes 131104 | tf_op jit(solution)/shard_map/ppermute | solution.py:26
  122.1 8.9 %collective-permute-start.19 = (bf16[256,256]{1,0:T(8,128)(2,1)S(1)}, bf16[256,256]{1,0:T(8,128)(2,1)S(1)}, u32[]{:S(2)}, u32[]{:S(2)}) collective-permute-start(bf16[256,256]{1,0:T(8,128)(2,1)S(1)} %pad_maximum_fusion.6), channel_id=1, source_target_pairs={{0,12},{4,16},{8,20},{12,24},{16,28},{20,32},{24,36},{28,40},{32,4... | collective-permute-start | bytes 393224 | tf_op jit(solution)/shard_map/ppermute | solution.py:26
  132.4 7.1 %collective-permute-start.21 = (bf16[256,256]{1,0:T(8,128)(2,1)S(1)}, bf16[256,256]{1,0:T(8,128)(2,1)S(1)}, u32[]{:S(2)}, u32[]{:S(2)}) collective-permute-start(bf16[256,256]{1,0:T(8,128)(2,1)S(1)} %pad_maximum_fusion.8), channel_id=1, source_target_pairs={{0,16},{4,20},{8,24},{12,28},{16,32},{20,36},{24,40},{28,44},{32,4... | collective-permute-start | bytes 393224 | tf_op jit(solution)/shard_map/ppermute | solution.py:26
  140.9 7.8 %collective-permute-start.23 = (bf16[256,256]{1,0:T(8,128)(2,1)S(1)}, bf16[256,256]{1,0:T(8,128)(2,1)S(1)}, u32[]{:S(2)}, u32[]{:S(2)}) collective-permute-start(bf16[256,256]{1,0:T(8,128)(2,1)S(1)} %pad_maximum_fusion.10), channel_id=1, source_target_pairs={{0,32},{4,36},{8,40},{12,44},{16,48},{20,52},{24,56},{28,60},{32,6... | collective-permute-start | bytes 393224 | tf_op jit(solution)/shard_map/ppermute | solution.py:26
  150.0 10.5 %collective-permute-start.25 = (bf16[256,256]{1,0:T(8,128)(2,1)S(1)}, bf16[256,256]{1,0:T(8,128)(2,1)S(1)}, u32[]{:S(2)}, u32[]{:S(2)}) collective-permute-start(bf16[256,256]{1,0:T(8,128)(2,1)S(1)} %pad_maximum_fusion.12), channel_id=1, source_target_pairs={{0,64},{4,68},{8,72},{12,76},{16,80},{20,84},{24,88},{28,92},{32,9... | collective-permute-start | bytes 393224 | tf_op jit(solution)/shard_map/ppermute | solution.py:26
  161.9 7.4 %collective-permute-start.27 = (bf16[256,256]{1,0:T(8,128)(2,1)S(1)}, bf16[256,256]{1,0:T(8,128)(2,1)S(1)}, u32[]{:S(2)}, u32[]{:S(2)}) collective-permute-start(bf16[256,256]{1,0:T(8,128)(2,1)S(1)} %pad_maximum_fusion.14), channel_id=1, source_target_pairs={{0,128},{4,132},{8,136},{12,140},{16,144},{20,148},{24,152},{28,15... | collective-permute-start | bytes 393224 | tf_op jit(solution)/shard_map/ppermute | solution.py:26
  170.7 14.2 %collective-permute-start.29 = (bf16[256,256]{1,0:T(8,128)(2,1)S(1)}, bf16[256,256]{1,0:T(8,128)(2,1)S(1)}, u32[]{:S(2)}, u32[]{:S(2)}) collective-permute-start(bf16[256,256]{1,0:T(8,128)(2,1)S(1)} %pad_maximum_fusion.16), channel_id=1, source_target_pairs={{0,256},{4,260},{8,264},{12,268},{16,272},{20,276},{24,280},{28,28... | collective-permute-start | bytes 393224 | tf_op jit(solution)/shard_map/ppermute | solution.py:146
  184.9 10.5 %collective-permute-start.15 = (bf16[256,256]{1,0:T(8,128)(2,1)S(1)}, bf16[256,256]{1,0:T(8,128)(2,1)S(1)}, u32[]{:S(2)}, u32[]{:S(2)}) collective-permute-start(bf16[256,256]{1,0:T(8,128)(2,1)S(1)} %get-tuple-element.38), channel_id=1, source_target_pairs={{4,0},{8,4},{12,8},{16,12},{20,16},{24,20},{28,24},{32,28},{36,32}... | collective-permute-start | bytes 393224 | tf_op jit(solution)/shard_map/ppermute | solution.py:26
  195.4 1.9 collective-permute-start.16
  (116 shorter events, 35.4 us)
Async XLA Ops:
  2.4 112.0 %collective-permute-start.14 = (bf16[256,256]{1,0:T(8,128)(2,1)S(1)}, bf16[256,256]{1,0:T(8,128)(2,1)S(1)}, u32[]{:S(2)}, u32[]{:S(2)}) collective-permute-start(bf16[256,256]{1,0:T(8,128)(2,1)S(1)} %constant_dynamic-update-slice_fusion), channel_id=1, source_target_pairs={{0,256},{4,260},{8,264},{12,268},{16,272},{20,276},{24,280},{28,28... | collective-permute-start | bytes 393224 | tf_op jit(solution)/shard_map/ppermute | solution.py:94
  10.7 103.6 %collective-permute-start.13 = (bf16[256,256]{1,0:T(8,128)(2,1)S(1)}, bf16[256,256]{1,0:T(8,128)(2,1)S(1)}, u32[]{:S(2)}, u32[]{:S(2)}) collective-permute-start(bf16[256,256]{1,0:T(8,128)(2,1)S(1)} %constant_dynamic-update-slice_fusion), channel_id=1, source_target_pairs={{0,128},{4,132},{8,136},{12,140},{16,144},{20,148},{24,152},{28,15... | collective-permute-start | bytes 393224 | tf_op jit(solution)/shard_map/ppermute | solution.py:26
  13.1 101.2 %collective-permute-start.12 = (bf16[256,256]{1,0:T(8,128)(2,1)S(1)}, bf16[256,256]{1,0:T(8,128)(2,1)S(1)}, u32[]{:S(2)}, u32[]{:S(2)}) collective-permute-start(bf16[256,256]{1,0:T(8,128)(2,1)S(1)} %constant_dynamic-update-slice_fusion), channel_id=1, source_target_pairs={{128,0},{132,4},{136,8},{140,12},{144,16},{148,20},{152,24},{156,2... | collective-permute-start | bytes 393224 | tf_op jit(solution)/shard_map/ppermute | solution.py:26
  14.4 27.5 %collective-permute-start.2 = (bf16[256,256]{1,0:T(8,128)(2,1)S(1)}, bf16[256,256]{1,0:T(8,128)(2,1)S(1)}, u32[]{:S(2)}, u32[]{:S(2)}) collective-permute-start(bf16[256,256]{1,0:T(8,128)(2,1)S(1)} %constant_dynamic-update-slice_fusion), channel_id=1, source_target_pairs={{8,0},{12,4},{16,8},{20,12},{24,16},{28,20},{32,24},{36,28},{40,32... | collective-permute-start | bytes 393224 | tf_op jit(solution)/shard_map/ppermute | solution.py:26
  15.7 7.7 %collective-permute-start = (bf16[256,256]{1,0:T(8,128)(2,1)S(1)}, bf16[256,256]{1,0:T(8,128)(2,1)S(1)}, u32[]{:S(2)}, u32[]{:S(2)}) collective-permute-start(bf16[256,256]{1,0:T(8,128)(2,1)S(1)} %constant_dynamic-update-slice_fusion), channel_id=1, source_target_pairs={{0,4},{4,8},{8,12},{12,16},{16,20},{20,24},{24,28},{28,32},{32,36}... | collective-permute-start | bytes 393224 | tf_op jit(solution)/shard_map/ppermute | solution.py:17
  30.4 83.9 %collective-permute-start.11 = (bf16[256,256]{1,0:T(8,128)(2,1)S(1)}, bf16[256,256]{1,0:T(8,128)(2,1)S(1)}, u32[]{:S(2)}, u32[]{:S(2)}) collective-permute-start(bf16[256,256]{1,0:T(8,128)(2,1)S(1)} %constant_dynamic-update-slice_fusion), channel_id=1, source_target_pairs={{0,64},{4,68},{8,72},{12,76},{16,80},{20,84},{24,88},{28,92},{32,9... | collective-permute-start | bytes 393224 | tf_op jit(solution)/shard_map/ppermute | solution.py:26
  56.0 12.3 %collective-permute-start.6 = (bf16[256,256]{1,0:T(8,128)(2,1)S(1)}, bf16[256,256]{1,0:T(8,128)(2,1)S(1)}, u32[]{:S(2)}, u32[]{:S(2)}) collective-permute-start(bf16[256,256]{1,0:T(8,128)(2,1)S(1)} %constant_dynamic-update-slice_fusion), channel_id=1, source_target_pairs={{16,0},{20,4},{24,8},{28,12},{32,16},{36,20},{40,24},{44,28},{48,3... | collective-permute-start | bytes 393224 | tf_op jit(solution)/shard_map/ppermute | solution.py:26
  68.3 12.0 %collective-permute-start.7 = (bf16[256,256]{1,0:T(8,128)(2,1)S(1)}, bf16[256,256]{1,0:T(8,128)(2,1)S(1)}, u32[]{:S(2)}, u32[]{:S(2)}) collective-permute-start(bf16[256,256]{1,0:T(8,128)(2,1)S(1)} %constant_dynamic-update-slice_fusion), channel_id=1, source_target_pairs={{0,16},{4,20},{8,24},{12,28},{16,32},{20,36},{24,40},{28,44},{32,4... | collective-permute-start | bytes 393224 | tf_op jit(solution)/shard_map/ppermute | solution.py:26
  80.3 15.3 %collective-permute-start.8 = (bf16[256,256]{1,0:T(8,128)(2,1)S(1)}, bf16[256,256]{1,0:T(8,128)(2,1)S(1)}, u32[]{:S(2)}, u32[]{:S(2)}) collective-permute-start(bf16[256,256]{1,0:T(8,128)(2,1)S(1)} %constant_dynamic-update-slice_fusion), channel_id=1, source_target_pairs={{32,0},{36,4},{40,8},{44,12},{48,16},{52,20},{56,24},{60,28},{64,3... | collective-permute-start | bytes 393224 | tf_op jit(solution)/shard_map/ppermute | solution.py:26
  95.6 10.7 %collective-permute-start.9 = (bf16[256,256]{1,0:T(8,128)(2,1)S(1)}, bf16[256,256]{1,0:T(8,128)(2,1)S(1)}, u32[]{:S(2)}, u32[]{:S(2)}) collective-permute-start(bf16[256,256]{1,0:T(8,128)(2,1)S(1)} %constant_dynamic-update-slice_fusion), channel_id=1, source_target_pairs={{0,32},{4,36},{8,40},{12,44},{16,48},{20,52},{24,56},{28,60},{32,6... | collective-permute-start | bytes 393224 | tf_op jit(solution)/shard_map/ppermute | solution.py:26
  106.2 8.0 %collective-permute-start.10 = (bf16[256,256]{1,0:T(8,128)(2,1)S(1)}, bf16[256,256]{1,0:T(8,128)(2,1)S(1)}, u32[]{:S(2)}, u32[]{:S(2)}) collective-permute-start(bf16[256,256]{1,0:T(8,128)(2,1)S(1)} %constant_dynamic-update-slice_fusion), channel_id=1, source_target_pairs={{64,0},{68,4},{72,8},{76,12},{80,16},{84,20},{88,24},{92,28},{96,3... | collective-permute-start | bytes 393224 | tf_op jit(solution)/shard_map/ppermute | solution.py:26
  120.8 20.1 %collective-permute-start.18 = (bf16[256,256]{1,0:T(8,128)(2,1)S(1)}, bf16[256,256]{1,0:T(8,128)(2,1)S(1)}, u32[]{:S(2)}, u32[]{:S(2)}) collective-permute-start(bf16[256,256]{1,0:T(8,128)(2,1)S(1)} %pad_maximum_fusion.5), channel_id=1, source_target_pairs={{8,0},{12,4},{16,8},{20,12},{24,16},{28,20},{32,24},{36,28},{40,32... | collective-permute-start | bytes 393224 | tf_op jit(solution)/shard_map/ppermute | solution.py:26
  122.1 26.6 %collective-permute-start.19 = (bf16[256,256]{1,0:T(8,128)(2,1)S(1)}, bf16[256,256]{1,0:T(8,128)(2,1)S(1)}, u32[]{:S(2)}, u32[]{:S(2)}) collective-permute-start(bf16[256,256]{1,0:T(8,128)(2,1)S(1)} %pad_maximum_fusion.6), channel_id=1, source_target_pairs={{0,12},{4,16},{8,20},{12,24},{16,28},{20,32},{24,36},{28,40},{32,4... | collective-permute-start | bytes 393224 | tf_op jit(solution)/shard_map/ppermute | solution.py:26
  131.1 19.0 %collective-permute-start.20 = (bf16[256,256]{1,0:T(8,128)(2,1)S(1)}, bf16[256,256]{1,0:T(8,128)(2,1)S(1)}, u32[]{:S(2)}, u32[]{:S(2)}) collective-permute-start(bf16[256,256]{1,0:T(8,128)(2,1)S(1)} %pad_maximum_fusion.7), channel_id=1, source_target_pairs={{12,0},{16,4},{20,8},{24,12},{28,16},{32,20},{36,24},{40,28},{44,3... | collective-permute-start | bytes 393224 | tf_op jit(solution)/shard_map/ppermute | solution.py:26
  132.4 28.2 %collective-permute-start.21 = (bf16[256,256]{1,0:T(8,128)(2,1)S(1)}, bf16[256,256]{1,0:T(8,128)(2,1)S(1)}, u32[]{:S(2)}, u32[]{:S(2)}) collective-permute-start(bf16[256,256]{1,0:T(8,128)(2,1)S(1)} %pad_maximum_fusion.8), channel_id=1, source_target_pairs={{0,16},{4,20},{8,24},{12,28},{16,32},{20,36},{24,40},{28,44},{32,4... | collective-permute-start | bytes 393224 | tf_op jit(solution)/shard_map/ppermute | solution.py:26
  139.5 22.4 %collective-permute-start.22 = (bf16[256,256]{1,0:T(8,128)(2,1)S(1)}, bf16[256,256]{1,0:T(8,128)(2,1)S(1)}, u32[]{:S(2)}, u32[]{:S(2)}) collective-permute-start(bf16[256,256]{1,0:T(8,128)(2,1)S(1)} %pad_maximum_fusion.9), channel_id=1, source_target_pairs={{16,0},{20,4},{24,8},{28,12},{32,16},{36,20},{40,24},{44,28},{48,3... | collective-permute-start | bytes 393224 | tf_op jit(solution)/shard_map/ppermute | solution.py:26
  140.9 28.5 %collective-permute-start.23 = (bf16[256,256]{1,0:T(8,128)(2,1)S(1)}, bf16[256,256]{1,0:T(8,128)(2,1)S(1)}, u32[]{:S(2)}, u32[]{:S(2)}) collective-permute-start(bf16[256,256]{1,0:T(8,128)(2,1)S(1)} %pad_maximum_fusion.10), channel_id=1, source_target_pairs={{0,32},{4,36},{8,40},{12,44},{16,48},{20,52},{24,56},{28,60},{32,6... | collective-permute-start | bytes 393224 | tf_op jit(solution)/shard_map/ppermute | solution.py:26
  148.7 21.9 %collective-permute-start.24 = (bf16[256,256]{1,0:T(8,128)(2,1)S(1)}, bf16[256,256]{1,0:T(8,128)(2,1)S(1)}, u32[]{:S(2)}, u32[]{:S(2)}) collective-permute-start(bf16[256,256]{1,0:T(8,128)(2,1)S(1)} %pad_maximum_fusion.11), channel_id=1, source_target_pairs={{32,0},{36,4},{40,8},{44,12},{48,16},{52,20},{56,24},{60,28},{64,3... | collective-permute-start | bytes 393224 | tf_op jit(solution)/shard_map/ppermute | solution.py:26
  150.0 34.8 %collective-permute-start.25 = (bf16[256,256]{1,0:T(8,128)(2,1)S(1)}, bf16[256,256]{1,0:T(8,128)(2,1)S(1)}, u32[]{:S(2)}, u32[]{:S(2)}) collective-permute-start(bf16[256,256]{1,0:T(8,128)(2,1)S(1)} %pad_maximum_fusion.12), channel_id=1, source_target_pairs={{0,64},{4,68},{8,72},{12,76},{16,80},{20,84},{24,88},{28,92},{32,9... | collective-permute-start | bytes 393224 | tf_op jit(solution)/shard_map/ppermute | solution.py:26
  160.6 34.8 %collective-permute-start.26 = (bf16[256,256]{1,0:T(8,128)(2,1)S(1)}, bf16[256,256]{1,0:T(8,128)(2,1)S(1)}, u32[]{:S(2)}, u32[]{:S(2)}) collective-permute-start(bf16[256,256]{1,0:T(8,128)(2,1)S(1)} %pad_maximum_fusion.13), channel_id=1, source_target_pairs={{64,0},{68,4},{72,8},{76,12},{80,16},{84,20},{88,24},{92,28},{96,3... | collective-permute-start | bytes 393224 | tf_op jit(solution)/shard_map/ppermute | solution.py:26
  161.9 35.5 %collective-permute-start.27 = (bf16[256,256]{1,0:T(8,128)(2,1)S(1)}, bf16[256,256]{1,0:T(8,128)(2,1)S(1)}, u32[]{:S(2)}, u32[]{:S(2)}) collective-permute-start(bf16[256,256]{1,0:T(8,128)(2,1)S(1)} %pad_maximum_fusion.14), channel_id=1, source_target_pairs={{0,128},{4,132},{8,136},{12,140},{16,144},{20,148},{24,152},{28,15... | collective-permute-start | bytes 393224 | tf_op jit(solution)/shard_map/ppermute | solution.py:26
  169.4 30.6 %collective-permute-start.28 = (bf16[256,256]{1,0:T(8,128)(2,1)S(1)}, bf16[256,256]{1,0:T(8,128)(2,1)S(1)}, u32[]{:S(2)}, u32[]{:S(2)}) collective-permute-start(bf16[256,256]{1,0:T(8,128)(2,1)S(1)} %pad_maximum_fusion.15), channel_id=1, source_target_pairs={{128,0},{132,4},{136,8},{140,12},{144,16},{148,20},{152,24},{156,2... | collective-permute-start | bytes 393224 | tf_op jit(solution)/shard_map/ppermute | solution.py:26
  170.7 29.3 %collective-permute-start.29 = (bf16[256,256]{1,0:T(8,128)(2,1)S(1)}, bf16[256,256]{1,0:T(8,128)(2,1)S(1)}, u32[]{:S(2)}, u32[]{:S(2)}) collective-permute-start(bf16[256,256]{1,0:T(8,128)(2,1)S(1)} %pad_maximum_fusion.16), channel_id=1, source_target_pairs={{0,256},{4,260},{8,264},{12,268},{16,272},{20,276},{24,280},{28,28... | collective-permute-start | bytes 393224 | tf_op jit(solution)/shard_map/ppermute | solution.py:146
  184.9 15.1 %collective-permute-start.15 = (bf16[256,256]{1,0:T(8,128)(2,1)S(1)}, bf16[256,256]{1,0:T(8,128)(2,1)S(1)}, u32[]{:S(2)}, u32[]{:S(2)}) collective-permute-start(bf16[256,256]{1,0:T(8,128)(2,1)S(1)} %get-tuple-element.38), channel_id=1, source_target_pairs={{4,0},{8,4},{12,8},{16,12},{20,16},{24,20},{28,24},{32,28},{36,32}... | collective-permute-start | bytes 393224 | tf_op jit(solution)/shard_map/ppermute | solution.py:26
  (9 other events, 109.2 us)

commit v8 on v6

--- a/solution.py
+++ b/solution.py
@@ -88,7 +88,7 @@
     near_ok = (neighbour >= 0) & (neighbour < frame_count)
     pieces = [near_keys]
     half = frame_count // 2
-    offsets = [o for o in offsets if o != -half]
+    offsets = [o for o in (8, -8, half, 4, -4, 32, -32, 3, -3, 16, -16, 2, -2) if o in offsets]
     for offset in offsets:
         if offset == half:
             arrived = lax.ppermute(

time: 180 us -> 166 us (0.922)
  the two profiles are of different devices: /device:TPU:34 before, /device:TPU:1 now
where the time goes in v8:
time: 166 us; the launch traced here: 164 us
  starting transfers between devices  124 us (75%)
  waiting for transfers between devices  18.5 us (11%)
  local copies, waits for them, and re-layouts  8.93 us (5%)
  matrix products  7.99 us (5%)
  other arithmetic  3.02 us (2%)
    ppermute x26, starting transfers between devices, from_behind(): lax.ppermute(value, axis, [(source, source + steps) for source in range(l...  103 us
    ppermute x1, starting transfers between devices, shards(): lax.ppermute(grad_piece, 'seq', [(src, (src + half) % frame_count) for sr...  10.2 us
    ppermute x26, waiting for transfers between devices, from_behind(): lax.ppermute(value, axis, [(source, source + steps) for source in range(l...  9.86 us
    ppermute x1, starting transfers between devices, shards(): lax.ppermute(joined, 'seq', [(src, (src + half) % frame_count) for src in...  7.2 us
    unnamed x29, local copies, waits for them, and re-layouts  5.43 us
    ppermute x1, waiting for transfers between devices, extended(): after = lax.ppermute(leading, axis, down)  4.19 us
  transfers between devices with their start and end apart: 30, of which 7 were waited for; matrix products, arithmetic and copies ran while one was open for 5% of the time, Pallas kernels for 0%

profile of v8, /device:TPU:1, one launch (start us, length us, event | category | flops | bytes accessed | tf_op | source)
XLA Modules:
  0.0 164.1 jit_solution(12350842688543179820)
XLA Ops:
  2.4 4.8 %collective-permute-start.14 = (bf16[256,256]{1,0:T(8,128)(2,1)S(1)}, bf16[256,256]{1,0:T(8,128)(2,1)S(1)}, u32[]{:S(2)}, u32[]{:S(2)}) collective-permute-start(bf16[256,256]{1,0:T(8,128)(2,1)S(1)} %constant_dynamic-update-slice_fusion), channel_id=1, source_target_pairs={{0,8},{4,12},{8,16},{12,20},{16,24},{20,28},{24,32},{28,36},{32,40... | collective-permute-start | bytes 393224 | tf_op jit(solution)/shard_map/ppermute | solution.py:26
  8.6 10.4 %collective-permute-start.12 = (bf16[256,256]{1,0:T(8,128)(2,1)S(1)}, bf16[256,256]{1,0:T(8,128)(2,1)S(1)}, u32[]{:S(2)}, u32[]{:S(2)}) collective-permute-start(bf16[256,256]{1,0:T(8,128)(2,1)S(1)} %constant_dynamic-update-slice_fusion), channel_id=1, source_target_pairs={{0,64},{4,68},{8,72},{12,76},{16,80},{20,84},{24,88},{28,92},{32,9... | collective-permute-start | bytes 393224 | tf_op jit(solution)/shard_map/ppermute | solution.py:26
  20.2 1.9 %collective-permute-start = (bf16[256,256]{1,0:T(8,128)(2,1)S(1)}, bf16[256,256]{1,0:T(8,128)(2,1)S(1)}, u32[]{:S(2)}, u32[]{:S(2)}) collective-permute-start(bf16[256,256]{1,0:T(8,128)(2,1)S(1)} %constant_dynamic-update-slice_fusion), channel_id=1, source_target_pairs={{0,4},{4,8},{8,12},{12,16},{16,20},{20,24},{24,28},{28,32},{32,36}... | collective-permute-start | bytes 393224 | tf_op jit(solution)/shard_map/ppermute | solution.py:17
  26.4 3.2 %collective-permute-done = bf16[256,256]{1,0:T(8,128)(2,1)S(1)} collective-permute-done((bf16[256,256]{1,0:T(8,128)(2,1)S(1)}, bf16[256,256]{1,0:T(8,128)(2,1)S(1)}, u32[]{:S(2)}, u32[]{:S(2)}) %collective-permute-start) | collective-permute-done | bytes 131104 | tf_op jit(solution)/shard_map/ppermute | solution.py:17
  29.7 1.9 %collective-permute-start.1 = (bf16[256,256]{1,0:T(8,128)(2,1)S(1)}, bf16[256,256]{1,0:T(8,128)(2,1)S(1)}, u32[]{:S(2)}, u32[]{:S(2)}) collective-permute-start(bf16[256,256]{1,0:T(8,128)(2,1)S(1)} %constant_dynamic-update-slice_fusion), channel_id=1, source_target_pairs={{4,0},{8,4},{12,8},{16,12},{20,16},{24,20},{28,24},{32,28},{36,32}... | collective-permute-start | bytes 393224 | tf_op jit(solution)/shard_map/ppermute | solution.py:18
  32.5 4.2 %collective-permute-done.1 = bf16[256,256]{1,0:T(8,128)(2,1)S(1)} collective-permute-done((bf16[256,256]{1,0:T(8,128)(2,1)S(1)}, bf16[256,256]{1,0:T(8,128)(2,1)S(1)}, u32[]{:S(2)}, u32[]{:S(2)}) %collective-permute-start.1) | collective-permute-done | bytes 131104 | tf_op jit(solution)/shard_map/ppermute | solution.py:18
  36.7 6.3 %collective-permute-start.3 = (bf16[256,256]{1,0:T(8,128)(2,1)S(1)}, bf16[256,256]{1,0:T(8,128)(2,1)S(1)}, u32[]{:S(2)}, u32[]{:S(2)}) collective-permute-start(bf16[256,256]{1,0:T(8,128)(2,1)S(1)} %constant_dynamic-update-slice_fusion), channel_id=1, source_target_pairs={{0,32},{4,36},{8,40},{12,44},{16,48},{20,52},{24,56},{28,60},{32,6... | collective-permute-start | bytes 393224 | tf_op jit(solution)/shard_map/ppermute | solution.py:26
  43.0 7.2 %collective-permute-start.4 = (bf16[256,256]{1,0:T(8,128)(2,1)S(1)}, bf16[256,256]{1,0:T(8,128)(2,1)S(1)}, u32[]{:S(2)}, u32[]{:S(2)}) collective-permute-start(bf16[256,256]{1,0:T(8,128)(2,1)S(1)} %constant_dynamic-update-slice_fusion), channel_id=1, source_target_pairs={{0,256},{4,260},{8,264},{12,268},{16,272},{20,276},{24,280},{28,28... | collective-permute-start | bytes 393224 | tf_op jit(solution)/shard_map/ppermute | solution.py:94
  52.7 3.7 %collective-permute-start.6 = (bf16[256,256]{1,0:T(8,128)(2,1)S(1)}, bf16[256,256]{1,0:T(8,128)(2,1)S(1)}, u32[]{:S(2)}, u32[]{:S(2)}) collective-permute-start(bf16[256,256]{1,0:T(8,128)(2,1)S(1)} %constant_dynamic-update-slice_fusion), channel_id=1, source_target_pairs={{0,16},{4,20},{8,24},{12,28},{16,32},{20,36},{24,40},{28,44},{32,4... | collective-permute-start | bytes 393224 | tf_op jit(solution)/shard_map/ppermute | solution.py:26
  58.6 12.6 %collective-permute-start.8 = (bf16[256,256]{1,0:T(8,128)(2,1)S(1)}, bf16[256,256]{1,0:T(8,128)(2,1)S(1)}, u32[]{:S(2)}, u32[]{:S(2)}) collective-permute-start(bf16[256,256]{1,0:T(8,128)(2,1)S(1)} %constant_dynamic-update-slice_fusion), channel_id=1, source_target_pairs={{0,128},{4,132},{8,136},{12,140},{16,144},{20,148},{24,152},{28,15... | collective-permute-start | bytes 393224 | tf_op jit(solution)/shard_map/ppermute | solution.py:26
  73.2 5.9 %collective-permute-start.10 = (bf16[256,256]{1,0:T(8,128)(2,1)S(1)}, bf16[256,256]{1,0:T(8,128)(2,1)S(1)}, u32[]{:S(2)}, u32[]{:S(2)}) collective-permute-start(bf16[256,256]{1,0:T(8,128)(2,1)S(1)} %constant_dynamic-update-slice_fusion), channel_id=1, source_target_pairs={{0,12},{4,16},{8,20},{12,24},{16,28},{20,32},{24,36},{28,40},{32,4... | collective-permute-start | bytes 393224 | tf_op jit(solution)/shard_map/ppermute | solution.py:26
  79.1 3.8 %collective-permute-done.9 = bf16[256,256]{1,0:T(8,128)(2,1)S(1)} collective-permute-done((bf16[256,256]{1,0:T(8,128)(2,1)S(1)}, bf16[256,256]{1,0:T(8,128)(2,1)S(1)}, u32[]{:S(2)}, u32[]{:S(2)}) %collective-permute-start.9) | collective-permute-done | bytes 131104 | tf_op jit(solution)/shard_map/ppermute | solution.py:26
  84.3 4.6 %collective-permute-done.11 = bf16[256,256]{1,0:T(8,128)(2,1)S(1)} collective-permute-done((bf16[256,256]{1,0:T(8,128)(2,1)S(1)}, bf16[256,256]{1,0:T(8,128)(2,1)S(1)}, u32[]{:S(2)}, u32[]{:S(2)}) %collective-permute-start.11) | collective-permute-done | bytes 131104 | tf_op jit(solution)/shard_map/ppermute | solution.py:26
  89.0 3.3 %fusion.36 = (f32[256]{0:T(256)S(1)}, f32[256,4096]{0,1:T(8,128)S(1)}) fusion(bf16[256,128]{1,0:T(8,128)(2,1)S(1)} %copy-done.3, bf16[4096,256]{1,0:T(8,128)(2,1)S(1)} %constant_dynamic-update-slice_fusion.2, pred[256,3328]{0,1:T(32,128)(4,1)S(1)} %bitcast.21, pred[4096]{0:T(1024)(128)(4,1)S(1)} %pad.4.clone), kind=kOutput, calls=%fused_computation.93 | convolution fusion | flops 272629504 | bytes 6165504 | tf_op jit(solution)/shard_map/dot_general | solution.py:54
  97.7 5.1 %collective-permute-start.17 = (bf16[256,256]{0,1:T(8,128)(2,1)S(1)}, bf16[256,256]{0,1:T(8,128)(2,1)S(1)}, u32[]{:S(2)}, u32[]{:S(2)}) collective-permute-start(bf16[256,256]{0,1:T(8,128)(2,1)S(1)} %get-tuple-element.18), channel_id=1, source_target_pairs={{0,32},{4,36},{8,40},{12,44},{16,48},{20,52},{24,56},{28,60},{32,6... | collective-permute-start | bytes 393224 | tf_op jit(solution)/shard_map/ppermute | solution.py:26
  104.1 4.0 %collective-permute-start.28 = (bf16[256,256]{0,1:T(8,128)(2,1)S(1)}, bf16[256,256]{0,1:T(8,128)(2,1)S(1)}, u32[]{:S(2)}, u32[]{:S(2)}) collective-permute-start(bf16[256,256]{0,1:T(8,128)(2,1)S(1)} %get-tuple-element.20), channel_id=1, source_target_pairs={{0,8},{4,12},{8,16},{12,20},{16,24},{20,28},{24,32},{28,36},{32,40... | collective-permute-start | bytes 393224 | tf_op jit(solution)/shard_map/ppermute | solution.py:26
  109.4 4.9 %collective-permute-start.26 = (bf16[256,256]{0,1:T(8,128)(2,1)S(1)}, bf16[256,256]{0,1:T(8,128)(2,1)S(1)}, u32[]{:S(2)}, u32[]{:S(2)}) collective-permute-start(bf16[256,256]{0,1:T(8,128)(2,1)S(1)} %get-tuple-element.22), channel_id=1, source_target_pairs={{0,64},{4,68},{8,72},{12,76},{16,80},{20,84},{24,88},{28,92},{32,9... | collective-permute-start | bytes 393224 | tf_op jit(solution)/shard_map/ppermute | solution.py:26
  116.0 6.9 %collective-permute-start.24 = (bf16[256,256]{0,1:T(8,128)(2,1)S(1)}, bf16[256,256]{0,1:T(8,128)(2,1)S(1)}, u32[]{:S(2)}, u32[]{:S(2)}) collective-permute-start(bf16[256,256]{0,1:T(8,128)(2,1)S(1)} %get-tuple-element.24), channel_id=1, source_target_pairs={{0,12},{4,16},{8,20},{12,24},{16,28},{20,32},{24,36},{28,40},{32,4... | collective-permute-start | bytes 393224 | tf_op jit(solution)/shard_map/ppermute | solution.py:26
  124.2 8.8 %collective-permute-start.22 = (bf16[256,256]{0,1:T(8,128)(2,1)S(1)}, bf16[256,256]{0,1:T(8,128)(2,1)S(1)}, u32[]{:S(2)}, u32[]{:S(2)}) collective-permute-start(bf16[256,256]{0,1:T(8,128)(2,1)S(1)} %get-tuple-element.26), channel_id=1, source_target_pairs={{0,128},{4,132},{8,136},{12,140},{16,144},{20,148},{24,152},{28,15... | collective-permute-start | bytes 393224 | tf_op jit(solution)/shard_map/ppermute | solution.py:26
  134.3 4.9 %collective-permute-start.20 = (bf16[256,256]{0,1:T(8,128)(2,1)}, bf16[256,256]{0,1:T(8,128)(2,1)S(1)}, u32[]{:S(2)}, u32[]{:S(2)}) collective-permute-start(bf16[256,256]{0,1:T(8,128)(2,1)} %get-tuple-element.28), channel_id=1, source_target_pairs={{0,16},{4,20},{8,24},{12,28},{16,32},{20,36},{24,40},{28,44},{32,4... | collective-permute-start | bytes 393224 | tf_op jit(solution)/shard_map/ppermute | solution.py:26
  139.2 10.2 %collective-permute-start.19 = (bf16[256,256]{0,1:T(8,128)(2,1)S(1)}, bf16[256,256]{0,1:T(8,128)(2,1)S(1)}, u32[]{:S(2)}, u32[]{:S(2)}) collective-permute-start(bf16[256,256]{0,1:T(8,128)(2,1)S(1)} %get-tuple-element.29), channel_id=1, source_target_pairs={{0,256},{4,260},{8,264},{12,268},{16,272},{20,276},{24,280},{28,28... | collective-permute-start | bytes 393224 | tf_op jit(solution)/shard_map/ppermute | solution.py:135
  150.8 1.9 %collective-permute-start.15 = (bf16[256,256]{0,1:T(8,128)(2,1)S(1)}, bf16[256,256]{0,1:T(8,128)(2,1)S(1)}, u32[]{:S(2)}, u32[]{:S(2)}) collective-permute-start(bf16[256,256]{0,1:T(8,128)(2,1)S(1)} %get-tuple-element.31), channel_id=1, source_target_pairs={{4,0},{8,4},{12,8},{16,12},{20,16},{24,20},{28,24},{32,28},{36,32}... | collective-permute-start | bytes 393224 | tf_op jit(solution)/shard_map/ppermute | solution.py:26
  152.7 7.3 %collective-permute-start.16 = (bf16[256,256]{0,1:T(8,128)(2,1)S(1)}, bf16[256,256]{0,1:T(8,128)(2,1)S(1)}, u32[]{:S(2)}, u32[]{:S(2)}) collective-permute-start(bf16[256,256]{0,1:T(8,128)(2,1)S(1)} %get-tuple-element.32), channel_id=1, source_target_pairs={{0,4},{4,8},{8,12},{12,16},{16,20},{20,24},{24,28},{28,32},{32,36}... | collective-permute-start | bytes 393224 | tf_op jit(solution)/shard_map/ppermute | solution.py:26
  160.0 1.4 convolution_multiply_fusion.3
  (103 shorter events, 33.3 us)
Async XLA Ops:
  2.4 86.6 %collective-permute-start.14 = (bf16[256,256]{1,0:T(8,128)(2,1)S(1)}, bf16[256,256]{1,0:T(8,128)(2,1)S(1)}, u32[]{:S(2)}, u32[]{:S(2)}) collective-permute-start(bf16[256,256]{1,0:T(8,128)(2,1)S(1)} %constant_dynamic-update-slice_fusion), channel_id=1, source_target_pairs={{0,8},{4,12},{8,16},{12,20},{16,24},{20,28},{24,32},{28,36},{32,40... | collective-permute-start | bytes 393224 | tf_op jit(solution)/shard_map/ppermute | solution.py:26
  7.3 81.7 %collective-permute-start.13 = (bf16[256,256]{1,0:T(8,128)(2,1)S(1)}, bf16[256,256]{1,0:T(8,128)(2,1)S(1)}, u32[]{:S(2)}, u32[]{:S(2)}) collective-permute-start(bf16[256,256]{1,0:T(8,128)(2,1)S(1)} %constant_dynamic-update-slice_fusion), channel_id=1, source_target_pairs={{8,0},{12,4},{16,8},{20,12},{24,16},{28,20},{32,24},{36,28},{40,32... | collective-permute-start | bytes 393224 | tf_op jit(solution)/shard_map/ppermute | solution.py:26
  8.6 80.4 %collective-permute-start.12 = (bf16[256,256]{1,0:T(8,128)(2,1)S(1)}, bf16[256,256]{1,0:T(8,128)(2,1)S(1)}, u32[]{:S(2)}, u32[]{:S(2)}) collective-permute-start(bf16[256,256]{1,0:T(8,128)(2,1)S(1)} %constant_dynamic-update-slice_fusion), channel_id=1, source_target_pairs={{0,64},{4,68},{8,72},{12,76},{16,80},{20,84},{24,88},{28,92},{32,9... | collective-permute-start | bytes 393224 | tf_op jit(solution)/shard_map/ppermute | solution.py:26
  18.9 24.0 %collective-permute-start.2 = (bf16[256,256]{1,0:T(8,128)(2,1)S(1)}, bf16[256,256]{1,0:T(8,128)(2,1)S(1)}, u32[]{:S(2)}, u32[]{:S(2)}) collective-permute-start(bf16[256,256]{1,0:T(8,128)(2,1)S(1)} %constant_dynamic-update-slice_fusion), channel_id=1, source_target_pairs={{32,0},{36,4},{40,8},{44,12},{48,16},{52,20},{56,24},{60,28},{64,3... | collective-permute-start | bytes 393224 | tf_op jit(solution)/shard_map/ppermute | solution.py:26
  36.7 13.5 %collective-permute-start.3 = (bf16[256,256]{1,0:T(8,128)(2,1)S(1)}, bf16[256,256]{1,0:T(8,128)(2,1)S(1)}, u32[]{:S(2)}, u32[]{:S(2)}) collective-permute-start(bf16[256,256]{1,0:T(8,128)(2,1)S(1)} %constant_dynamic-update-slice_fusion), channel_id=1, source_target_pairs={{0,32},{4,36},{8,40},{12,44},{16,48},{20,52},{24,56},{28,60},{32,6... | collective-permute-start | bytes 393224 | tf_op jit(solution)/shard_map/ppermute | solution.py:26
  43.0 9.7 %collective-permute-start.4 = (bf16[256,256]{1,0:T(8,128)(2,1)S(1)}, bf16[256,256]{1,0:T(8,128)(2,1)S(1)}, u32[]{:S(2)}, u32[]{:S(2)}) collective-permute-start(bf16[256,256]{1,0:T(8,128)(2,1)S(1)} %constant_dynamic-update-slice_fusion), channel_id=1, source_target_pairs={{0,256},{4,260},{8,264},{12,268},{16,272},{20,276},{24,280},{28,28... | collective-permute-start | bytes 393224 | tf_op jit(solution)/shard_map/ppermute | solution.py:94
  57.3 14.0 %collective-permute-start.7 = (bf16[256,256]{1,0:T(8,128)(2,1)S(1)}, bf16[256,256]{1,0:T(8,128)(2,1)S(1)}, u32[]{:S(2)}, u32[]{:S(2)}) collective-permute-start(bf16[256,256]{1,0:T(8,128)(2,1)S(1)} %constant_dynamic-update-slice_fusion), channel_id=1, source_target_pairs={{128,0},{132,4},{136,8},{140,12},{144,16},{148,20},{152,24},{156,2... | collective-permute-start | bytes 393224 | tf_op jit(solution)/shard_map/ppermute | solution.py:26
  58.6 14.6 %collective-permute-start.8 = (bf16[256,256]{1,0:T(8,128)(2,1)S(1)}, bf16[256,256]{1,0:T(8,128)(2,1)S(1)}, u32[]{:S(2)}, u32[]{:S(2)}) collective-permute-start(bf16[256,256]{1,0:T(8,128)(2,1)S(1)} %constant_dynamic-update-slice_fusion), channel_id=1, source_target_pairs={{0,128},{4,132},{8,136},{12,140},{16,144},{20,148},{24,152},{28,15... | collective-permute-start | bytes 393224 | tf_op jit(solution)/shard_map/ppermute | solution.py:26
  71.3 11.7 %collective-permute-start.9 = (bf16[256,256]{1,0:T(8,128)(2,1)S(1)}, bf16[256,256]{1,0:T(8,128)(2,1)S(1)}, u32[]{:S(2)}, u32[]{:S(2)}) collective-permute-start(bf16[256,256]{1,0:T(8,128)(2,1)S(1)} %constant_dynamic-update-slice_fusion), channel_id=1, source_target_pairs={{12,0},{16,4},{20,8},{24,12},{28,16},{32,20},{36,24},{40,28},{44,3... | collective-permute-start | bytes 393224 | tf_op jit(solution)/shard_map/ppermute | solution.py:26
  73.2 11.1 %collective-permute-start.10 = (bf16[256,256]{1,0:T(8,128)(2,1)S(1)}, bf16[256,256]{1,0:T(8,128)(2,1)S(1)}, u32[]{:S(2)}, u32[]{:S(2)}) collective-permute-start(bf16[256,256]{1,0:T(8,128)(2,1)S(1)} %constant_dynamic-update-slice_fusion), channel_id=1, source_target_pairs={{0,12},{4,16},{8,20},{12,24},{16,28},{20,32},{24,36},{28,40},{32,4... | collective-permute-start | bytes 393224 | tf_op jit(solution)/shard_map/ppermute | solution.py:26
  97.7 16.9 %collective-permute-start.17 = (bf16[256,256]{0,1:T(8,128)(2,1)S(1)}, bf16[256,256]{0,1:T(8,128)(2,1)S(1)}, u32[]{:S(2)}, u32[]{:S(2)}) collective-permute-start(bf16[256,256]{0,1:T(8,128)(2,1)S(1)} %get-tuple-element.18), channel_id=1, source_target_pairs={{0,32},{4,36},{8,40},{12,44},{16,48},{20,52},{24,56},{28,60},{32,6... | collective-permute-start | bytes 393224 | tf_op jit(solution)/shard_map/ppermute | solution.py:26
  102.8 13.1 %collective-permute-start.29 = (bf16[256,256]{0,1:T(8,128)(2,1)S(1)}, bf16[256,256]{0,1:T(8,128)(2,1)S(1)}, u32[]{:S(2)}, u32[]{:S(2)}) collective-permute-start(bf16[256,256]{0,1:T(8,128)(2,1)S(1)} %get-tuple-element.19), channel_id=1, source_target_pairs={{8,0},{12,4},{16,8},{20,12},{24,16},{28,20},{32,24},{36,28},{40,32... | collective-permute-start | bytes 393224 | tf_op jit(solution)/shard_map/ppermute | solution.py:26
  104.1 18.7 %collective-permute-start.28 = (bf16[256,256]{0,1:T(8,128)(2,1)S(1)}, bf16[256,256]{0,1:T(8,128)(2,1)S(1)}, u32[]{:S(2)}, u32[]{:S(2)}) collective-permute-start(bf16[256,256]{0,1:T(8,128)(2,1)S(1)} %get-tuple-element.20), channel_id=1, source_target_pairs={{0,8},{4,12},{8,16},{12,20},{16,24},{20,28},{24,32},{28,36},{32,40... | collective-permute-start | bytes 393224 | tf_op jit(solution)/shard_map/ppermute | solution.py:26
  108.1 16.0 %collective-permute-start.27 = (bf16[256,256]{0,1:T(8,128)(2,1)S(1)}, bf16[256,256]{0,1:T(8,128)(2,1)S(1)}, u32[]{:S(2)}, u32[]{:S(2)}) collective-permute-start(bf16[256,256]{0,1:T(8,128)(2,1)S(1)} %get-tuple-element.21), channel_id=1, source_target_pairs={{64,0},{68,4},{72,8},{76,12},{80,16},{84,20},{88,24},{92,28},{96,3... | collective-permute-start | bytes 393224 | tf_op jit(solution)/shard_map/ppermute | solution.py:26
  109.4 23.6 %collective-permute-start.26 = (bf16[256,256]{0,1:T(8,128)(2,1)S(1)}, bf16[256,256]{0,1:T(8,128)(2,1)S(1)}, u32[]{:S(2)}, u32[]{:S(2)}) collective-permute-start(bf16[256,256]{0,1:T(8,128)(2,1)S(1)} %get-tuple-element.22), channel_id=1, source_target_pairs={{0,64},{4,68},{8,72},{12,76},{16,80},{20,84},{24,88},{28,92},{32,9... | collective-permute-start | bytes 393224 | tf_op jit(solution)/shard_map/ppermute | solution.py:26
  114.7 19.7 %collective-permute-start.25 = (bf16[256,256]{0,1:T(8,128)(2,1)S(1)}, bf16[256,256]{0,1:T(8,128)(2,1)S(1)}, u32[]{:S(2)}, u32[]{:S(2)}) collective-permute-start(bf16[256,256]{0,1:T(8,128)(2,1)S(1)} %get-tuple-element.23), channel_id=1, source_target_pairs={{12,0},{16,4},{20,8},{24,12},{28,16},{32,20},{36,24},{40,28},{44,3... | collective-permute-start | bytes 393224 | tf_op jit(solution)/shard_map/ppermute | solution.py:26
  116.0 23.3 %collective-permute-start.24 = (bf16[256,256]{0,1:T(8,128)(2,1)S(1)}, bf16[256,256]{0,1:T(8,128)(2,1)S(1)}, u32[]{:S(2)}, u32[]{:S(2)}) collective-permute-start(bf16[256,256]{0,1:T(8,128)(2,1)S(1)} %get-tuple-element.24), channel_id=1, source_target_pairs={{0,12},{4,16},{8,20},{12,24},{16,28},{20,32},{24,36},{28,40},{32,4... | collective-permute-start | bytes 393224 | tf_op jit(solution)/shard_map/ppermute | solution.py:26
  122.9 26.6 %collective-permute-start.23 = (bf16[256,256]{0,1:T(8,128)(2,1)S(1)}, bf16[256,256]{0,1:T(8,128)(2,1)S(1)}, u32[]{:S(2)}, u32[]{:S(2)}) collective-permute-start(bf16[256,256]{0,1:T(8,128)(2,1)S(1)} %get-tuple-element.25), channel_id=1, source_target_pairs={{128,0},{132,4},{136,8},{140,12},{144,16},{148,20},{152,24},{156,2... | collective-permute-start | bytes 393224 | tf_op jit(solution)/shard_map/ppermute | solution.py:26
  124.2 26.6 %collective-permute-start.22 = (bf16[256,256]{0,1:T(8,128)(2,1)S(1)}, bf16[256,256]{0,1:T(8,128)(2,1)S(1)}, u32[]{:S(2)}, u32[]{:S(2)}) collective-permute-start(bf16[256,256]{0,1:T(8,128)(2,1)S(1)} %get-tuple-element.26), channel_id=1, source_target_pairs={{0,128},{4,132},{8,136},{12,140},{16,144},{20,148},{24,152},{28,15... | collective-permute-start | bytes 393224 | tf_op jit(solution)/shard_map/ppermute | solution.py:26
  133.0 19.7 %collective-permute-start.21 = (bf16[256,256]{0,1:T(8,128)(2,1)S(1)}, bf16[256,256]{0,1:T(8,128)(2,1)S(1)}, u32[]{:S(2)}, u32[]{:S(2)}) collective-permute-start(bf16[256,256]{0,1:T(8,128)(2,1)S(1)} %get-tuple-element.27), channel_id=1, source_target_pairs={{16,0},{20,4},{24,8},{28,12},{32,16},{36,20},{40,24},{44,28},{48,3... | collective-permute-start | bytes 393224 | tf_op jit(solution)/shard_map/ppermute | solution.py:26
  134.3 27.9 %collective-permute-start.20 = (bf16[256,256]{0,1:T(8,128)(2,1)}, bf16[256,256]{0,1:T(8,128)(2,1)S(1)}, u32[]{:S(2)}, u32[]{:S(2)}) collective-permute-start(bf16[256,256]{0,1:T(8,128)(2,1)} %get-tuple-element.28), channel_id=1, source_target_pairs={{0,16},{4,20},{8,24},{12,28},{16,32},{20,36},{24,40},{28,44},{32,4... | collective-permute-start | bytes 393224 | tf_op jit(solution)/shard_map/ppermute | solution.py:26
  139.2 23.0 %collective-permute-start.19 = (bf16[256,256]{0,1:T(8,128)(2,1)S(1)}, bf16[256,256]{0,1:T(8,128)(2,1)S(1)}, u32[]{:S(2)}, u32[]{:S(2)}) collective-permute-start(bf16[256,256]{0,1:T(8,128)(2,1)S(1)} %get-tuple-element.29), channel_id=1, source_target_pairs={{0,256},{4,260},{8,264},{12,268},{16,272},{20,276},{24,280},{28,28... | collective-permute-start | bytes 393224 | tf_op jit(solution)/shard_map/ppermute | solution.py:135
  149.5 12.8 %collective-permute-start.18 = (bf16[256,256]{0,1:T(8,128)(2,1)S(1)}, bf16[256,256]{0,1:T(8,128)(2,1)S(1)}, u32[]{:S(2)}, u32[]{:S(2)}) collective-permute-start(bf16[256,256]{0,1:T(8,128)(2,1)S(1)} %get-tuple-element.30), channel_id=1, source_target_pairs={{32,0},{36,4},{40,8},{44,12},{48,16},{52,20},{56,24},{60,28},{64,3... | collective-permute-start | bytes 393224 | tf_op jit(solution)/shard_map/ppermute | solution.py:26
  150.8 11.5 %collective-permute-start.15 = (bf16[256,256]{0,1:T(8,128)(2,1)S(1)}, bf16[256,256]{0,1:T(8,128)(2,1)S(1)}, u32[]{:S(2)}, u32[]{:S(2)}) collective-permute-start(bf16[256,256]{0,1:T(8,128)(2,1)S(1)} %get-tuple-element.31), channel_id=1, source_target_pairs={{4,0},{8,4},{12,8},{16,12},{20,16},{24,20},{28,24},{32,28},{36,32}... | collective-permute-start | bytes 393224 | tf_op jit(solution)/shard_map/ppermute | solution.py:26
  (10 other events, 161.8 us)

commit v9 on v8

--- a/solution.py
+++ b/solution.py
@@ -88,7 +88,7 @@
     near_ok = (neighbour >= 0) & (neighbour < frame_count)
     pieces = [near_keys]
     half = frame_count // 2
-    offsets = [o for o in (8, -8, half, 4, -4, 32, -32, 3, -3, 16, -16, 2, -2) if o in offsets]
+    offsets = [o for o in (8, half, -8, 32, 4, -32, -4, 16, 3, -16, -3, 2, -2) if o in offsets]
     for offset in offsets:
         if offset == half:
             arrived = lax.ppermute(

time: 166 us -> 166 us (level)
  waiting for transfers between devices: 18.5 us -> 21.1 us
    ppermute x26, starting transfers between devices: 103 us -> 93.5 us  [from_behind(): lax.ppermute(value, axis, [(source, source + steps) for source in range(l...]
    ppermute x26, waiting for transfers between devices: 9.86 us -> 14.6 us  [from_behind(): lax.ppermute(value, axis, [(source, source + steps) for source in range(l...]
    ppermute x1, starting transfers between devices: 7.2 us -> 11.8 us  [shards(): lax.ppermute(joined, 'seq', [(src, (src + half) % frame_count) for src in...]
    ppermute x1, waiting for transfers between devices: 3.25 us -> 0.01 us  [extended(): before = lax.ppermute(last, axis, up)]
    ppermute x1, starting transfers between devices: 10.2 us -> 13 us  [shards(): lax.ppermute(grad_piece, 'seq', [(src, (src + half) % frame_count) for sr...]
    ppermute x1, waiting for transfers between devices: 4.19 us -> 6.43 us  [extended(): after = lax.ppermute(leading, axis, down)]
  transfers between devices with their start and end apart: 30 -> 30, of which waited for: 7 -> 6; matrix products, arithmetic and copies ran while one was open for 5% -> 5% of each run, Pallas kernels for 0% -> 0%
where the time goes in v9:
time: 166 us; the launch traced here: 165 us
  starting transfers between devices  123 us (74%)
  waiting for transfers between devices  21.1 us (13%)
  local copies, waits for them, and re-layouts  8.93 us (5%)
  matrix products  8 us (5%)
  other arithmetic  3.02 us (2%)
    ppermute x26, starting transfers between devices, from_behind(): lax.ppermute(value, axis, [(source, source + steps) for source in range(l...  93.5 us
    ppermute x26, waiting for transfers between devices, from_behind(): lax.ppermute(value, axis, [(source, source + steps) for source in range(l...  14.6 us
    ppermute x1, starting transfers between devices, shards(): lax.ppermute(grad_piece, 'seq', [(src, (src + half) % frame_count) for sr...  13 us
    ppermute x1, starting transfers between devices, shards(): lax.ppermute(joined, 'seq', [(src, (src + half) % frame_count) for src in...  11.8 us
    ppermute x1, waiting for transfers between devices, extended(): after = lax.ppermute(leading, axis, down)  6.43 us
    unnamed x29, local copies, waits for them, and re-layouts  5.43 us
  transfers between devices with their start and end apart: 30, of which 6 were waited for; matrix products, arithmetic and copies ran while one was open for 5% of the time, Pallas kernels for 0%

profile of v9, /device:TPU:1, one launch (start us, length us, event | category | flops | bytes accessed | tf_op | source)
XLA Modules:
  0.0 165.1 jit_solution(3286981230973637307)
XLA Ops:
  2.4 4.8 %collective-permute-start.14 = (bf16[256,256]{1,0:T(8,128)(2,1)S(1)}, bf16[256,256]{1,0:T(8,128)(2,1)S(1)}, u32[]{:S(2)}, u32[]{:S(2)}) collective-permute-start(bf16[256,256]{1,0:T(8,128)(2,1)S(1)} %constant_dynamic-update-slice_fusion), channel_id=1, source_target_pairs={{0,8},{4,12},{8,16},{12,20},{16,24},{20,28},{24,32},{28,36},{32,40... | collective-permute-start | bytes 393224 | tf_op jit(solution)/shard_map/ppermute | solution.py:26
  8.6 7.3 %collective-permute-start.12 = (bf16[256,256]{1,0:T(8,128)(2,1)S(1)}, bf16[256,256]{1,0:T(8,128)(2,1)S(1)}, u32[]{:S(2)}, u32[]{:S(2)}) collective-permute-start(bf16[256,256]{1,0:T(8,128)(2,1)S(1)} %constant_dynamic-update-slice_fusion), channel_id=1, source_target_pairs={{0,12},{4,16},{8,20},{12,24},{16,28},{20,32},{24,36},{28,40},{32,4... | collective-permute-start | bytes 393224 | tf_op jit(solution)/shard_map/ppermute | solution.py:26
  17.1 1.9 %collective-permute-start = (bf16[256,256]{1,0:T(8,128)(2,1)S(1)}, bf16[256,256]{1,0:T(8,128)(2,1)S(1)}, u32[]{:S(2)}, u32[]{:S(2)}) collective-permute-start(bf16[256,256]{1,0:T(8,128)(2,1)S(1)} %constant_dynamic-update-slice_fusion), channel_id=1, source_target_pairs={{0,4},{4,8},{8,12},{12,16},{16,20},{20,24},{24,28},{28,32},{32,36}... | collective-permute-start | bytes 393224 | tf_op jit(solution)/shard_map/ppermute | solution.py:17
  23.3 2.4 %collective-permute-start.1 = (bf16[256,256]{1,0:T(8,128)(2,1)S(1)}, bf16[256,256]{1,0:T(8,128)(2,1)S(1)}, u32[]{:S(2)}, u32[]{:S(2)}) collective-permute-start(bf16[256,256]{1,0:T(8,128)(2,1)S(1)} %constant_dynamic-update-slice_fusion), channel_id=1, source_target_pairs={{4,0},{8,4},{12,8},{16,12},{20,16},{24,20},{28,24},{32,28},{36,32}... | collective-permute-start | bytes 393224 | tf_op jit(solution)/shard_map/ppermute | solution.py:18
  26.6 6.4 %collective-permute-done.1 = bf16[256,256]{1,0:T(8,128)(2,1)S(1)} collective-permute-done((bf16[256,256]{1,0:T(8,128)(2,1)S(1)}, bf16[256,256]{1,0:T(8,128)(2,1)S(1)}, u32[]{:S(2)}, u32[]{:S(2)}) %collective-permute-start.1) | collective-permute-done | bytes 131104 | tf_op jit(solution)/shard_map/ppermute | solution.py:18
  33.1 11.8 %collective-permute-start.3 = (bf16[256,256]{1,0:T(8,128)(2,1)S(1)}, bf16[256,256]{1,0:T(8,128)(2,1)S(1)}, u32[]{:S(2)}, u32[]{:S(2)}) collective-permute-start(bf16[256,256]{1,0:T(8,128)(2,1)S(1)} %constant_dynamic-update-slice_fusion), channel_id=1, source_target_pairs={{0,256},{4,260},{8,264},{12,268},{16,272},{20,276},{24,280},{28,28... | collective-permute-start | bytes 393224 | tf_op jit(solution)/shard_map/ppermute | solution.py:94
  44.9 5.4 %collective-permute-start.4 = (bf16[256,256]{1,0:T(8,128)(2,1)S(1)}, bf16[256,256]{1,0:T(8,128)(2,1)S(1)}, u32[]{:S(2)}, u32[]{:S(2)}) collective-permute-start(bf16[256,256]{1,0:T(8,128)(2,1)S(1)} %constant_dynamic-update-slice_fusion), channel_id=1, source_target_pairs={{0,32},{4,36},{8,40},{12,44},{16,48},{20,52},{24,56},{28,60},{32,6... | collective-permute-start | bytes 393224 | tf_op jit(solution)/shard_map/ppermute | solution.py:26
  53.6 4.5 %collective-permute-done.5 = bf16[256,256]{1,0:T(8,128)(2,1)S(1)} collective-permute-done((bf16[256,256]{1,0:T(8,128)(2,1)S(1)}, bf16[256,256]{1,0:T(8,128)(2,1)S(1)}, u32[]{:S(2)}, u32[]{:S(2)}) %collective-permute-start.5) | collective-permute-done | bytes 131104 | tf_op jit(solution)/shard_map/ppermute | solution.py:26
  58.0 8.1 %collective-permute-start.7 = (bf16[256,256]{1,0:T(8,128)(2,1)S(1)}, bf16[256,256]{1,0:T(8,128)(2,1)S(1)}, u32[]{:S(2)}, u32[]{:S(2)}) collective-permute-start(bf16[256,256]{1,0:T(8,128)(2,1)S(1)} %constant_dynamic-update-slice_fusion), channel_id=1, source_target_pairs={{0,128},{4,132},{8,136},{12,140},{16,144},{20,148},{24,152},{28,15... | collective-permute-start | bytes 393224 | tf_op jit(solution)/shard_map/ppermute | solution.py:26
  66.2 3.4 %collective-permute-start.8 = (bf16[256,256]{1,0:T(8,128)(2,1)S(1)}, bf16[256,256]{1,0:T(8,128)(2,1)S(1)}, u32[]{:S(2)}, u32[]{:S(2)}) collective-permute-start(bf16[256,256]{1,0:T(8,128)(2,1)S(1)} %constant_dynamic-update-slice_fusion), channel_id=1, source_target_pairs={{0,16},{4,20},{8,24},{12,28},{16,32},{20,36},{24,40},{28,44},{32,4... | collective-permute-start | bytes 393224 | tf_op jit(solution)/shard_map/ppermute | solution.py:26
  72.9 7.1 %collective-permute-done.9 = bf16[256,256]{1,0:T(8,128)(2,1)S(1)} collective-permute-done((bf16[256,256]{1,0:T(8,128)(2,1)S(1)}, bf16[256,256]{1,0:T(8,128)(2,1)S(1)}, u32[]{:S(2)}, u32[]{:S(2)}) %collective-permute-start.9) | collective-permute-done | bytes 131104 | tf_op jit(solution)/shard_map/ppermute | solution.py:26
  80.0 6.7 %collective-permute-start.11 = (bf16[256,256]{1,0:T(8,128)(2,1)S(1)}, bf16[256,256]{1,0:T(8,128)(2,1)S(1)}, u32[]{:S(2)}, u32[]{:S(2)}) collective-permute-start(bf16[256,256]{1,0:T(8,128)(2,1)S(1)} %constant_dynamic-update-slice_fusion), channel_id=1, source_target_pairs={{0,64},{4,68},{8,72},{12,76},{16,80},{20,84},{24,88},{28,92},{32,9... | collective-permute-start | bytes 393224 | tf_op jit(solution)/shard_map/ppermute | solution.py:26
  86.7 1.9 %collective-permute-done.11 = bf16[256,256]{1,0:T(8,128)(2,1)S(1)} collective-permute-done((bf16[256,256]{1,0:T(8,128)(2,1)S(1)}, bf16[256,256]{1,0:T(8,128)(2,1)S(1)}, u32[]{:S(2)}, u32[]{:S(2)}) %collective-permute-start.11) | collective-permute-done | bytes 131104 | tf_op jit(solution)/shard_map/ppermute | solution.py:26
  88.7 3.3 %fusion.36 = (f32[256]{0:T(256)S(1)}, f32[256,4096]{0,1:T(8,128)S(1)}) fusion(bf16[256,128]{1,0:T(8,128)(2,1)S(1)} %copy-done.3, bf16[4096,256]{1,0:T(8,128)(2,1)S(1)} %constant_dynamic-update-slice_fusion.2, pred[256,3328]{0,1:T(32,128)(4,1)S(1)} %bitcast.21, pred[4096]{0:T(1024)(128)(4,1)S(1)} %pad.4.clone), kind=kOutput, calls=%fused_computation.93 | convolution fusion | flops 272629504 | bytes 6165504 | tf_op jit(solution)/shard_map/dot_general | solution.py:54
  97.4 7.2 %collective-permute-start.17 = (bf16[256,256]{0,1:T(8,128)(2,1)S(1)}, bf16[256,256]{0,1:T(8,128)(2,1)S(1)}, u32[]{:S(2)}, u32[]{:S(2)}) collective-permute-start(bf16[256,256]{0,1:T(8,128)(2,1)S(1)} %get-tuple-element.18), channel_id=1, source_target_pairs={{0,32},{4,36},{8,40},{12,44},{16,48},{20,52},{24,56},{28,60},{32,6... | collective-permute-start | bytes 393224 | tf_op jit(solution)/shard_map/ppermute | solution.py:26
  106.0 4.0 %collective-permute-start.28 = (bf16[256,256]{0,1:T(8,128)(2,1)S(1)}, bf16[256,256]{0,1:T(8,128)(2,1)S(1)}, u32[]{:S(2)}, u32[]{:S(2)}) collective-permute-start(bf16[256,256]{0,1:T(8,128)(2,1)S(1)} %get-tuple-element.20), channel_id=1, source_target_pairs={{0,8},{4,12},{8,16},{12,20},{16,24},{20,28},{24,32},{28,36},{32,40... | collective-permute-start | bytes 393224 | tf_op jit(solution)/shard_map/ppermute | solution.py:26
  112.9 5.2 %collective-permute-start.25 = (bf16[256,256]{0,1:T(8,128)(2,1)S(1)}, bf16[256,256]{0,1:T(8,128)(2,1)S(1)}, u32[]{:S(2)}, u32[]{:S(2)}) collective-permute-start(bf16[256,256]{0,1:T(8,128)(2,1)S(1)} %get-tuple-element.23), channel_id=1, source_target_pairs={{0,12},{4,16},{8,20},{12,24},{16,28},{20,32},{24,36},{28,40},{32,4... | collective-permute-start | bytes 393224 | tf_op jit(solution)/shard_map/ppermute | solution.py:26
  118.1 7.4 %collective-permute-start.24 = (bf16[256,256]{0,1:T(8,128)(2,1)S(1)}, bf16[256,256]{0,1:T(8,128)(2,1)S(1)}, u32[]{:S(2)}, u32[]{:S(2)}) collective-permute-start(bf16[256,256]{0,1:T(8,128)(2,1)S(1)} %get-tuple-element.24), channel_id=1, source_target_pairs={{0,64},{4,68},{8,72},{12,76},{16,80},{20,84},{24,88},{28,92},{32,9... | collective-permute-start | bytes 393224 | tf_op jit(solution)/shard_map/ppermute | solution.py:26
  128.2 4.9 %collective-permute-start.21 = (bf16[256,256]{0,1:T(8,128)(2,1)S(1)}, bf16[256,256]{0,1:T(8,128)(2,1)S(1)}, u32[]{:S(2)}, u32[]{:S(2)}) collective-permute-start(bf16[256,256]{0,1:T(8,128)(2,1)S(1)} %get-tuple-element.27), channel_id=1, source_target_pairs={{0,16},{4,20},{8,24},{12,28},{16,32},{20,36},{24,40},{28,44},{32,4... | collective-permute-start | bytes 393224 | tf_op jit(solution)/shard_map/ppermute | solution.py:26
  133.1 4.9 %collective-permute-start.20 = (bf16[256,256]{0,1:T(8,128)(2,1)}, bf16[256,256]{0,1:T(8,128)(2,1)S(1)}, u32[]{:S(2)}, u32[]{:S(2)}) collective-permute-start(bf16[256,256]{0,1:T(8,128)(2,1)} %get-tuple-element.28), channel_id=1, source_target_pairs={{0,128},{4,132},{8,136},{12,140},{16,144},{20,148},{24,152},{28,15... | collective-permute-start | bytes 393224 | tf_op jit(solution)/shard_map/ppermute | solution.py:26
  139.3 13.0 %collective-permute-start.18 = (bf16[256,256]{0,1:T(8,128)(2,1)S(1)}, bf16[256,256]{0,1:T(8,128)(2,1)S(1)}, u32[]{:S(2)}, u32[]{:S(2)}) collective-permute-start(bf16[256,256]{0,1:T(8,128)(2,1)S(1)} %get-tuple-element.30), channel_id=1, source_target_pairs={{0,256},{4,260},{8,264},{12,268},{16,272},{20,276},{24,280},{28,28... | collective-permute-start | bytes 393224 | tf_op jit(solution)/shard_map/ppermute | solution.py:135
  152.4 4.2 %collective-permute-start.15 = (bf16[256,256]{0,1:T(8,128)(2,1)S(1)}, bf16[256,256]{0,1:T(8,128)(2,1)S(1)}, u32[]{:S(2)}, u32[]{:S(2)}) collective-permute-start(bf16[256,256]{0,1:T(8,128)(2,1)S(1)} %get-tuple-element.31), channel_id=1, source_target_pairs={{4,0},{8,4},{12,8},{16,12},{20,16},{24,20},{28,24},{32,28},{36,32}... | collective-permute-start | bytes 393224 | tf_op jit(solution)/shard_map/ppermute | solution.py:26
  156.6 4.5 %collective-permute-start.16 = (bf16[256,256]{0,1:T(8,128)(2,1)S(1)}, bf16[256,256]{0,1:T(8,128)(2,1)S(1)}, u32[]{:S(2)}, u32[]{:S(2)}) collective-permute-start(bf16[256,256]{0,1:T(8,128)(2,1)S(1)} %get-tuple-element.32), channel_id=1, source_target_pairs={{0,4},{4,8},{8,12},{12,16},{16,20},{20,24},{24,28},{28,32},{32,36}... | collective-permute-start | bytes 393224 | tf_op jit(solution)/shard_map/ppermute | solution.py:26
  161.0 1.4 convolution_multiply_fusion.3
  (103 shorter events, 31.9 us)
Async XLA Ops:
  2.4 86.3 %collective-permute-start.14 = (bf16[256,256]{1,0:T(8,128)(2,1)S(1)}, bf16[256,256]{1,0:T(8,128)(2,1)S(1)}, u32[]{:S(2)}, u32[]{:S(2)}) collective-permute-start(bf16[256,256]{1,0:T(8,128)(2,1)S(1)} %constant_dynamic-update-slice_fusion), channel_id=1, source_target_pairs={{0,8},{4,12},{8,16},{12,20},{16,24},{20,28},{24,32},{28,36},{32,40... | collective-permute-start | bytes 393224 | tf_op jit(solution)/shard_map/ppermute | solution.py:26
  7.3 81.4 %collective-permute-start.13 = (bf16[256,256]{1,0:T(8,128)(2,1)S(1)}, bf16[256,256]{1,0:T(8,128)(2,1)S(1)}, u32[]{:S(2)}, u32[]{:S(2)}) collective-permute-start(bf16[256,256]{1,0:T(8,128)(2,1)S(1)} %constant_dynamic-update-slice_fusion), channel_id=1, source_target_pairs={{8,0},{12,4},{16,8},{20,12},{24,16},{28,20},{32,24},{36,28},{40,32... | collective-permute-start | bytes 393224 | tf_op jit(solution)/shard_map/ppermute | solution.py:26
  8.6 80.1 %collective-permute-start.12 = (bf16[256,256]{1,0:T(8,128)(2,1)S(1)}, bf16[256,256]{1,0:T(8,128)(2,1)S(1)}, u32[]{:S(2)}, u32[]{:S(2)}) collective-permute-start(bf16[256,256]{1,0:T(8,128)(2,1)S(1)} %constant_dynamic-update-slice_fusion), channel_id=1, source_target_pairs={{0,12},{4,16},{8,20},{12,24},{16,28},{20,32},{24,36},{28,40},{32,4... | collective-permute-start | bytes 393224 | tf_op jit(solution)/shard_map/ppermute | solution.py:26
  15.8 29.0 %collective-permute-start.2 = (bf16[256,256]{1,0:T(8,128)(2,1)S(1)}, bf16[256,256]{1,0:T(8,128)(2,1)S(1)}, u32[]{:S(2)}, u32[]{:S(2)}) collective-permute-start(bf16[256,256]{1,0:T(8,128)(2,1)S(1)} %constant_dynamic-update-slice_fusion), channel_id=1, source_target_pairs={{32,0},{36,4},{40,8},{44,12},{48,16},{52,20},{56,24},{60,28},{64,3... | collective-permute-start | bytes 393224 | tf_op jit(solution)/shard_map/ppermute | solution.py:26
  23.3 9.8 %collective-permute-start.1 = (bf16[256,256]{1,0:T(8,128)(2,1)S(1)}, bf16[256,256]{1,0:T(8,128)(2,1)S(1)}, u32[]{:S(2)}, u32[]{:S(2)}) collective-permute-start(bf16[256,256]{1,0:T(8,128)(2,1)S(1)} %constant_dynamic-update-slice_fusion), channel_id=1, source_target_pairs={{4,0},{8,4},{12,8},{16,12},{20,16},{24,20},{28,24},{32,28},{36,32}... | collective-permute-start | bytes 393224 | tf_op jit(solution)/shard_map/ppermute | solution.py:18
  33.1 17.3 %collective-permute-start.3 = (bf16[256,256]{1,0:T(8,128)(2,1)S(1)}, bf16[256,256]{1,0:T(8,128)(2,1)S(1)}, u32[]{:S(2)}, u32[]{:S(2)}) collective-permute-start(bf16[256,256]{1,0:T(8,128)(2,1)S(1)} %constant_dynamic-update-slice_fusion), channel_id=1, source_target_pairs={{0,256},{4,260},{8,264},{12,268},{16,272},{20,276},{24,280},{28,28... | collective-permute-start | bytes 393224 | tf_op jit(solution)/shard_map/ppermute | solution.py:94
  52.3 13.9 %collective-permute-start.6 = (bf16[256,256]{1,0:T(8,128)(2,1)S(1)}, bf16[256,256]{1,0:T(8,128)(2,1)S(1)}, u32[]{:S(2)}, u32[]{:S(2)}) collective-permute-start(bf16[256,256]{1,0:T(8,128)(2,1)S(1)} %constant_dynamic-update-slice_fusion), channel_id=1, source_target_pairs={{16,0},{20,4},{24,8},{28,12},{32,16},{36,20},{40,24},{44,28},{48,3... | collective-permute-start | bytes 393224 | tf_op jit(solution)/shard_map/ppermute | solution.py:26
  58.0 11.6 %collective-permute-start.7 = (bf16[256,256]{1,0:T(8,128)(2,1)S(1)}, bf16[256,256]{1,0:T(8,128)(2,1)S(1)}, u32[]{:S(2)}, u32[]{:S(2)}) collective-permute-start(bf16[256,256]{1,0:T(8,128)(2,1)S(1)} %constant_dynamic-update-slice_fusion), channel_id=1, source_target_pairs={{0,128},{4,132},{8,136},{12,140},{16,144},{20,148},{24,152},{28,15... | collective-permute-start | bytes 393224 | tf_op jit(solution)/shard_map/ppermute | solution.py:26
  69.7 10.3 %collective-permute-start.9 = (bf16[256,256]{1,0:T(8,128)(2,1)S(1)}, bf16[256,256]{1,0:T(8,128)(2,1)S(1)}, u32[]{:S(2)}, u32[]{:S(2)}) collective-permute-start(bf16[256,256]{1,0:T(8,128)(2,1)S(1)} %constant_dynamic-update-slice_fusion), channel_id=1, source_target_pairs={{64,0},{68,4},{72,8},{76,12},{80,16},{84,20},{88,24},{92,28},{96,3... | collective-permute-start | bytes 393224 | tf_op jit(solution)/shard_map/ppermute | solution.py:26
  71.6 15.1 %collective-permute-start.10 = (bf16[256,256]{1,0:T(8,128)(2,1)S(1)}, bf16[256,256]{1,0:T(8,128)(2,1)S(1)}, u32[]{:S(2)}, u32[]{:S(2)}) collective-permute-start(bf16[256,256]{1,0:T(8,128)(2,1)S(1)} %constant_dynamic-update-slice_fusion), channel_id=1, source_target_pairs={{12,0},{16,4},{20,8},{24,12},{28,16},{32,20},{36,24},{40,28},{44,3... | collective-permute-start | bytes 393224 | tf_op jit(solution)/shard_map/ppermute | solution.py:26
  97.4 15.5 %collective-permute-start.17 = (bf16[256,256]{0,1:T(8,128)(2,1)S(1)}, bf16[256,256]{0,1:T(8,128)(2,1)S(1)}, u32[]{:S(2)}, u32[]{:S(2)}) collective-permute-start(bf16[256,256]{0,1:T(8,128)(2,1)S(1)} %get-tuple-element.18), channel_id=1, source_target_pairs={{0,32},{4,36},{8,40},{12,44},{16,48},{20,52},{24,56},{28,60},{32,6... | collective-permute-start | bytes 393224 | tf_op jit(solution)/shard_map/ppermute | solution.py:26
  104.7 13.4 %collective-permute-start.29 = (bf16[256,256]{0,1:T(8,128)(2,1)S(1)}, bf16[256,256]{0,1:T(8,128)(2,1)S(1)}, u32[]{:S(2)}, u32[]{:S(2)}) collective-permute-start(bf16[256,256]{0,1:T(8,128)(2,1)S(1)} %get-tuple-element.19), channel_id=1, source_target_pairs={{8,0},{12,4},{16,8},{20,12},{24,16},{28,20},{32,24},{36,28},{40,32... | collective-permute-start | bytes 393224 | tf_op jit(solution)/shard_map/ppermute | solution.py:26
  106.0 19.6 %collective-permute-start.28 = (bf16[256,256]{0,1:T(8,128)(2,1)S(1)}, bf16[256,256]{0,1:T(8,128)(2,1)S(1)}, u32[]{:S(2)}, u32[]{:S(2)}) collective-permute-start(bf16[256,256]{0,1:T(8,128)(2,1)S(1)} %get-tuple-element.20), channel_id=1, source_target_pairs={{0,8},{4,12},{8,16},{12,20},{16,24},{20,28},{24,32},{28,36},{32,40... | collective-permute-start | bytes 393224 | tf_op jit(solution)/shard_map/ppermute | solution.py:26
  110.0 16.9 %collective-permute-start.27 = (bf16[256,256]{0,1:T(8,128)(2,1)S(1)}, bf16[256,256]{0,1:T(8,128)(2,1)S(1)}, u32[]{:S(2)}, u32[]{:S(2)}) collective-permute-start(bf16[256,256]{0,1:T(8,128)(2,1)S(1)} %get-tuple-element.21), channel_id=1, source_target_pairs={{12,0},{16,4},{20,8},{24,12},{28,16},{32,20},{36,24},{40,28},{44,3... | collective-permute-start | bytes 393224 | tf_op jit(solution)/shard_map/ppermute | solution.py:26
  111.3 16.9 %collective-permute-start.26 = (bf16[256,256]{0,1:T(8,128)(2,1)S(1)}, bf16[256,256]{0,1:T(8,128)(2,1)S(1)}, u32[]{:S(2)}, u32[]{:S(2)}) collective-permute-start(bf16[256,256]{0,1:T(8,128)(2,1)S(1)} %get-tuple-element.22), channel_id=1, source_target_pairs={{64,0},{68,4},{72,8},{76,12},{80,16},{84,20},{88,24},{92,28},{96,3... | collective-permute-start | bytes 393224 | tf_op jit(solution)/shard_map/ppermute | solution.py:26
  112.9 20.2 %collective-permute-start.25 = (bf16[256,256]{0,1:T(8,128)(2,1)S(1)}, bf16[256,256]{0,1:T(8,128)(2,1)S(1)}, u32[]{:S(2)}, u32[]{:S(2)}) collective-permute-start(bf16[256,256]{0,1:T(8,128)(2,1)S(1)} %get-tuple-element.23), channel_id=1, source_target_pairs={{0,12},{4,16},{8,20},{12,24},{16,28},{20,32},{24,36},{28,40},{32,4... | collective-permute-start | bytes 393224 | tf_op jit(solution)/shard_map/ppermute | solution.py:26
  118.1 19.9 %collective-permute-start.24 = (bf16[256,256]{0,1:T(8,128)(2,1)S(1)}, bf16[256,256]{0,1:T(8,128)(2,1)S(1)}, u32[]{:S(2)}, u32[]{:S(2)}) collective-permute-start(bf16[256,256]{0,1:T(8,128)(2,1)S(1)} %get-tuple-element.24), channel_id=1, source_target_pairs={{0,64},{4,68},{8,72},{12,76},{16,80},{20,84},{24,88},{28,92},{32,9... | collective-permute-start | bytes 393224 | tf_op jit(solution)/shard_map/ppermute | solution.py:26
  125.6 13.8 %collective-permute-start.23 = (bf16[256,256]{0,1:T(8,128)(2,1)S(1)}, bf16[256,256]{0,1:T(8,128)(2,1)S(1)}, u32[]{:S(2)}, u32[]{:S(2)}) collective-permute-start(bf16[256,256]{0,1:T(8,128)(2,1)S(1)} %get-tuple-element.25), channel_id=1, source_target_pairs={{16,0},{20,4},{24,8},{28,12},{32,16},{36,20},{40,24},{44,28},{48,3... | collective-permute-start | bytes 393224 | tf_op jit(solution)/shard_map/ppermute | solution.py:26
  126.9 25.5 %collective-permute-start.22 = (bf16[256,256]{0,1:T(8,128)(2,1)S(1)}, bf16[256,256]{0,1:T(8,128)(2,1)S(1)}, u32[]{:S(2)}, u32[]{:S(2)}) collective-permute-start(bf16[256,256]{0,1:T(8,128)(2,1)S(1)} %get-tuple-element.26), channel_id=1, source_target_pairs={{128,0},{132,4},{136,8},{140,12},{144,16},{148,20},{152,24},{156,2... | collective-permute-start | bytes 393224 | tf_op jit(solution)/shard_map/ppermute | solution.py:26
  128.2 28.4 %collective-permute-start.21 = (bf16[256,256]{0,1:T(8,128)(2,1)S(1)}, bf16[256,256]{0,1:T(8,128)(2,1)S(1)}, u32[]{:S(2)}, u32[]{:S(2)}) collective-permute-start(bf16[256,256]{0,1:T(8,128)(2,1)S(1)} %get-tuple-element.27), channel_id=1, source_target_pairs={{0,16},{4,20},{8,24},{12,28},{16,32},{20,36},{24,40},{28,44},{32,4... | collective-permute-start | bytes 393224 | tf_op jit(solution)/shard_map/ppermute | solution.py:26
  133.1 30.1 %collective-permute-start.20 = (bf16[256,256]{0,1:T(8,128)(2,1)}, bf16[256,256]{0,1:T(8,128)(2,1)S(1)}, u32[]{:S(2)}, u32[]{:S(2)}) collective-permute-start(bf16[256,256]{0,1:T(8,128)(2,1)} %get-tuple-element.28), channel_id=1, source_target_pairs={{0,128},{4,132},{8,136},{12,140},{16,144},{20,148},{24,152},{28,15... | collective-permute-start | bytes 393224 | tf_op jit(solution)/shard_map/ppermute | solution.py:26
  138.0 25.2 %collective-permute-start.19 = (bf16[256,256]{0,1:T(8,128)(2,1)S(1)}, bf16[256,256]{0,1:T(8,128)(2,1)S(1)}, u32[]{:S(2)}, u32[]{:S(2)}) collective-permute-start(bf16[256,256]{0,1:T(8,128)(2,1)S(1)} %get-tuple-element.29), channel_id=1, source_target_pairs={{32,0},{36,4},{40,8},{44,12},{48,16},{52,20},{56,24},{60,28},{64,3... | collective-permute-start | bytes 393224 | tf_op jit(solution)/shard_map/ppermute | solution.py:26
  139.3 23.9 %collective-permute-start.18 = (bf16[256,256]{0,1:T(8,128)(2,1)S(1)}, bf16[256,256]{0,1:T(8,128)(2,1)S(1)}, u32[]{:S(2)}, u32[]{:S(2)}) collective-permute-start(bf16[256,256]{0,1:T(8,128)(2,1)S(1)} %get-tuple-element.30), channel_id=1, source_target_pairs={{0,256},{4,260},{8,264},{12,268},{16,272},{20,276},{24,280},{28,28... | collective-permute-start | bytes 393224 | tf_op jit(solution)/shard_map/ppermute | solution.py:135
  152.4 10.8 %collective-permute-start.15 = (bf16[256,256]{0,1:T(8,128)(2,1)S(1)}, bf16[256,256]{0,1:T(8,128)(2,1)S(1)}, u32[]{:S(2)}, u32[]{:S(2)}) collective-permute-start(bf16[256,256]{0,1:T(8,128)(2,1)S(1)} %get-tuple-element.31), channel_id=1, source_target_pairs={{4,0},{8,4},{12,8},{16,12},{20,16},{24,20},{28,24},{32,28},{36,32}... | collective-permute-start | bytes 393224 | tf_op jit(solution)/shard_map/ppermute | solution.py:26
  (10 other events, 152.7 us)

commit v10 on v8

--- a/solution.py
+++ b/solution.py
@@ -128,7 +128,7 @@
     far_terms = key_terms(
         weights[:, 3 * tok_rows :], dscores[:, 3 * tok_rows :], query_tokens, grad_out
     )
-    for slot_index in range(len(offsets)):
+    for slot_index in reversed(range(len(offsets))):
         first_row = slot_index * 2 * BLK
         grad_piece = far_terms[first_row : first_row + 2 * BLK].astype(jnp.bfloat16)
         if offsets[slot_index] == half:

time: 166 us -> 173 us (1.042)
  the two profiles are of different devices: /device:TPU:1 before, /device:TPU:38 now
where the time goes in v10:
time: 173 us; the launch traced here: 172 us
  starting transfers between devices  109 us (63%)
  waiting for transfers between devices  41.5 us (24%)
  local copies, waits for them, and re-layouts  8.93 us (5%)
  matrix products  7.99 us (5%)
  other arithmetic  3.01 us (2%)
    ppermute x26, starting transfers between devices, from_behind(): lax.ppermute(value, axis, [(source, source + steps) for source in range(l...  99.7 us
    ppermute x26, waiting for transfers between devices, from_behind(): lax.ppermute(value, axis, [(source, source + steps) for source in range(l...  36.3 us
    unnamed x29, local copies, waits for them, and re-layouts  5.43 us
    ppermute x1, waiting for transfers between devices, extended(): before = lax.ppermute(last, axis, up)  3.55 us
  transfers between devices with their start and end apart: 30, of which 9 were waited for; matrix products, arithmetic and copies ran while one was open for 4% of the time, Pallas kernels for 0%

profile of v10, /device:TPU:38, one launch (start us, length us, event | category | flops | bytes accessed | tf_op | source)
XLA Modules:
  0.0 171.8 jit_solution(3181365763133561477)
XLA Ops:
  2.4 4.3 %collective-permute-start.14 = (bf16[256,256]{1,0:T(8,128)(2,1)S(1)}, bf16[256,256]{1,0:T(8,128)(2,1)S(1)}, u32[]{:S(2)}, u32[]{:S(2)}) collective-permute-start(bf16[256,256]{1,0:T(8,128)(2,1)S(1)} %constant_dynamic-update-slice_fusion), channel_id=1, source_target_pairs={{0,8},{4,12},{8,16},{12,20},{16,24},{20,28},{24,32},{28,36},{32,40... | collective-permute-start | bytes 393224 | tf_op jit(solution)/shard_map/ppermute | solution.py:26
  6.7 8.5 %collective-permute-start.13 = (bf16[256,256]{1,0:T(8,128)(2,1)S(1)}, bf16[256,256]{1,0:T(8,128)(2,1)S(1)}, u32[]{:S(2)}, u32[]{:S(2)}) collective-permute-start(bf16[256,256]{1,0:T(8,128)(2,1)S(1)} %constant_dynamic-update-slice_fusion), channel_id=1, source_target_pairs={{8,0},{12,4},{16,8},{20,12},{24,16},{28,20},{32,24},{36,28},{40,32... | collective-permute-start | bytes 393224 | tf_op jit(solution)/shard_map/ppermute | solution.py:26
  15.2 3.5 %collective-permute-start.12 = (bf16[256,256]{1,0:T(8,128)(2,1)S(1)}, bf16[256,256]{1,0:T(8,128)(2,1)S(1)}, u32[]{:S(2)}, u32[]{:S(2)}) collective-permute-start(bf16[256,256]{1,0:T(8,128)(2,1)S(1)} %constant_dynamic-update-slice_fusion), channel_id=1, source_target_pairs={{0,64},{4,68},{8,72},{12,76},{16,80},{20,84},{24,88},{28,92},{32,9... | collective-permute-start | bytes 393224 | tf_op jit(solution)/shard_map/ppermute | solution.py:26
  18.7 6.3 %collective-permute-start.2 = (bf16[256,256]{1,0:T(8,128)(2,1)S(1)}, bf16[256,256]{1,0:T(8,128)(2,1)S(1)}, u32[]{:S(2)}, u32[]{:S(2)}) collective-permute-start(bf16[256,256]{1,0:T(8,128)(2,1)S(1)} %constant_dynamic-update-slice_fusion), channel_id=1, source_target_pairs={{32,0},{36,4},{40,8},{44,12},{48,16},{52,20},{56,24},{60,28},{64,3... | collective-permute-start | bytes 393224 | tf_op jit(solution)/shard_map/ppermute | solution.py:26
  31.2 3.5 %collective-permute-done = bf16[256,256]{1,0:T(8,128)(2,1)S(1)} collective-permute-done((bf16[256,256]{1,0:T(8,128)(2,1)S(1)}, bf16[256,256]{1,0:T(8,128)(2,1)S(1)}, u32[]{:S(2)}, u32[]{:S(2)}) %collective-permute-start) | collective-permute-done | bytes 131104 | tf_op jit(solution)/shard_map/ppermute | solution.py:17
  34.7 3.4 %collective-permute-start.1 = (bf16[256,256]{1,0:T(8,128)(2,1)S(1)}, bf16[256,256]{1,0:T(8,128)(2,1)S(1)}, u32[]{:S(2)}, u32[]{:S(2)}) collective-permute-start(bf16[256,256]{1,0:T(8,128)(2,1)S(1)} %constant_dynamic-update-slice_fusion), channel_id=1, source_target_pairs={{4,0},{8,4},{12,8},{16,12},{20,16},{24,20},{28,24},{32,28},{36,32}... | collective-permute-start | bytes 393224 | tf_op jit(solution)/shard_map/ppermute | solution.py:18
  42.6 2.1 %collective-permute-start.4 = (bf16[256,256]{1,0:T(8,128)(2,1)S(1)}, bf16[256,256]{1,0:T(8,128)(2,1)S(1)}, u32[]{:S(2)}, u32[]{:S(2)}) collective-permute-start(bf16[256,256]{1,0:T(8,128)(2,1)S(1)} %constant_dynamic-update-slice_fusion), channel_id=1, source_target_pairs={{0,256},{4,260},{8,264},{12,268},{16,272},{20,276},{24,280},{28,28... | collective-permute-start | bytes 393224 | tf_op jit(solution)/shard_map/ppermute | solution.py:94
  44.7 13.9 %collective-permute-done.3 = bf16[256,256]{1,0:T(8,128)(2,1)S(1)} collective-permute-done((bf16[256,256]{1,0:T(8,128)(2,1)S(1)}, bf16[256,256]{1,0:T(8,128)(2,1)S(1)}, u32[]{:S(2)}, u32[]{:S(2)}) %collective-permute-start.3) | collective-permute-done | bytes 131104 | tf_op jit(solution)/shard_map/ppermute | solution.py:26
  60.6 4.8 %collective-permute-start.6 = (bf16[256,256]{1,0:T(8,128)(2,1)S(1)}, bf16[256,256]{1,0:T(8,128)(2,1)S(1)}, u32[]{:S(2)}, u32[]{:S(2)}) collective-permute-start(bf16[256,256]{1,0:T(8,128)(2,1)S(1)} %constant_dynamic-update-slice_fusion), channel_id=1, source_target_pairs={{0,16},{4,20},{8,24},{12,28},{16,32},{20,36},{24,40},{28,44},{32,4... | collective-permute-start | bytes 393224 | tf_op jit(solution)/shard_map/ppermute | solution.py:26
  68.3 4.2 %collective-permute-done.6 = bf16[256,256]{1,0:T(8,128)(2,1)S(1)} collective-permute-done((bf16[256,256]{1,0:T(8,128)(2,1)S(1)}, bf16[256,256]{1,0:T(8,128)(2,1)S(1)}, u32[]{:S(2)}, u32[]{:S(2)}) %collective-permute-start.6) | collective-permute-done | bytes 131104 | tf_op jit(solution)/shard_map/ppermute | solution.py:26
  74.5 1.9 %collective-permute-start.9 = (bf16[256,256]{1,0:T(8,128)(2,1)S(1)}, bf16[256,256]{1,0:T(8,128)(2,1)S(1)}, u32[]{:S(2)}, u32[]{:S(2)}) collective-permute-start(bf16[256,256]{1,0:T(8,128)(2,1)S(1)} %constant_dynamic-update-slice_fusion), channel_id=1, source_target_pairs={{12,0},{16,4},{20,8},{24,12},{28,16},{32,20},{36,24},{40,28},{44,3... | collective-permute-start | bytes 393224 | tf_op jit(solution)/shard_map/ppermute | solution.py:26
  76.5 5.1 %collective-permute-done.8 = bf16[256,256]{1,0:T(8,128)(2,1)S(1)} collective-permute-done((bf16[256,256]{1,0:T(8,128)(2,1)S(1)}, bf16[256,256]{1,0:T(8,128)(2,1)S(1)}, u32[]{:S(2)}, u32[]{:S(2)}) %collective-permute-start.8) | collective-permute-done | bytes 131104 | tf_op jit(solution)/shard_map/ppermute | solution.py:26
  83.5 1.9 %collective-permute-start.11 = (bf16[256,256]{1,0:T(8,128)(2,1)S(1)}, bf16[256,256]{1,0:T(8,128)(2,1)S(1)}, u32[]{:S(2)}, u32[]{:S(2)}) collective-permute-start(bf16[256,256]{1,0:T(8,128)(2,1)S(1)} %constant_dynamic-update-slice_fusion), channel_id=1, source_target_pairs={{64,0},{68,4},{72,8},{76,12},{80,16},{84,20},{88,24},{92,28},{96,3... | collective-permute-start | bytes 393224 | tf_op jit(solution)/shard_map/ppermute | solution.py:26
  85.4 6.6 %collective-permute-done.10 = bf16[256,256]{1,0:T(8,128)(2,1)S(1)} collective-permute-done((bf16[256,256]{1,0:T(8,128)(2,1)S(1)}, bf16[256,256]{1,0:T(8,128)(2,1)S(1)}, u32[]{:S(2)}, u32[]{:S(2)}) %collective-permute-start.10) | collective-permute-done | bytes 131104 | tf_op jit(solution)/shard_map/ppermute | solution.py:26
  92.2 3.3 %fusion.36 = (f32[256]{0:T(256)S(1)}, f32[256,4096]{0,1:T(8,128)S(1)}) fusion(bf16[256,128]{1,0:T(8,128)(2,1)S(1)} %copy-done.3, bf16[4096,256]{1,0:T(8,128)(2,1)S(1)} %constant_dynamic-update-slice_fusion.2, pred[256,3328]{0,1:T(32,128)(4,1)S(1)} %bitcast.21, pred[4096]{0:T(1024)(128)(4,1)S(1)} %pad.4.clone), kind=kOutput, calls=%fused_computation.93 | convolution fusion | flops 272629504 | bytes 6165504 | tf_op jit(solution)/shard_map/dot_general | solution.py:54
  100.9 4.8 %collective-permute-start.17 = (bf16[256,256]{0,1:T(8,128)(2,1)S(1)}, bf16[256,256]{0,1:T(8,128)(2,1)S(1)}, u32[]{:S(2)}, u32[]{:S(2)}) collective-permute-start(bf16[256,256]{0,1:T(8,128)(2,1)S(1)} %get-tuple-element.18), channel_id=1, source_target_pairs={{8,0},{12,4},{16,8},{20,12},{24,16},{28,20},{32,24},{36,28},{40,32... | collective-permute-start | bytes 393224 | tf_op jit(solution)/shard_map/ppermute | solution.py:26
  105.7 1.9 %collective-permute-start.29 = (bf16[256,256]{0,1:T(8,128)(2,1)S(1)}, bf16[256,256]{0,1:T(8,128)(2,1)S(1)}, u32[]{:S(2)}, u32[]{:S(2)}) collective-permute-start(bf16[256,256]{0,1:T(8,128)(2,1)S(1)} %get-tuple-element.19), channel_id=1, source_target_pairs={{0,32},{4,36},{8,40},{12,44},{16,48},{20,52},{24,56},{28,60},{32,6... | collective-permute-start | bytes 393224 | tf_op jit(solution)/shard_map/ppermute | solution.py:26
  107.6 9.9 %collective-permute-start.28 = (bf16[256,256]{0,1:T(8,128)(2,1)S(1)}, bf16[256,256]{0,1:T(8,128)(2,1)S(1)}, u32[]{:S(2)}, u32[]{:S(2)}) collective-permute-start(bf16[256,256]{0,1:T(8,128)(2,1)S(1)} %get-tuple-element.20), channel_id=1, source_target_pairs={{32,0},{36,4},{40,8},{44,12},{48,16},{52,20},{56,24},{60,28},{64,3... | collective-permute-start | bytes 393224 | tf_op jit(solution)/shard_map/ppermute | solution.py:26
  121.8 8.1 %collective-permute-start.25 = (bf16[256,256]{0,1:T(8,128)(2,1)S(1)}, bf16[256,256]{0,1:T(8,128)(2,1)S(1)}, u32[]{:S(2)}, u32[]{:S(2)}) collective-permute-start(bf16[256,256]{0,1:T(8,128)(2,1)S(1)} %get-tuple-element.23), channel_id=1, source_target_pairs={{16,0},{20,4},{24,8},{28,12},{32,16},{36,20},{40,24},{44,28},{48,3... | collective-permute-start | bytes 393224 | tf_op jit(solution)/shard_map/ppermute | solution.py:26
  131.9 6.0 %collective-permute-start.23 = (bf16[256,256]{0,1:T(8,128)(2,1)S(1)}, bf16[256,256]{0,1:T(8,128)(2,1)S(1)}, u32[]{:S(2)}, u32[]{:S(2)}) collective-permute-start(bf16[256,256]{0,1:T(8,128)(2,1)S(1)} %get-tuple-element.25), channel_id=1, source_target_pairs={{128,0},{132,4},{136,8},{140,12},{144,16},{148,20},{152,24},{156,2... | collective-permute-start | bytes 393224 | tf_op jit(solution)/shard_map/ppermute | solution.py:26
  139.8 7.9 %collective-permute-start.21 = (bf16[256,256]{0,1:T(8,128)(2,1)S(1)}, bf16[256,256]{0,1:T(8,128)(2,1)S(1)}, u32[]{:S(2)}, u32[]{:S(2)}) collective-permute-start(bf16[256,256]{0,1:T(8,128)(2,1)S(1)} %get-tuple-element.27), channel_id=1, source_target_pairs={{12,0},{16,4},{20,8},{24,12},{28,16},{32,20},{36,24},{40,28},{44,3... | collective-permute-start | bytes 393224 | tf_op jit(solution)/shard_map/ppermute | solution.py:26
  149.7 5.1 %collective-permute-start.19 = (bf16[256,256]{0,1:T(8,128)(2,1)S(1)}, bf16[256,256]{0,1:T(8,128)(2,1)S(1)}, u32[]{:S(2)}, u32[]{:S(2)}) collective-permute-start(bf16[256,256]{0,1:T(8,128)(2,1)S(1)} %get-tuple-element.29), channel_id=1, source_target_pairs={{64,0},{68,4},{72,8},{76,12},{80,16},{84,20},{88,24},{92,28},{96,3... | collective-permute-start | bytes 393224 | tf_op jit(solution)/shard_map/ppermute | solution.py:26
  156.8 3.6 %collective-permute-start.15 = (bf16[256,256]{0,1:T(8,128)(2,1)S(1)}, bf16[256,256]{0,1:T(8,128)(2,1)S(1)}, u32[]{:S(2)}, u32[]{:S(2)}) collective-permute-start(bf16[256,256]{0,1:T(8,128)(2,1)S(1)} %get-tuple-element.31), channel_id=1, source_target_pairs={{4,0},{8,4},{12,8},{16,12},{20,16},{24,20},{28,24},{32,28},{36,32}... | collective-permute-start | bytes 393224 | tf_op jit(solution)/shard_map/ppermute | solution.py:26
  165.0 5.0 %collective-permute-done.16 = bf16[256,256]{0,1:T(8,128)(2,1)S(1)} collective-permute-done((bf16[256,256]{0,1:T(8,128)(2,1)S(1)}, bf16[256,256]{0,1:T(8,128)(2,1)S(1)}, u32[]{:S(2)}, u32[]{:S(2)}) %collective-permute-start.16) | collective-permute-done | bytes 131104 | tf_op jit(solution)/shard_map/ppermute | solution.py:26
  (103 shorter events, 44.7 us)
Async XLA Ops:
  2.4 89.7 %collective-permute-start.14 = (bf16[256,256]{1,0:T(8,128)(2,1)S(1)}, bf16[256,256]{1,0:T(8,128)(2,1)S(1)}, u32[]{:S(2)}, u32[]{:S(2)}) collective-permute-start(bf16[256,256]{1,0:T(8,128)(2,1)S(1)} %constant_dynamic-update-slice_fusion), channel_id=1, source_target_pairs={{0,8},{4,12},{8,16},{12,20},{16,24},{20,28},{24,32},{28,36},{32,40... | collective-permute-start | bytes 393224 | tf_op jit(solution)/shard_map/ppermute | solution.py:26
  6.7 85.4 %collective-permute-start.13 = (bf16[256,256]{1,0:T(8,128)(2,1)S(1)}, bf16[256,256]{1,0:T(8,128)(2,1)S(1)}, u32[]{:S(2)}, u32[]{:S(2)}) collective-permute-start(bf16[256,256]{1,0:T(8,128)(2,1)S(1)} %constant_dynamic-update-slice_fusion), channel_id=1, source_target_pairs={{8,0},{12,4},{16,8},{20,12},{24,16},{28,20},{32,24},{36,28},{40,32... | collective-permute-start | bytes 393224 | tf_op jit(solution)/shard_map/ppermute | solution.py:26
  15.2 76.9 %collective-permute-start.12 = (bf16[256,256]{1,0:T(8,128)(2,1)S(1)}, bf16[256,256]{1,0:T(8,128)(2,1)S(1)}, u32[]{:S(2)}, u32[]{:S(2)}) collective-permute-start(bf16[256,256]{1,0:T(8,128)(2,1)S(1)} %constant_dynamic-update-slice_fusion), channel_id=1, source_target_pairs={{0,64},{4,68},{8,72},{12,76},{16,80},{20,84},{24,88},{28,92},{32,9... | collective-permute-start | bytes 393224 | tf_op jit(solution)/shard_map/ppermute | solution.py:26
  18.7 23.9 %collective-permute-start.2 = (bf16[256,256]{1,0:T(8,128)(2,1)S(1)}, bf16[256,256]{1,0:T(8,128)(2,1)S(1)}, u32[]{:S(2)}, u32[]{:S(2)}) collective-permute-start(bf16[256,256]{1,0:T(8,128)(2,1)S(1)} %constant_dynamic-update-slice_fusion), channel_id=1, source_target_pairs={{32,0},{36,4},{40,8},{44,12},{48,16},{52,20},{56,24},{60,28},{64,3... | collective-permute-start | bytes 393224 | tf_op jit(solution)/shard_map/ppermute | solution.py:26
  25.0 9.7 %collective-permute-start = (bf16[256,256]{1,0:T(8,128)(2,1)S(1)}, bf16[256,256]{1,0:T(8,128)(2,1)S(1)}, u32[]{:S(2)}, u32[]{:S(2)}) collective-permute-start(bf16[256,256]{1,0:T(8,128)(2,1)S(1)} %constant_dynamic-update-slice_fusion), channel_id=1, source_target_pairs={{0,4},{4,8},{8,12},{12,16},{16,20},{20,24},{24,28},{28,32},{32,36}... | collective-permute-start | bytes 393224 | tf_op jit(solution)/shard_map/ppermute | solution.py:17
  40.6 18.0 %collective-permute-start.3 = (bf16[256,256]{1,0:T(8,128)(2,1)S(1)}, bf16[256,256]{1,0:T(8,128)(2,1)S(1)}, u32[]{:S(2)}, u32[]{:S(2)}) collective-permute-start(bf16[256,256]{1,0:T(8,128)(2,1)S(1)} %constant_dynamic-update-slice_fusion), channel_id=1, source_target_pairs={{0,32},{4,36},{8,40},{12,44},{16,48},{20,52},{24,56},{28,60},{32,6... | collective-permute-start | bytes 393224 | tf_op jit(solution)/shard_map/ppermute | solution.py:26
  42.6 18.0 %collective-permute-start.4 = (bf16[256,256]{1,0:T(8,128)(2,1)S(1)}, bf16[256,256]{1,0:T(8,128)(2,1)S(1)}, u32[]{:S(2)}, u32[]{:S(2)}) collective-permute-start(bf16[256,256]{1,0:T(8,128)(2,1)S(1)} %constant_dynamic-update-slice_fusion), channel_id=1, source_target_pairs={{0,256},{4,260},{8,264},{12,268},{16,272},{20,276},{24,280},{28,28... | collective-permute-start | bytes 393224 | tf_op jit(solution)/shard_map/ppermute | solution.py:94
  60.6 12.0 %collective-permute-start.6 = (bf16[256,256]{1,0:T(8,128)(2,1)S(1)}, bf16[256,256]{1,0:T(8,128)(2,1)S(1)}, u32[]{:S(2)}, u32[]{:S(2)}) collective-permute-start(bf16[256,256]{1,0:T(8,128)(2,1)S(1)} %constant_dynamic-update-slice_fusion), channel_id=1, source_target_pairs={{0,16},{4,20},{8,24},{12,28},{16,32},{20,36},{24,40},{28,44},{32,4... | collective-permute-start | bytes 393224 | tf_op jit(solution)/shard_map/ppermute | solution.py:26
  72.6 9.0 %collective-permute-start.8 = (bf16[256,256]{1,0:T(8,128)(2,1)S(1)}, bf16[256,256]{1,0:T(8,128)(2,1)S(1)}, u32[]{:S(2)}, u32[]{:S(2)}) collective-permute-start(bf16[256,256]{1,0:T(8,128)(2,1)S(1)} %constant_dynamic-update-slice_fusion), channel_id=1, source_target_pairs={{0,128},{4,132},{8,136},{12,140},{16,144},{20,148},{24,152},{28,15... | collective-permute-start | bytes 393224 | tf_op jit(solution)/shard_map/ppermute | solution.py:26
  81.5 10.5 %collective-permute-start.10 = (bf16[256,256]{1,0:T(8,128)(2,1)S(1)}, bf16[256,256]{1,0:T(8,128)(2,1)S(1)}, u32[]{:S(2)}, u32[]{:S(2)}) collective-permute-start(bf16[256,256]{1,0:T(8,128)(2,1)S(1)} %constant_dynamic-update-slice_fusion), channel_id=1, source_target_pairs={{0,12},{4,16},{8,20},{12,24},{16,28},{20,32},{24,36},{28,40},{32,4... | collective-permute-start | bytes 393224 | tf_op jit(solution)/shard_map/ppermute | solution.py:26
  100.9 20.9 %collective-permute-start.17 = (bf16[256,256]{0,1:T(8,128)(2,1)S(1)}, bf16[256,256]{0,1:T(8,128)(2,1)S(1)}, u32[]{:S(2)}, u32[]{:S(2)}) collective-permute-start(bf16[256,256]{0,1:T(8,128)(2,1)S(1)} %get-tuple-element.18), channel_id=1, source_target_pairs={{8,0},{12,4},{16,8},{20,12},{24,16},{28,20},{32,24},{36,28},{40,32... | collective-permute-start | bytes 393224 | tf_op jit(solution)/shard_map/ppermute | solution.py:26
  105.7 24.2 %collective-permute-start.29 = (bf16[256,256]{0,1:T(8,128)(2,1)S(1)}, bf16[256,256]{0,1:T(8,128)(2,1)S(1)}, u32[]{:S(2)}, u32[]{:S(2)}) collective-permute-start(bf16[256,256]{0,1:T(8,128)(2,1)S(1)} %get-tuple-element.19), channel_id=1, source_target_pairs={{0,32},{4,36},{8,40},{12,44},{16,48},{20,52},{24,56},{28,60},{32,6... | collective-permute-start | bytes 393224 | tf_op jit(solution)/shard_map/ppermute | solution.py:26
  107.6 24.2 %collective-permute-start.28 = (bf16[256,256]{0,1:T(8,128)(2,1)S(1)}, bf16[256,256]{0,1:T(8,128)(2,1)S(1)}, u32[]{:S(2)}, u32[]{:S(2)}) collective-permute-start(bf16[256,256]{0,1:T(8,128)(2,1)S(1)} %get-tuple-element.20), channel_id=1, source_target_pairs={{32,0},{36,4},{40,8},{44,12},{48,16},{52,20},{56,24},{60,28},{64,3... | collective-permute-start | bytes 393224 | tf_op jit(solution)/shard_map/ppermute | solution.py:26
  117.5 20.4 %collective-permute-start.27 = (bf16[256,256]{0,1:T(8,128)(2,1)S(1)}, bf16[256,256]{0,1:T(8,128)(2,1)S(1)}, u32[]{:S(2)}, u32[]{:S(2)}) collective-permute-start(bf16[256,256]{0,1:T(8,128)(2,1)S(1)} %get-tuple-element.21), channel_id=1, source_target_pairs={{0,256},{4,260},{8,264},{12,268},{16,272},{20,276},{24,280},{28,28... | collective-permute-start | bytes 393224 | tf_op jit(solution)/shard_map/ppermute | solution.py:135
  119.5 20.4 %collective-permute-start.26 = (bf16[256,256]{0,1:T(8,128)(2,1)S(1)}, bf16[256,256]{0,1:T(8,128)(2,1)S(1)}, u32[]{:S(2)}, u32[]{:S(2)}) collective-permute-start(bf16[256,256]{0,1:T(8,128)(2,1)S(1)} %get-tuple-element.22), channel_id=1, source_target_pairs={{0,16},{4,20},{8,24},{12,28},{16,32},{20,36},{24,40},{28,44},{32,4... | collective-permute-start | bytes 393224 | tf_op jit(solution)/shard_map/ppermute | solution.py:26
  121.8 26.0 %collective-permute-start.25 = (bf16[256,256]{0,1:T(8,128)(2,1)S(1)}, bf16[256,256]{0,1:T(8,128)(2,1)S(1)}, u32[]{:S(2)}, u32[]{:S(2)}) collective-permute-start(bf16[256,256]{0,1:T(8,128)(2,1)S(1)} %get-tuple-element.23), channel_id=1, source_target_pairs={{16,0},{20,4},{24,8},{28,12},{32,16},{36,20},{40,24},{44,28},{48,3... | collective-permute-start | bytes 393224 | tf_op jit(solution)/shard_map/ppermute | solution.py:26
  129.9 19.8 %collective-permute-start.24 = (bf16[256,256]{0,1:T(8,128)(2,1)S(1)}, bf16[256,256]{0,1:T(8,128)(2,1)S(1)}, u32[]{:S(2)}, u32[]{:S(2)}) collective-permute-start(bf16[256,256]{0,1:T(8,128)(2,1)S(1)} %get-tuple-element.24), channel_id=1, source_target_pairs={{0,128},{4,132},{8,136},{12,140},{16,144},{20,148},{24,152},{28,15... | collective-permute-start | bytes 393224 | tf_op jit(solution)/shard_map/ppermute | solution.py:26
  131.9 23.0 %collective-permute-start.23 = (bf16[256,256]{0,1:T(8,128)(2,1)S(1)}, bf16[256,256]{0,1:T(8,128)(2,1)S(1)}, u32[]{:S(2)}, u32[]{:S(2)}) collective-permute-start(bf16[256,256]{0,1:T(8,128)(2,1)S(1)} %get-tuple-element.25), channel_id=1, source_target_pairs={{128,0},{132,4},{136,8},{140,12},{144,16},{148,20},{152,24},{156,2... | collective-permute-start | bytes 393224 | tf_op jit(solution)/shard_map/ppermute | solution.py:26
  137.9 18.9 %collective-permute-start.22 = (bf16[256,256]{0,1:T(8,128)(2,1)S(1)}, bf16[256,256]{0,1:T(8,128)(2,1)S(1)}, u32[]{:S(2)}, u32[]{:S(2)}) collective-permute-start(bf16[256,256]{0,1:T(8,128)(2,1)S(1)} %get-tuple-element.26), channel_id=1, source_target_pairs={{0,12},{4,16},{8,20},{12,24},{16,28},{20,32},{24,36},{28,40},{32,4... | collective-permute-start | bytes 393224 | tf_op jit(solution)/shard_map/ppermute | solution.py:26
  139.8 20.6 %collective-permute-start.21 = (bf16[256,256]{0,1:T(8,128)(2,1)S(1)}, bf16[256,256]{0,1:T(8,128)(2,1)S(1)}, u32[]{:S(2)}, u32[]{:S(2)}) collective-permute-start(bf16[256,256]{0,1:T(8,128)(2,1)S(1)} %get-tuple-element.27), channel_id=1, source_target_pairs={{12,0},{16,4},{20,8},{24,12},{28,16},{32,20},{36,24},{40,28},{44,3... | collective-permute-start | bytes 393224 | tf_op jit(solution)/shard_map/ppermute | solution.py:26
  147.7 16.8 %collective-permute-start.20 = (bf16[256,256]{0,1:T(8,128)(2,1)}, bf16[256,256]{0,1:T(8,128)(2,1)S(1)}, u32[]{:S(2)}, u32[]{:S(2)}) collective-permute-start(bf16[256,256]{0,1:T(8,128)(2,1)} %get-tuple-element.28), channel_id=1, source_target_pairs={{0,64},{4,68},{8,72},{12,76},{16,80},{20,84},{24,88},{28,92},{32,9... | collective-permute-start | bytes 393224 | tf_op jit(solution)/shard_map/ppermute | solution.py:26
  149.7 14.8 %collective-permute-start.19 = (bf16[256,256]{0,1:T(8,128)(2,1)S(1)}, bf16[256,256]{0,1:T(8,128)(2,1)S(1)}, u32[]{:S(2)}, u32[]{:S(2)}) collective-permute-start(bf16[256,256]{0,1:T(8,128)(2,1)S(1)} %get-tuple-element.29), channel_id=1, source_target_pairs={{64,0},{68,4},{72,8},{76,12},{80,16},{84,20},{88,24},{92,28},{96,3... | collective-permute-start | bytes 393224 | tf_op jit(solution)/shard_map/ppermute | solution.py:26
  154.8 10.2 %collective-permute-start.18 = (bf16[256,256]{0,1:T(8,128)(2,1)S(1)}, bf16[256,256]{0,1:T(8,128)(2,1)S(1)}, u32[]{:S(2)}, u32[]{:S(2)}) collective-permute-start(bf16[256,256]{0,1:T(8,128)(2,1)S(1)} %get-tuple-element.30), channel_id=1, source_target_pairs={{0,8},{4,12},{8,16},{12,20},{16,24},{20,28},{24,32},{28,36},{32,40... | collective-permute-start | bytes 393224 | tf_op jit(solution)/shard_map/ppermute | solution.py:26
  160.4 9.6 %collective-permute-start.16 = (bf16[256,256]{0,1:T(8,128)(2,1)S(1)}, bf16[256,256]{0,1:T(8,128)(2,1)S(1)}, u32[]{:S(2)}, u32[]{:S(2)}) collective-permute-start(bf16[256,256]{0,1:T(8,128)(2,1)S(1)} %get-tuple-element.32), channel_id=1, source_target_pairs={{0,4},{4,8},{8,12},{12,16},{16,20},{20,24},{24,28},{28,32},{32,36}... | collective-permute-start | bytes 393224 | tf_op jit(solution)/shard_map/ppermute | solution.py:26
  (10 other events, 174.3 us)

commit v11 on v9

--- a/solution.py
+++ b/solution.py
@@ -88,7 +88,7 @@
     near_ok = (neighbour >= 0) & (neighbour < frame_count)
     pieces = [near_keys]
     half = frame_count // 2
-    offsets = [o for o in (8, half, -8, 32, 4, -32, -4, 16, 3, -16, -3, 2, -2) if o in offsets]
+    offsets = [o for o in (half, 8, -8, 32, -32, 4, -4, 16, -16, 3, -3, 2, -2) if o in offsets]
     for offset in offsets:
         if offset == half:
             arrived = lax.ppermute(

time: 166 us -> 173 us (1.042)
  the two profiles are of different devices: /device:TPU:1 before, /device:TPU:38 now
where the time goes in v11:
time: 173 us; the launch traced here: 172 us
  starting transfers between devices  125 us (72%)
  waiting for transfers between devices  25.9 us (15%)
  local copies, waits for them, and re-layouts  8.93 us (5%)
  matrix products  7.99 us (5%)
  other arithmetic  3.01 us (2%)
    ppermute x26, starting transfers between devices, from_behind(): lax.ppermute(value, axis, [(source, source + steps) for source in range(l...  114 us
    ppermute x26, waiting for transfers between devices, from_behind(): lax.ppermute(value, axis, [(source, source + steps) for source in range(l...  18.3 us
    ppermute x1, waiting for transfers between devices, extended(): before = lax.ppermute(last, axis, up)  5.99 us
    ppermute x1, starting transfers between devices, shards(): lax.ppermute(grad_piece, 'seq', [(src, (src + half) % frame_count) for sr...  5.77 us
    unnamed x29, local copies, waits for them, and re-layouts  5.42 us
  transfers between devices with their start and end apart: 30, of which 9 were waited for; matrix products, arithmetic and copies ran while one was open for 4% of the time, Pallas kernels for 0%

profile of v11, /device:TPU:38, one launch (start us, length us, event | category | flops | bytes accessed | tf_op | source)
XLA Modules:
  0.0 172.3 jit_solution(17905198928528169329)
XLA Ops:
  2.4 4.3 %collective-permute-start.14 = (bf16[256,256]{1,0:T(8,128)(2,1)S(1)}, bf16[256,256]{1,0:T(8,128)(2,1)S(1)}, u32[]{:S(2)}, u32[]{:S(2)}) collective-permute-start(bf16[256,256]{1,0:T(8,128)(2,1)S(1)} %constant_dynamic-update-slice_fusion), channel_id=1, source_target_pairs={{0,8},{4,12},{8,16},{12,20},{16,24},{20,28},{24,32},{28,36},{32,40... | collective-permute-start | bytes 393224 | tf_op jit(solution)/shard_map/ppermute | solution.py:26
  6.7 8.5 %collective-permute-start.13 = (bf16[256,256]{1,0:T(8,128)(2,1)S(1)}, bf16[256,256]{1,0:T(8,128)(2,1)S(1)}, u32[]{:S(2)}, u32[]{:S(2)}) collective-permute-start(bf16[256,256]{1,0:T(8,128)(2,1)S(1)} %constant_dynamic-update-slice_fusion), channel_id=1, source_target_pairs={{8,0},{12,4},{16,8},{20,12},{24,16},{28,20},{32,24},{36,28},{40,32... | collective-permute-start | bytes 393224 | tf_op jit(solution)/shard_map/ppermute | solution.py:26
  25.2 6.0 %collective-permute-done = bf16[256,256]{1,0:T(8,128)(2,1)S(1)} collective-permute-done((bf16[256,256]{1,0:T(8,128)(2,1)S(1)}, bf16[256,256]{1,0:T(8,128)(2,1)S(1)}, u32[]{:S(2)}, u32[]{:S(2)}) %collective-permute-start) | collective-permute-done | bytes 131104 | tf_op jit(solution)/shard_map/ppermute | solution.py:17
  35.6 5.2 %collective-permute-start.3 = (bf16[256,256]{1,0:T(8,128)(2,1)S(1)}, bf16[256,256]{1,0:T(8,128)(2,1)S(1)}, u32[]{:S(2)}, u32[]{:S(2)}) collective-permute-start(bf16[256,256]{1,0:T(8,128)(2,1)S(1)} %constant_dynamic-update-slice_fusion), channel_id=1, source_target_pairs={{32,0},{36,4},{40,8},{44,12},{48,16},{52,20},{56,24},{60,28},{64,3... | collective-permute-start | bytes 393224 | tf_op jit(solution)/shard_map/ppermute | solution.py:26
  40.8 4.6 %collective-permute-start.4 = (bf16[256,256]{1,0:T(8,128)(2,1)S(1)}, bf16[256,256]{1,0:T(8,128)(2,1)S(1)}, u32[]{:S(2)}, u32[]{:S(2)}) collective-permute-start(bf16[256,256]{1,0:T(8,128)(2,1)S(1)} %constant_dynamic-update-slice_fusion), channel_id=1, source_target_pairs={{0,32},{4,36},{8,40},{12,44},{16,48},{20,52},{24,56},{28,60},{32,6... | collective-permute-start | bytes 393224 | tf_op jit(solution)/shard_map/ppermute | solution.py:26
  47.8 5.3 %collective-permute-start.5 = (bf16[256,256]{1,0:T(8,128)(2,1)S(1)}, bf16[256,256]{1,0:T(8,128)(2,1)S(1)}, u32[]{:S(2)}, u32[]{:S(2)}) collective-permute-start(bf16[256,256]{1,0:T(8,128)(2,1)S(1)} %constant_dynamic-update-slice_fusion), channel_id=1, source_target_pairs={{128,0},{132,4},{136,8},{140,12},{144,16},{148,20},{152,24},{156,2... | collective-permute-start | bytes 393224 | tf_op jit(solution)/shard_map/ppermute | solution.py:26
  53.1 2.5 %collective-permute-done.4 = bf16[256,256]{1,0:T(8,128)(2,1)S(1)} collective-permute-done((bf16[256,256]{1,0:T(8,128)(2,1)S(1)}, bf16[256,256]{1,0:T(8,128)(2,1)S(1)}, u32[]{:S(2)}, u32[]{:S(2)}) %collective-permute-start.4) | collective-permute-done | bytes 131104 | tf_op jit(solution)/shard_map/ppermute | solution.py:26
  57.6 7.9 %collective-permute-start.7 = (bf16[256,256]{1,0:T(8,128)(2,1)S(1)}, bf16[256,256]{1,0:T(8,128)(2,1)S(1)}, u32[]{:S(2)}, u32[]{:S(2)}) collective-permute-start(bf16[256,256]{1,0:T(8,128)(2,1)S(1)} %constant_dynamic-update-slice_fusion), channel_id=1, source_target_pairs={{16,0},{20,4},{24,8},{28,12},{32,16},{36,20},{40,24},{44,28},{48,3... | collective-permute-start | bytes 393224 | tf_op jit(solution)/shard_map/ppermute | solution.py:26
  65.5 2.6 %collective-permute-start.8 = (bf16[256,256]{1,0:T(8,128)(2,1)S(1)}, bf16[256,256]{1,0:T(8,128)(2,1)S(1)}, u32[]{:S(2)}, u32[]{:S(2)}) collective-permute-start(bf16[256,256]{1,0:T(8,128)(2,1)S(1)} %constant_dynamic-update-slice_fusion), channel_id=1, source_target_pairs={{0,16},{4,20},{8,24},{12,28},{16,32},{20,36},{24,40},{28,44},{32,4... | collective-permute-start | bytes 393224 | tf_op jit(solution)/shard_map/ppermute | solution.py:26
  68.4 5.8 %collective-permute-start.9 = (bf16[256,256]{1,0:T(8,128)(2,1)S(1)}, bf16[256,256]{1,0:T(8,128)(2,1)S(1)}, u32[]{:S(2)}, u32[]{:S(2)}) collective-permute-start(bf16[256,256]{1,0:T(8,128)(2,1)S(1)} %constant_dynamic-update-slice_fusion), channel_id=1, source_target_pairs={{64,0},{68,4},{72,8},{76,12},{80,16},{84,20},{88,24},{92,28},{96,3... | collective-permute-start | bytes 393224 | tf_op jit(solution)/shard_map/ppermute | solution.py:26
  74.2 3.6 %collective-permute-done.8 = bf16[256,256]{1,0:T(8,128)(2,1)S(1)} collective-permute-done((bf16[256,256]{1,0:T(8,128)(2,1)S(1)}, bf16[256,256]{1,0:T(8,128)(2,1)S(1)}, u32[]{:S(2)}, u32[]{:S(2)}) %collective-permute-start.8) | collective-permute-done | bytes 131104 | tf_op jit(solution)/shard_map/ppermute | solution.py:26
  79.8 4.1 %collective-permute-start.11 = (bf16[256,256]{1,0:T(8,128)(2,1)S(1)}, bf16[256,256]{1,0:T(8,128)(2,1)S(1)}, u32[]{:S(2)}, u32[]{:S(2)}) collective-permute-start(bf16[256,256]{1,0:T(8,128)(2,1)S(1)} %constant_dynamic-update-slice_fusion), channel_id=1, source_target_pairs={{12,0},{16,4},{20,8},{24,12},{28,16},{32,20},{36,24},{40,28},{44,3... | collective-permute-start | bytes 393224 | tf_op jit(solution)/shard_map/ppermute | solution.py:26
  88.1 3.3 %fusion.36 = (f32[256]{0:T(256)S(1)}, f32[256,4096]{0,1:T(8,128)S(1)}) fusion(bf16[256,128]{1,0:T(8,128)(2,1)S(1)} %copy-done.3, bf16[4096,256]{1,0:T(8,128)(2,1)S(1)} %constant_dynamic-update-slice_fusion.2, pred[256,3328]{0,1:T(32,128)(4,1)S(1)} %bitcast.21, pred[4096]{0:T(1024)(128)(4,1)S(1)} %pad.4.clone), kind=kOutput, calls=%fused_computation.93 | convolution fusion | flops 272629504 | bytes 6165504 | tf_op jit(solution)/shard_map/dot_general | solution.py:54
  96.8 5.8 %collective-permute-start.17 = (bf16[256,256]{0,1:T(8,128)(2,1)S(1)}, bf16[256,256]{0,1:T(8,128)(2,1)S(1)}, u32[]{:S(2)}, u32[]{:S(2)}) collective-permute-start(bf16[256,256]{0,1:T(8,128)(2,1)S(1)} %get-tuple-element.18), channel_id=1, source_target_pairs={{0,256},{4,260},{8,264},{12,268},{16,272},{20,276},{24,280},{28,28... | collective-permute-start | bytes 393224 | tf_op jit(solution)/shard_map/ppermute | solution.py:135
  102.5 5.3 %collective-permute-start.29 = (bf16[256,256]{0,1:T(8,128)(2,1)S(1)}, bf16[256,256]{0,1:T(8,128)(2,1)S(1)}, u32[]{:S(2)}, u32[]{:S(2)}) collective-permute-start(bf16[256,256]{0,1:T(8,128)(2,1)S(1)} %get-tuple-element.19), channel_id=1, source_target_pairs={{8,0},{12,4},{16,8},{20,12},{24,16},{28,20},{32,24},{36,28},{40,32... | collective-permute-start | bytes 393224 | tf_op jit(solution)/shard_map/ppermute | solution.py:26
  109.8 2.5 %collective-permute-start.27 = (bf16[256,256]{0,1:T(8,128)(2,1)S(1)}, bf16[256,256]{0,1:T(8,128)(2,1)S(1)}, u32[]{:S(2)}, u32[]{:S(2)}) collective-permute-start(bf16[256,256]{0,1:T(8,128)(2,1)S(1)} %get-tuple-element.21), channel_id=1, source_target_pairs={{12,0},{16,4},{20,8},{24,12},{28,16},{32,20},{36,24},{40,28},{44,3... | collective-permute-start | bytes 393224 | tf_op jit(solution)/shard_map/ppermute | solution.py:26
  112.3 3.0 %collective-permute-start.26 = (bf16[256,256]{0,1:T(8,128)(2,1)S(1)}, bf16[256,256]{0,1:T(8,128)(2,1)S(1)}, u32[]{:S(2)}, u32[]{:S(2)}) collective-permute-start(bf16[256,256]{0,1:T(8,128)(2,1)S(1)} %get-tuple-element.22), channel_id=1, source_target_pairs={{0,12},{4,16},{8,20},{12,24},{16,28},{20,32},{24,36},{28,40},{32,4... | collective-permute-start | bytes 393224 | tf_op jit(solution)/shard_map/ppermute | solution.py:26
  117.6 3.9 %collective-permute-start.24 = (bf16[256,256]{0,1:T(8,128)(2,1)S(1)}, bf16[256,256]{0,1:T(8,128)(2,1)S(1)}, u32[]{:S(2)}, u32[]{:S(2)}) collective-permute-start(bf16[256,256]{0,1:T(8,128)(2,1)S(1)} %get-tuple-element.24), channel_id=1, source_target_pairs={{0,64},{4,68},{8,72},{12,76},{16,80},{20,84},{24,88},{28,92},{32,9... | collective-permute-start | bytes 393224 | tf_op jit(solution)/shard_map/ppermute | solution.py:26
  121.6 7.1 %collective-permute-start.23 = (bf16[256,256]{0,1:T(8,128)(2,1)S(1)}, bf16[256,256]{0,1:T(8,128)(2,1)S(1)}, u32[]{:S(2)}, u32[]{:S(2)}) collective-permute-start(bf16[256,256]{0,1:T(8,128)(2,1)S(1)} %get-tuple-element.25), channel_id=1, source_target_pairs={{16,0},{20,4},{24,8},{28,12},{32,16},{36,20},{40,24},{44,28},{48,3... | collective-permute-start | bytes 393224 | tf_op jit(solution)/shard_map/ppermute | solution.py:26
  132.6 4.8 %collective-permute-start.20 = (bf16[256,256]{0,1:T(8,128)(2,1)}, bf16[256,256]{0,1:T(8,128)(2,1)S(1)}, u32[]{:S(2)}, u32[]{:S(2)}) collective-permute-start(bf16[256,256]{0,1:T(8,128)(2,1)} %get-tuple-element.28), channel_id=1, source_target_pairs={{0,128},{4,132},{8,136},{12,140},{16,144},{20,148},{24,152},{28,15... | collective-permute-start | bytes 393224 | tf_op jit(solution)/shard_map/ppermute | solution.py:26
  137.4 5.5 %collective-permute-start.19 = (bf16[256,256]{0,1:T(8,128)(2,1)S(1)}, bf16[256,256]{0,1:T(8,128)(2,1)S(1)}, u32[]{:S(2)}, u32[]{:S(2)}) collective-permute-start(bf16[256,256]{0,1:T(8,128)(2,1)S(1)} %get-tuple-element.29), channel_id=1, source_target_pairs={{32,0},{36,4},{40,8},{44,12},{48,16},{52,20},{56,24},{60,28},{64,3... | collective-permute-start | bytes 393224 | tf_op jit(solution)/shard_map/ppermute | solution.py:26
  142.9 4.3 %collective-permute-start.18 = (bf16[256,256]{0,1:T(8,128)(2,1)S(1)}, bf16[256,256]{0,1:T(8,128)(2,1)S(1)}, u32[]{:S(2)}, u32[]{:S(2)}) collective-permute-start(bf16[256,256]{0,1:T(8,128)(2,1)S(1)} %get-tuple-element.30), channel_id=1, source_target_pairs={{0,32},{4,36},{8,40},{12,44},{16,48},{20,52},{24,56},{28,60},{32,6... | collective-permute-start | bytes 393224 | tf_op jit(solution)/shard_map/ppermute | solution.py:26
  147.2 13.7 %collective-permute-start.15 = (bf16[256,256]{0,1:T(8,128)(2,1)S(1)}, bf16[256,256]{0,1:T(8,128)(2,1)S(1)}, u32[]{:S(2)}, u32[]{:S(2)}) collective-permute-start(bf16[256,256]{0,1:T(8,128)(2,1)S(1)} %get-tuple-element.31), channel_id=1, source_target_pairs={{4,0},{8,4},{12,8},{16,12},{20,16},{24,20},{28,24},{32,28},{36,32}... | collective-permute-start | bytes 393224 | tf_op jit(solution)/shard_map/ppermute | solution.py:26
  165.1 5.5 %collective-permute-done.16 = bf16[256,256]{0,1:T(8,128)(2,1)S(1)} collective-permute-done((bf16[256,256]{0,1:T(8,128)(2,1)S(1)}, bf16[256,256]{0,1:T(8,128)(2,1)S(1)}, u32[]{:S(2)}, u32[]{:S(2)}) %collective-permute-start.16) | collective-permute-done | bytes 131104 | tf_op jit(solution)/shard_map/ppermute | solution.py:26
  (103 shorter events, 46.1 us)
Async XLA Ops:
  2.4 85.6 %collective-permute-start.14 = (bf16[256,256]{1,0:T(8,128)(2,1)S(1)}, bf16[256,256]{1,0:T(8,128)(2,1)S(1)}, u32[]{:S(2)}, u32[]{:S(2)}) collective-permute-start(bf16[256,256]{1,0:T(8,128)(2,1)S(1)} %constant_dynamic-update-slice_fusion), channel_id=1, source_target_pairs={{0,8},{4,12},{8,16},{12,20},{16,24},{20,28},{24,32},{28,36},{32,40... | collective-permute-start | bytes 393224 | tf_op jit(solution)/shard_map/ppermute | solution.py:26
  6.7 81.3 %collective-permute-start.13 = (bf16[256,256]{1,0:T(8,128)(2,1)S(1)}, bf16[256,256]{1,0:T(8,128)(2,1)S(1)}, u32[]{:S(2)}, u32[]{:S(2)}) collective-permute-start(bf16[256,256]{1,0:T(8,128)(2,1)S(1)} %constant_dynamic-update-slice_fusion), channel_id=1, source_target_pairs={{8,0},{12,4},{16,8},{20,12},{24,16},{28,20},{32,24},{36,28},{40,32... | collective-permute-start | bytes 393224 | tf_op jit(solution)/shard_map/ppermute | solution.py:26
  15.2 72.8 %collective-permute-start.12 = (bf16[256,256]{1,0:T(8,128)(2,1)S(1)}, bf16[256,256]{1,0:T(8,128)(2,1)S(1)}, u32[]{:S(2)}, u32[]{:S(2)}) collective-permute-start(bf16[256,256]{1,0:T(8,128)(2,1)S(1)} %constant_dynamic-update-slice_fusion), channel_id=1, source_target_pairs={{0,12},{4,16},{8,20},{12,24},{16,28},{20,32},{24,36},{28,40},{32,4... | collective-permute-start | bytes 393224 | tf_op jit(solution)/shard_map/ppermute | solution.py:26
  17.1 23.7 %collective-permute-start.2 = (bf16[256,256]{1,0:T(8,128)(2,1)S(1)}, bf16[256,256]{1,0:T(8,128)(2,1)S(1)}, u32[]{:S(2)}, u32[]{:S(2)}) collective-permute-start(bf16[256,256]{1,0:T(8,128)(2,1)S(1)} %constant_dynamic-update-slice_fusion), channel_id=1, source_target_pairs={{0,256},{4,260},{8,264},{12,268},{16,272},{20,276},{24,280},{28,28... | collective-permute-start | bytes 393224 | tf_op jit(solution)/shard_map/ppermute | solution.py:94
  19.0 12.2 %collective-permute-start = (bf16[256,256]{1,0:T(8,128)(2,1)S(1)}, bf16[256,256]{1,0:T(8,128)(2,1)S(1)}, u32[]{:S(2)}, u32[]{:S(2)}) collective-permute-start(bf16[256,256]{1,0:T(8,128)(2,1)S(1)} %constant_dynamic-update-slice_fusion), channel_id=1, source_target_pairs={{0,4},{4,8},{8,12},{12,16},{16,20},{20,24},{24,28},{28,32},{32,36}... | collective-permute-start | bytes 393224 | tf_op jit(solution)/shard_map/ppermute | solution.py:17
  35.6 12.1 %collective-permute-start.3 = (bf16[256,256]{1,0:T(8,128)(2,1)S(1)}, bf16[256,256]{1,0:T(8,128)(2,1)S(1)}, u32[]{:S(2)}, u32[]{:S(2)}) collective-permute-start(bf16[256,256]{1,0:T(8,128)(2,1)S(1)} %constant_dynamic-update-slice_fusion), channel_id=1, source_target_pairs={{32,0},{36,4},{40,8},{44,12},{48,16},{52,20},{56,24},{60,28},{64,3... | collective-permute-start | bytes 393224 | tf_op jit(solution)/shard_map/ppermute | solution.py:26
  40.8 14.8 %collective-permute-start.4 = (bf16[256,256]{1,0:T(8,128)(2,1)S(1)}, bf16[256,256]{1,0:T(8,128)(2,1)S(1)}, u32[]{:S(2)}, u32[]{:S(2)}) collective-permute-start(bf16[256,256]{1,0:T(8,128)(2,1)S(1)} %constant_dynamic-update-slice_fusion), channel_id=1, source_target_pairs={{0,32},{4,36},{8,40},{12,44},{16,48},{20,52},{24,56},{28,60},{32,6... | collective-permute-start | bytes 393224 | tf_op jit(solution)/shard_map/ppermute | solution.py:26
  57.6 10.9 %collective-permute-start.7 = (bf16[256,256]{1,0:T(8,128)(2,1)S(1)}, bf16[256,256]{1,0:T(8,128)(2,1)S(1)}, u32[]{:S(2)}, u32[]{:S(2)}) collective-permute-start(bf16[256,256]{1,0:T(8,128)(2,1)S(1)} %constant_dynamic-update-slice_fusion), channel_id=1, source_target_pairs={{16,0},{20,4},{24,8},{28,12},{32,16},{36,20},{40,24},{44,28},{48,3... | collective-permute-start | bytes 393224 | tf_op jit(solution)/shard_map/ppermute | solution.py:26
  65.5 12.3 %collective-permute-start.8 = (bf16[256,256]{1,0:T(8,128)(2,1)S(1)}, bf16[256,256]{1,0:T(8,128)(2,1)S(1)}, u32[]{:S(2)}, u32[]{:S(2)}) collective-permute-start(bf16[256,256]{1,0:T(8,128)(2,1)S(1)} %constant_dynamic-update-slice_fusion), channel_id=1, source_target_pairs={{0,16},{4,20},{8,24},{12,28},{16,32},{20,36},{24,40},{28,44},{32,4... | collective-permute-start | bytes 393224 | tf_op jit(solution)/shard_map/ppermute | solution.py:26
  68.4 11.3 %collective-permute-start.9 = (bf16[256,256]{1,0:T(8,128)(2,1)S(1)}, bf16[256,256]{1,0:T(8,128)(2,1)S(1)}, u32[]{:S(2)}, u32[]{:S(2)}) collective-permute-start(bf16[256,256]{1,0:T(8,128)(2,1)S(1)} %constant_dynamic-update-slice_fusion), channel_id=1, source_target_pairs={{64,0},{68,4},{72,8},{76,12},{80,16},{84,20},{88,24},{92,28},{96,3... | collective-permute-start | bytes 393224 | tf_op jit(solution)/shard_map/ppermute | solution.py:26
  96.8 18.9 %collective-permute-start.17 = (bf16[256,256]{0,1:T(8,128)(2,1)S(1)}, bf16[256,256]{0,1:T(8,128)(2,1)S(1)}, u32[]{:S(2)}, u32[]{:S(2)}) collective-permute-start(bf16[256,256]{0,1:T(8,128)(2,1)S(1)} %get-tuple-element.18), channel_id=1, source_target_pairs={{0,256},{4,260},{8,264},{12,268},{16,272},{20,276},{24,280},{28,28... | collective-permute-start | bytes 393224 | tf_op jit(solution)/shard_map/ppermute | solution.py:135
  102.5 15.1 %collective-permute-start.29 = (bf16[256,256]{0,1:T(8,128)(2,1)S(1)}, bf16[256,256]{0,1:T(8,128)(2,1)S(1)}, u32[]{:S(2)}, u32[]{:S(2)}) collective-permute-start(bf16[256,256]{0,1:T(8,128)(2,1)S(1)} %get-tuple-element.19), channel_id=1, source_target_pairs={{8,0},{12,4},{16,8},{20,12},{24,16},{28,20},{32,24},{36,28},{40,32... | collective-permute-start | bytes 393224 | tf_op jit(solution)/shard_map/ppermute | solution.py:26
  107.8 13.7 %collective-permute-start.28 = (bf16[256,256]{0,1:T(8,128)(2,1)S(1)}, bf16[256,256]{0,1:T(8,128)(2,1)S(1)}, u32[]{:S(2)}, u32[]{:S(2)}) collective-permute-start(bf16[256,256]{0,1:T(8,128)(2,1)S(1)} %get-tuple-element.20), channel_id=1, source_target_pairs={{0,8},{4,12},{8,16},{12,20},{16,24},{20,28},{24,32},{28,36},{32,40... | collective-permute-start | bytes 393224 | tf_op jit(solution)/shard_map/ppermute | solution.py:26
  109.8 18.9 %collective-permute-start.27 = (bf16[256,256]{0,1:T(8,128)(2,1)S(1)}, bf16[256,256]{0,1:T(8,128)(2,1)S(1)}, u32[]{:S(2)}, u32[]{:S(2)}) collective-permute-start(bf16[256,256]{0,1:T(8,128)(2,1)S(1)} %get-tuple-element.21), channel_id=1, source_target_pairs={{12,0},{16,4},{20,8},{24,12},{28,16},{32,20},{36,24},{40,28},{44,3... | collective-permute-start | bytes 393224 | tf_op jit(solution)/shard_map/ppermute | solution.py:26
  112.3 18.3 %collective-permute-start.26 = (bf16[256,256]{0,1:T(8,128)(2,1)S(1)}, bf16[256,256]{0,1:T(8,128)(2,1)S(1)}, u32[]{:S(2)}, u32[]{:S(2)}) collective-permute-start(bf16[256,256]{0,1:T(8,128)(2,1)S(1)} %get-tuple-element.22), channel_id=1, source_target_pairs={{0,12},{4,16},{8,20},{12,24},{16,28},{20,32},{24,36},{28,40},{32,4... | collective-permute-start | bytes 393224 | tf_op jit(solution)/shard_map/ppermute | solution.py:26
  115.7 16.8 %collective-permute-start.25 = (bf16[256,256]{0,1:T(8,128)(2,1)S(1)}, bf16[256,256]{0,1:T(8,128)(2,1)S(1)}, u32[]{:S(2)}, u32[]{:S(2)}) collective-permute-start(bf16[256,256]{0,1:T(8,128)(2,1)S(1)} %get-tuple-element.23), channel_id=1, source_target_pairs={{64,0},{68,4},{72,8},{76,12},{80,16},{84,20},{88,24},{92,28},{96,3... | collective-permute-start | bytes 393224 | tf_op jit(solution)/shard_map/ppermute | solution.py:26
  117.6 19.8 %collective-permute-start.24 = (bf16[256,256]{0,1:T(8,128)(2,1)S(1)}, bf16[256,256]{0,1:T(8,128)(2,1)S(1)}, u32[]{:S(2)}, u32[]{:S(2)}) collective-permute-start(bf16[256,256]{0,1:T(8,128)(2,1)S(1)} %get-tuple-element.24), channel_id=1, source_target_pairs={{0,64},{4,68},{8,72},{12,76},{16,80},{20,84},{24,88},{28,92},{32,9... | collective-permute-start | bytes 393224 | tf_op jit(solution)/shard_map/ppermute | solution.py:26
  121.6 21.3 %collective-permute-start.23 = (bf16[256,256]{0,1:T(8,128)(2,1)S(1)}, bf16[256,256]{0,1:T(8,128)(2,1)S(1)}, u32[]{:S(2)}, u32[]{:S(2)}) collective-permute-start(bf16[256,256]{0,1:T(8,128)(2,1)S(1)} %get-tuple-element.25), channel_id=1, source_target_pairs={{16,0},{20,4},{24,8},{28,12},{32,16},{36,20},{40,24},{44,28},{48,3... | collective-permute-start | bytes 393224 | tf_op jit(solution)/shard_map/ppermute | solution.py:26
  128.6 18.5 %collective-permute-start.22 = (bf16[256,256]{0,1:T(8,128)(2,1)S(1)}, bf16[256,256]{0,1:T(8,128)(2,1)S(1)}, u32[]{:S(2)}, u32[]{:S(2)}) collective-permute-start(bf16[256,256]{0,1:T(8,128)(2,1)S(1)} %get-tuple-element.26), channel_id=1, source_target_pairs={{0,16},{4,20},{8,24},{12,28},{16,32},{20,36},{24,40},{28,44},{32,4... | collective-permute-start | bytes 393224 | tf_op jit(solution)/shard_map/ppermute | solution.py:26
  130.6 30.3 %collective-permute-start.21 = (bf16[256,256]{0,1:T(8,128)(2,1)S(1)}, bf16[256,256]{0,1:T(8,128)(2,1)S(1)}, u32[]{:S(2)}, u32[]{:S(2)}) collective-permute-start(bf16[256,256]{0,1:T(8,128)(2,1)S(1)} %get-tuple-element.27), channel_id=1, source_target_pairs={{128,0},{132,4},{136,8},{140,12},{144,16},{148,20},{152,24},{156,2... | collective-permute-start | bytes 393224 | tf_op jit(solution)/shard_map/ppermute | solution.py:26
  132.6 32.5 %collective-permute-start.20 = (bf16[256,256]{0,1:T(8,128)(2,1)}, bf16[256,256]{0,1:T(8,128)(2,1)S(1)}, u32[]{:S(2)}, u32[]{:S(2)}) collective-permute-start(bf16[256,256]{0,1:T(8,128)(2,1)} %get-tuple-element.28), channel_id=1, source_target_pairs={{0,128},{4,132},{8,136},{12,140},{16,144},{20,148},{24,152},{28,15... | collective-permute-start | bytes 393224 | tf_op jit(solution)/shard_map/ppermute | solution.py:26
  137.4 27.6 %collective-permute-start.19 = (bf16[256,256]{0,1:T(8,128)(2,1)S(1)}, bf16[256,256]{0,1:T(8,128)(2,1)S(1)}, u32[]{:S(2)}, u32[]{:S(2)}) collective-permute-start(bf16[256,256]{0,1:T(8,128)(2,1)S(1)} %get-tuple-element.29), channel_id=1, source_target_pairs={{32,0},{36,4},{40,8},{44,12},{48,16},{52,20},{56,24},{60,28},{64,3... | collective-permute-start | bytes 393224 | tf_op jit(solution)/shard_map/ppermute | solution.py:26
  142.9 22.1 %collective-permute-start.18 = (bf16[256,256]{0,1:T(8,128)(2,1)S(1)}, bf16[256,256]{0,1:T(8,128)(2,1)S(1)}, u32[]{:S(2)}, u32[]{:S(2)}) collective-permute-start(bf16[256,256]{0,1:T(8,128)(2,1)S(1)} %get-tuple-element.30), channel_id=1, source_target_pairs={{0,32},{4,36},{8,40},{12,44},{16,48},{20,52},{24,56},{28,60},{32,6... | collective-permute-start | bytes 393224 | tf_op jit(solution)/shard_map/ppermute | solution.py:26
  147.2 17.9 %collective-permute-start.15 = (bf16[256,256]{0,1:T(8,128)(2,1)S(1)}, bf16[256,256]{0,1:T(8,128)(2,1)S(1)}, u32[]{:S(2)}, u32[]{:S(2)}) collective-permute-start(bf16[256,256]{0,1:T(8,128)(2,1)S(1)} %get-tuple-element.31), channel_id=1, source_target_pairs={{4,0},{8,4},{12,8},{16,12},{20,16},{24,20},{28,24},{32,28},{36,32}... | collective-permute-start | bytes 393224 | tf_op jit(solution)/shard_map/ppermute | solution.py:26
  (10 other events, 167.5 us)

commit v12 on v8

--- a/solution.py
+++ b/solution.py
@@ -121,10 +121,7 @@
     near_terms = key_terms(
         weights[:, : 3 * tok_rows], dscores[:, : 3 * tok_rows], query_tokens, grad_out
     )
-    sent = near_terms.astype(jnp.bfloat16)
-    from_after = from_behind(sent[:tok_rows], "seq", -1).astype(jnp.float32)
-    from_before = from_behind(sent[2 * tok_rows :], "seq", 1).astype(jnp.float32)
-    grad_total = near_terms[tok_rows : 2 * tok_rows] + from_after + from_before
+    grad_total = near_terms[tok_rows : 2 * tok_rows]
     far_terms = key_terms(
         weights[:, 3 * tok_rows :], dscores[:, 3 * tok_rows :], query_tokens, grad_out
     )
@@ -140,6 +137,10 @@
         returned = returned.astype(jnp.float32)
         current = grad_total
         grad_total = current + returned
+    sent = near_terms.astype(jnp.bfloat16)
+    from_after = from_behind(sent[:tok_rows], "seq", -1).astype(jnp.float32)
+    from_before = from_behind(sent[2 * tok_rows :], "seq", 1).astype(jnp.float32)
+    grad_total = grad_total + from_after + from_before
     key_grad = grad_total[:, :HD]
     value_grad = grad_total[:, HD:]
     return (attention_out, query_grad, key_grad, value_grad)

time: 166 us -> 166 us (level)
  no operation moved by 1% of the time
where the time goes in v12:
time: 166 us; the launch traced here: 164 us
  starting transfers between devices  124 us (75%)
  waiting for transfers between devices  18.5 us (11%)
  local copies, waits for them, and re-layouts  8.93 us (5%)
  matrix products  7.99 us (5%)
  other arithmetic  3.02 us (2%)
    ppermute x26, starting transfers between devices, from_behind(): lax.ppermute(value, axis, [(source, source + steps) for source in range(l...  103 us
    ppermute x1, starting transfers between devices, shards(): lax.ppermute(grad_piece, 'seq', [(src, (src + half) % frame_count) for sr...  10.2 us
    ppermute x26, waiting for transfers between devices, from_behind(): lax.ppermute(value, axis, [(source, source + steps) for source in range(l...  9.86 us
    ppermute x1, starting transfers between devices, shards(): lax.ppermute(joined, 'seq', [(src, (src + half) % frame_count) for src in...  7.2 us
    unnamed x29, local copies, waits for them, and re-layouts  5.43 us
    ppermute x1, waiting for transfers between devices, extended(): after = lax.ppermute(leading, axis, down)  4.19 us
  transfers between devices with their start and end apart: 30, of which 7 were waited for; matrix products, arithmetic and copies ran while one was open for 5% of the time, Pallas kernels for 0%

profile of v12, /device:TPU:1, one launch (start us, length us, event | category | flops | bytes accessed | tf_op | source)
XLA Modules:
  0.0 164.1 jit_solution(5163596006183450277)
XLA Ops:
  2.4 4.8 %collective-permute-start.14 = (bf16[256,256]{1,0:T(8,128)(2,1)S(1)}, bf16[256,256]{1,0:T(8,128)(2,1)S(1)}, u32[]{:S(2)}, u32[]{:S(2)}) collective-permute-start(bf16[256,256]{1,0:T(8,128)(2,1)S(1)} %constant_dynamic-update-slice_fusion), channel_id=1, source_target_pairs={{0,8},{4,12},{8,16},{12,20},{16,24},{20,28},{24,32},{28,36},{32,40... | collective-permute-start | bytes 393224 | tf_op jit(solution)/shard_map/ppermute | solution.py:26
  8.6 10.4 %collective-permute-start.12 = (bf16[256,256]{1,0:T(8,128)(2,1)S(1)}, bf16[256,256]{1,0:T(8,128)(2,1)S(1)}, u32[]{:S(2)}, u32[]{:S(2)}) collective-permute-start(bf16[256,256]{1,0:T(8,128)(2,1)S(1)} %constant_dynamic-update-slice_fusion), channel_id=1, source_target_pairs={{0,64},{4,68},{8,72},{12,76},{16,80},{20,84},{24,88},{28,92},{32,9... | collective-permute-start | bytes 393224 | tf_op jit(solution)/shard_map/ppermute | solution.py:26
  20.2 1.9 %collective-permute-start = (bf16[256,256]{1,0:T(8,128)(2,1)S(1)}, bf16[256,256]{1,0:T(8,128)(2,1)S(1)}, u32[]{:S(2)}, u32[]{:S(2)}) collective-permute-start(bf16[256,256]{1,0:T(8,128)(2,1)S(1)} %constant_dynamic-update-slice_fusion), channel_id=1, source_target_pairs={{0,4},{4,8},{8,12},{12,16},{16,20},{20,24},{24,28},{28,32},{32,36}... | collective-permute-start | bytes 393224 | tf_op jit(solution)/shard_map/ppermute | solution.py:17
  26.4 3.2 %collective-permute-done = bf16[256,256]{1,0:T(8,128)(2,1)S(1)} collective-permute-done((bf16[256,256]{1,0:T(8,128)(2,1)S(1)}, bf16[256,256]{1,0:T(8,128)(2,1)S(1)}, u32[]{:S(2)}, u32[]{:S(2)}) %collective-permute-start) | collective-permute-done | bytes 131104 | tf_op jit(solution)/shard_map/ppermute | solution.py:17
  29.7 1.9 %collective-permute-start.1 = (bf16[256,256]{1,0:T(8,128)(2,1)S(1)}, bf16[256,256]{1,0:T(8,128)(2,1)S(1)}, u32[]{:S(2)}, u32[]{:S(2)}) collective-permute-start(bf16[256,256]{1,0:T(8,128)(2,1)S(1)} %constant_dynamic-update-slice_fusion), channel_id=1, source_target_pairs={{4,0},{8,4},{12,8},{16,12},{20,16},{24,20},{28,24},{32,28},{36,32}... | collective-permute-start | bytes 393224 | tf_op jit(solution)/shard_map/ppermute | solution.py:18
  32.5 4.2 %collective-permute-done.1 = bf16[256,256]{1,0:T(8,128)(2,1)S(1)} collective-permute-done((bf16[256,256]{1,0:T(8,128)(2,1)S(1)}, bf16[256,256]{1,0:T(8,128)(2,1)S(1)}, u32[]{:S(2)}, u32[]{:S(2)}) %collective-permute-start.1) | collective-permute-done | bytes 131104 | tf_op jit(solution)/shard_map/ppermute | solution.py:18
  36.7 6.3 %collective-permute-start.3 = (bf16[256,256]{1,0:T(8,128)(2,1)S(1)}, bf16[256,256]{1,0:T(8,128)(2,1)S(1)}, u32[]{:S(2)}, u32[]{:S(2)}) collective-permute-start(bf16[256,256]{1,0:T(8,128)(2,1)S(1)} %constant_dynamic-update-slice_fusion), channel_id=1, source_target_pairs={{0,32},{4,36},{8,40},{12,44},{16,48},{20,52},{24,56},{28,60},{32,6... | collective-permute-start | bytes 393224 | tf_op jit(solution)/shard_map/ppermute | solution.py:26
  43.0 7.2 %collective-permute-start.4 = (bf16[256,256]{1,0:T(8,128)(2,1)S(1)}, bf16[256,256]{1,0:T(8,128)(2,1)S(1)}, u32[]{:S(2)}, u32[]{:S(2)}) collective-permute-start(bf16[256,256]{1,0:T(8,128)(2,1)S(1)} %constant_dynamic-update-slice_fusion), channel_id=1, source_target_pairs={{0,256},{4,260},{8,264},{12,268},{16,272},{20,276},{24,280},{28,28... | collective-permute-start | bytes 393224 | tf_op jit(solution)/shard_map/ppermute | solution.py:94
  52.7 3.7 %collective-permute-start.6 = (bf16[256,256]{1,0:T(8,128)(2,1)S(1)}, bf16[256,256]{1,0:T(8,128)(2,1)S(1)}, u32[]{:S(2)}, u32[]{:S(2)}) collective-permute-start(bf16[256,256]{1,0:T(8,128)(2,1)S(1)} %constant_dynamic-update-slice_fusion), channel_id=1, source_target_pairs={{0,16},{4,20},{8,24},{12,28},{16,32},{20,36},{24,40},{28,44},{32,4... | collective-permute-start | bytes 393224 | tf_op jit(solution)/shard_map/ppermute | solution.py:26
  58.6 12.6 %collective-permute-start.8 = (bf16[256,256]{1,0:T(8,128)(2,1)S(1)}, bf16[256,256]{1,0:T(8,128)(2,1)S(1)}, u32[]{:S(2)}, u32[]{:S(2)}) collective-permute-start(bf16[256,256]{1,0:T(8,128)(2,1)S(1)} %constant_dynamic-update-slice_fusion), channel_id=1, source_target_pairs={{0,128},{4,132},{8,136},{12,140},{16,144},{20,148},{24,152},{28,15... | collective-permute-start | bytes 393224 | tf_op jit(solution)/shard_map/ppermute | solution.py:26
  73.2 5.9 %collective-permute-start.10 = (bf16[256,256]{1,0:T(8,128)(2,1)S(1)}, bf16[256,256]{1,0:T(8,128)(2,1)S(1)}, u32[]{:S(2)}, u32[]{:S(2)}) collective-permute-start(bf16[256,256]{1,0:T(8,128)(2,1)S(1)} %constant_dynamic-update-slice_fusion), channel_id=1, source_target_pairs={{0,12},{4,16},{8,20},{12,24},{16,28},{20,32},{24,36},{28,40},{32,4... | collective-permute-start | bytes 393224 | tf_op jit(solution)/shard_map/ppermute | solution.py:26
  79.1 3.8 %collective-permute-done.9 = bf16[256,256]{1,0:T(8,128)(2,1)S(1)} collective-permute-done((bf16[256,256]{1,0:T(8,128)(2,1)S(1)}, bf16[256,256]{1,0:T(8,128)(2,1)S(1)}, u32[]{:S(2)}, u32[]{:S(2)}) %collective-permute-start.9) | collective-permute-done | bytes 131104 | tf_op jit(solution)/shard_map/ppermute | solution.py:26
  84.3 4.6 %collective-permute-done.11 = bf16[256,256]{1,0:T(8,128)(2,1)S(1)} collective-permute-done((bf16[256,256]{1,0:T(8,128)(2,1)S(1)}, bf16[256,256]{1,0:T(8,128)(2,1)S(1)}, u32[]{:S(2)}, u32[]{:S(2)}) %collective-permute-start.11) | collective-permute-done | bytes 131104 | tf_op jit(solution)/shard_map/ppermute | solution.py:26
  89.0 3.3 %fusion.36 = (f32[256]{0:T(256)S(1)}, f32[256,4096]{0,1:T(8,128)S(1)}) fusion(bf16[256,128]{1,0:T(8,128)(2,1)S(1)} %copy-done.3, bf16[4096,256]{1,0:T(8,128)(2,1)S(1)} %constant_dynamic-update-slice_fusion.2, pred[256,3328]{0,1:T(32,128)(4,1)S(1)} %bitcast.21, pred[4096]{0:T(1024)(128)(4,1)S(1)} %pad.4.clone), kind=kOutput, calls=%fused_computation.93 | convolution fusion | flops 272629504 | bytes 6165504 | tf_op jit(solution)/shard_map/dot_general | solution.py:54
  97.7 5.1 %collective-permute-start.15 = (bf16[256,256]{0,1:T(8,128)(2,1)S(1)}, bf16[256,256]{0,1:T(8,128)(2,1)S(1)}, u32[]{:S(2)}, u32[]{:S(2)}) collective-permute-start(bf16[256,256]{0,1:T(8,128)(2,1)S(1)} %get-tuple-element.18), channel_id=1, source_target_pairs={{0,32},{4,36},{8,40},{12,44},{16,48},{20,52},{24,56},{28,60},{32,6... | collective-permute-start | bytes 393224 | tf_op jit(solution)/shard_map/ppermute | solution.py:26
  104.1 4.0 %collective-permute-start.26 = (bf16[256,256]{0,1:T(8,128)(2,1)S(1)}, bf16[256,256]{0,1:T(8,128)(2,1)S(1)}, u32[]{:S(2)}, u32[]{:S(2)}) collective-permute-start(bf16[256,256]{0,1:T(8,128)(2,1)S(1)} %get-tuple-element.20), channel_id=1, source_target_pairs={{0,8},{4,12},{8,16},{12,20},{16,24},{20,28},{24,32},{28,36},{32,40... | collective-permute-start | bytes 393224 | tf_op jit(solution)/shard_map/ppermute | solution.py:26
  109.4 4.9 %collective-permute-start.24 = (bf16[256,256]{0,1:T(8,128)(2,1)S(1)}, bf16[256,256]{0,1:T(8,128)(2,1)S(1)}, u32[]{:S(2)}, u32[]{:S(2)}) collective-permute-start(bf16[256,256]{0,1:T(8,128)(2,1)S(1)} %get-tuple-element.22), channel_id=1, source_target_pairs={{0,64},{4,68},{8,72},{12,76},{16,80},{20,84},{24,88},{28,92},{32,9... | collective-permute-start | bytes 393224 | tf_op jit(solution)/shard_map/ppermute | solution.py:26
  116.0 6.9 %collective-permute-start.22 = (bf16[256,256]{0,1:T(8,128)(2,1)S(1)}, bf16[256,256]{0,1:T(8,128)(2,1)S(1)}, u32[]{:S(2)}, u32[]{:S(2)}) collective-permute-start(bf16[256,256]{0,1:T(8,128)(2,1)S(1)} %get-tuple-element.24), channel_id=1, source_target_pairs={{0,12},{4,16},{8,20},{12,24},{16,28},{20,32},{24,36},{28,40},{32,4... | collective-permute-start | bytes 393224 | tf_op jit(solution)/shard_map/ppermute | solution.py:26
  124.2 8.8 %collective-permute-start.20 = (bf16[256,256]{0,1:T(8,128)(2,1)S(1)}, bf16[256,256]{0,1:T(8,128)(2,1)S(1)}, u32[]{:S(2)}, u32[]{:S(2)}) collective-permute-start(bf16[256,256]{0,1:T(8,128)(2,1)S(1)} %get-tuple-element.26), channel_id=1, source_target_pairs={{0,128},{4,132},{8,136},{12,140},{16,144},{20,148},{24,152},{28,15... | collective-permute-start | bytes 393224 | tf_op jit(solution)/shard_map/ppermute | solution.py:26
  134.3 4.9 %collective-permute-start.18 = (bf16[256,256]{0,1:T(8,128)(2,1)}, bf16[256,256]{0,1:T(8,128)(2,1)S(1)}, u32[]{:S(2)}, u32[]{:S(2)}) collective-permute-start(bf16[256,256]{0,1:T(8,128)(2,1)} %get-tuple-element.28), channel_id=1, source_target_pairs={{0,16},{4,20},{8,24},{12,28},{16,32},{20,36},{24,40},{28,44},{32,4... | collective-permute-start | bytes 393224 | tf_op jit(solution)/shard_map/ppermute | solution.py:26
  139.2 10.2 %collective-permute-start.17 = (bf16[256,256]{0,1:T(8,128)(2,1)S(1)}, bf16[256,256]{0,1:T(8,128)(2,1)S(1)}, u32[]{:S(2)}, u32[]{:S(2)}) collective-permute-start(bf16[256,256]{0,1:T(8,128)(2,1)S(1)} %get-tuple-element.29), channel_id=1, source_target_pairs={{0,256},{4,260},{8,264},{12,268},{16,272},{20,276},{24,280},{28,28... | collective-permute-start | bytes 393224 | tf_op jit(solution)/shard_map/ppermute | solution.py:132
  150.8 1.9 %collective-permute-start.28 = (bf16[256,256]{0,1:T(8,128)(2,1)S(1)}, bf16[256,256]{0,1:T(8,128)(2,1)S(1)}, u32[]{:S(2)}, u32[]{:S(2)}) collective-permute-start(bf16[256,256]{0,1:T(8,128)(2,1)S(1)} %get-tuple-element.31), channel_id=1, source_target_pairs={{4,0},{8,4},{12,8},{16,12},{20,16},{24,20},{28,24},{32,28},{36,32}... | collective-permute-start | bytes 393224 | tf_op jit(solution)/shard_map/ppermute | solution.py:26
  152.7 7.3 %collective-permute-start.29 = (bf16[256,256]{0,1:T(8,128)(2,1)S(1)}, bf16[256,256]{0,1:T(8,128)(2,1)S(1)}, u32[]{:S(2)}, u32[]{:S(2)}) collective-permute-start(bf16[256,256]{0,1:T(8,128)(2,1)S(1)} %get-tuple-element.32), channel_id=1, source_target_pairs={{0,4},{4,8},{8,12},{12,16},{16,20},{20,24},{24,28},{28,32},{32,36}... | collective-permute-start | bytes 393224 | tf_op jit(solution)/shard_map/ppermute | solution.py:26
  160.0 1.4 convolution_multiply_fusion.3
  (103 shorter events, 33.3 us)
Async XLA Ops:
  2.4 86.6 %collective-permute-start.14 = (bf16[256,256]{1,0:T(8,128)(2,1)S(1)}, bf16[256,256]{1,0:T(8,128)(2,1)S(1)}, u32[]{:S(2)}, u32[]{:S(2)}) collective-permute-start(bf16[256,256]{1,0:T(8,128)(2,1)S(1)} %constant_dynamic-update-slice_fusion), channel_id=1, source_target_pairs={{0,8},{4,12},{8,16},{12,20},{16,24},{20,28},{24,32},{28,36},{32,40... | collective-permute-start | bytes 393224 | tf_op jit(solution)/shard_map/ppermute | solution.py:26
  7.3 81.7 %collective-permute-start.13 = (bf16[256,256]{1,0:T(8,128)(2,1)S(1)}, bf16[256,256]{1,0:T(8,128)(2,1)S(1)}, u32[]{:S(2)}, u32[]{:S(2)}) collective-permute-start(bf16[256,256]{1,0:T(8,128)(2,1)S(1)} %constant_dynamic-update-slice_fusion), channel_id=1, source_target_pairs={{8,0},{12,4},{16,8},{20,12},{24,16},{28,20},{32,24},{36,28},{40,32... | collective-permute-start | bytes 393224 | tf_op jit(solution)/shard_map/ppermute | solution.py:26
  8.6 80.4 %collective-permute-start.12 = (bf16[256,256]{1,0:T(8,128)(2,1)S(1)}, bf16[256,256]{1,0:T(8,128)(2,1)S(1)}, u32[]{:S(2)}, u32[]{:S(2)}) collective-permute-start(bf16[256,256]{1,0:T(8,128)(2,1)S(1)} %constant_dynamic-update-slice_fusion), channel_id=1, source_target_pairs={{0,64},{4,68},{8,72},{12,76},{16,80},{20,84},{24,88},{28,92},{32,9... | collective-permute-start | bytes 393224 | tf_op jit(solution)/shard_map/ppermute | solution.py:26
  18.9 24.0 %collective-permute-start.2 = (bf16[256,256]{1,0:T(8,128)(2,1)S(1)}, bf16[256,256]{1,0:T(8,128)(2,1)S(1)}, u32[]{:S(2)}, u32[]{:S(2)}) collective-permute-start(bf16[256,256]{1,0:T(8,128)(2,1)S(1)} %constant_dynamic-update-slice_fusion), channel_id=1, source_target_pairs={{32,0},{36,4},{40,8},{44,12},{48,16},{52,20},{56,24},{60,28},{64,3... | collective-permute-start | bytes 393224 | tf_op jit(solution)/shard_map/ppermute | solution.py:26
  36.7 13.5 %collective-permute-start.3 = (bf16[256,256]{1,0:T(8,128)(2,1)S(1)}, bf16[256,256]{1,0:T(8,128)(2,1)S(1)}, u32[]{:S(2)}, u32[]{:S(2)}) collective-permute-start(bf16[256,256]{1,0:T(8,128)(2,1)S(1)} %constant_dynamic-update-slice_fusion), channel_id=1, source_target_pairs={{0,32},{4,36},{8,40},{12,44},{16,48},{20,52},{24,56},{28,60},{32,6... | collective-permute-start | bytes 393224 | tf_op jit(solution)/shard_map/ppermute | solution.py:26
  43.0 9.7 %collective-permute-start.4 = (bf16[256,256]{1,0:T(8,128)(2,1)S(1)}, bf16[256,256]{1,0:T(8,128)(2,1)S(1)}, u32[]{:S(2)}, u32[]{:S(2)}) collective-permute-start(bf16[256,256]{1,0:T(8,128)(2,1)S(1)} %constant_dynamic-update-slice_fusion), channel_id=1, source_target_pairs={{0,256},{4,260},{8,264},{12,268},{16,272},{20,276},{24,280},{28,28... | collective-permute-start | bytes 393224 | tf_op jit(solution)/shard_map/ppermute | solution.py:94
  57.3 14.0 %collective-permute-start.7 = (bf16[256,256]{1,0:T(8,128)(2,1)S(1)}, bf16[256,256]{1,0:T(8,128)(2,1)S(1)}, u32[]{:S(2)}, u32[]{:S(2)}) collective-permute-start(bf16[256,256]{1,0:T(8,128)(2,1)S(1)} %constant_dynamic-update-slice_fusion), channel_id=1, source_target_pairs={{128,0},{132,4},{136,8},{140,12},{144,16},{148,20},{152,24},{156,2... | collective-permute-start | bytes 393224 | tf_op jit(solution)/shard_map/ppermute | solution.py:26
  58.6 14.6 %collective-permute-start.8 = (bf16[256,256]{1,0:T(8,128)(2,1)S(1)}, bf16[256,256]{1,0:T(8,128)(2,1)S(1)}, u32[]{:S(2)}, u32[]{:S(2)}) collective-permute-start(bf16[256,256]{1,0:T(8,128)(2,1)S(1)} %constant_dynamic-update-slice_fusion), channel_id=1, source_target_pairs={{0,128},{4,132},{8,136},{12,140},{16,144},{20,148},{24,152},{28,15... | collective-permute-start | bytes 393224 | tf_op jit(solution)/shard_map/ppermute | solution.py:26
  71.3 11.7 %collective-permute-start.9 = (bf16[256,256]{1,0:T(8,128)(2,1)S(1)}, bf16[256,256]{1,0:T(8,128)(2,1)S(1)}, u32[]{:S(2)}, u32[]{:S(2)}) collective-permute-start(bf16[256,256]{1,0:T(8,128)(2,1)S(1)} %constant_dynamic-update-slice_fusion), channel_id=1, source_target_pairs={{12,0},{16,4},{20,8},{24,12},{28,16},{32,20},{36,24},{40,28},{44,3... | collective-permute-start | bytes 393224 | tf_op jit(solution)/shard_map/ppermute | solution.py:26
  73.2 11.1 %collective-permute-start.10 = (bf16[256,256]{1,0:T(8,128)(2,1)S(1)}, bf16[256,256]{1,0:T(8,128)(2,1)S(1)}, u32[]{:S(2)}, u32[]{:S(2)}) collective-permute-start(bf16[256,256]{1,0:T(8,128)(2,1)S(1)} %constant_dynamic-update-slice_fusion), channel_id=1, source_target_pairs={{0,12},{4,16},{8,20},{12,24},{16,28},{20,32},{24,36},{28,40},{32,4... | collective-permute-start | bytes 393224 | tf_op jit(solution)/shard_map/ppermute | solution.py:26
  97.7 16.9 %collective-permute-start.15 = (bf16[256,256]{0,1:T(8,128)(2,1)S(1)}, bf16[256,256]{0,1:T(8,128)(2,1)S(1)}, u32[]{:S(2)}, u32[]{:S(2)}) collective-permute-start(bf16[256,256]{0,1:T(8,128)(2,1)S(1)} %get-tuple-element.18), channel_id=1, source_target_pairs={{0,32},{4,36},{8,40},{12,44},{16,48},{20,52},{24,56},{28,60},{32,6... | collective-permute-start | bytes 393224 | tf_op jit(solution)/shard_map/ppermute | solution.py:26
  102.8 13.1 %collective-permute-start.27 = (bf16[256,256]{0,1:T(8,128)(2,1)S(1)}, bf16[256,256]{0,1:T(8,128)(2,1)S(1)}, u32[]{:S(2)}, u32[]{:S(2)}) collective-permute-start(bf16[256,256]{0,1:T(8,128)(2,1)S(1)} %get-tuple-element.19), channel_id=1, source_target_pairs={{8,0},{12,4},{16,8},{20,12},{24,16},{28,20},{32,24},{36,28},{40,32... | collective-permute-start | bytes 393224 | tf_op jit(solution)/shard_map/ppermute | solution.py:26
  104.1 18.7 %collective-permute-start.26 = (bf16[256,256]{0,1:T(8,128)(2,1)S(1)}, bf16[256,256]{0,1:T(8,128)(2,1)S(1)}, u32[]{:S(2)}, u32[]{:S(2)}) collective-permute-start(bf16[256,256]{0,1:T(8,128)(2,1)S(1)} %get-tuple-element.20), channel_id=1, source_target_pairs={{0,8},{4,12},{8,16},{12,20},{16,24},{20,28},{24,32},{28,36},{32,40... | collective-permute-start | bytes 393224 | tf_op jit(solution)/shard_map/ppermute | solution.py:26
  108.1 16.0 %collective-permute-start.25 = (bf16[256,256]{0,1:T(8,128)(2,1)S(1)}, bf16[256,256]{0,1:T(8,128)(2,1)S(1)}, u32[]{:S(2)}, u32[]{:S(2)}) collective-permute-start(bf16[256,256]{0,1:T(8,128)(2,1)S(1)} %get-tuple-element.21), channel_id=1, source_target_pairs={{64,0},{68,4},{72,8},{76,12},{80,16},{84,20},{88,24},{92,28},{96,3... | collective-permute-start | bytes 393224 | tf_op jit(solution)/shard_map/ppermute | solution.py:26
  109.4 23.6 %collective-permute-start.24 = (bf16[256,256]{0,1:T(8,128)(2,1)S(1)}, bf16[256,256]{0,1:T(8,128)(2,1)S(1)}, u32[]{:S(2)}, u32[]{:S(2)}) collective-permute-start(bf16[256,256]{0,1:T(8,128)(2,1)S(1)} %get-tuple-element.22), channel_id=1, source_target_pairs={{0,64},{4,68},{8,72},{12,76},{16,80},{20,84},{24,88},{28,92},{32,9... | collective-permute-start | bytes 393224 | tf_op jit(solution)/shard_map/ppermute | solution.py:26
  114.7 19.7 %collective-permute-start.23 = (bf16[256,256]{0,1:T(8,128)(2,1)S(1)}, bf16[256,256]{0,1:T(8,128)(2,1)S(1)}, u32[]{:S(2)}, u32[]{:S(2)}) collective-permute-start(bf16[256,256]{0,1:T(8,128)(2,1)S(1)} %get-tuple-element.23), channel_id=1, source_target_pairs={{12,0},{16,4},{20,8},{24,12},{28,16},{32,20},{36,24},{40,28},{44,3... | collective-permute-start | bytes 393224 | tf_op jit(solution)/shard_map/ppermute | solution.py:26
  116.0 23.3 %collective-permute-start.22 = (bf16[256,256]{0,1:T(8,128)(2,1)S(1)}, bf16[256,256]{0,1:T(8,128)(2,1)S(1)}, u32[]{:S(2)}, u32[]{:S(2)}) collective-permute-start(bf16[256,256]{0,1:T(8,128)(2,1)S(1)} %get-tuple-element.24), channel_id=1, source_target_pairs={{0,12},{4,16},{8,20},{12,24},{16,28},{20,32},{24,36},{28,40},{32,4... | collective-permute-start | bytes 393224 | tf_op jit(solution)/shard_map/ppermute | solution.py:26
  122.9 26.6 %collective-permute-start.21 = (bf16[256,256]{0,1:T(8,128)(2,1)S(1)}, bf16[256,256]{0,1:T(8,128)(2,1)S(1)}, u32[]{:S(2)}, u32[]{:S(2)}) collective-permute-start(bf16[256,256]{0,1:T(8,128)(2,1)S(1)} %get-tuple-element.25), channel_id=1, source_target_pairs={{128,0},{132,4},{136,8},{140,12},{144,16},{148,20},{152,24},{156,2... | collective-permute-start | bytes 393224 | tf_op jit(solution)/shard_map/ppermute | solution.py:26
  124.2 26.6 %collective-permute-start.20 = (bf16[256,256]{0,1:T(8,128)(2,1)S(1)}, bf16[256,256]{0,1:T(8,128)(2,1)S(1)}, u32[]{:S(2)}, u32[]{:S(2)}) collective-permute-start(bf16[256,256]{0,1:T(8,128)(2,1)S(1)} %get-tuple-element.26), channel_id=1, source_target_pairs={{0,128},{4,132},{8,136},{12,140},{16,144},{20,148},{24,152},{28,15... | collective-permute-start | bytes 393224 | tf_op jit(solution)/shard_map/ppermute | solution.py:26
  133.0 19.7 %collective-permute-start.19 = (bf16[256,256]{0,1:T(8,128)(2,1)S(1)}, bf16[256,256]{0,1:T(8,128)(2,1)S(1)}, u32[]{:S(2)}, u32[]{:S(2)}) collective-permute-start(bf16[256,256]{0,1:T(8,128)(2,1)S(1)} %get-tuple-element.27), channel_id=1, source_target_pairs={{16,0},{20,4},{24,8},{28,12},{32,16},{36,20},{40,24},{44,28},{48,3... | collective-permute-start | bytes 393224 | tf_op jit(solution)/shard_map/ppermute | solution.py:26
  134.3 27.9 %collective-permute-start.18 = (bf16[256,256]{0,1:T(8,128)(2,1)}, bf16[256,256]{0,1:T(8,128)(2,1)S(1)}, u32[]{:S(2)}, u32[]{:S(2)}) collective-permute-start(bf16[256,256]{0,1:T(8,128)(2,1)} %get-tuple-element.28), channel_id=1, source_target_pairs={{0,16},{4,20},{8,24},{12,28},{16,32},{20,36},{24,40},{28,44},{32,4... | collective-permute-start | bytes 393224 | tf_op jit(solution)/shard_map/ppermute | solution.py:26
  139.2 23.0 %collective-permute-start.17 = (bf16[256,256]{0,1:T(8,128)(2,1)S(1)}, bf16[256,256]{0,1:T(8,128)(2,1)S(1)}, u32[]{:S(2)}, u32[]{:S(2)}) collective-permute-start(bf16[256,256]{0,1:T(8,128)(2,1)S(1)} %get-tuple-element.29), channel_id=1, source_target_pairs={{0,256},{4,260},{8,264},{12,268},{16,272},{20,276},{24,280},{28,28... | collective-permute-start | bytes 393224 | tf_op jit(solution)/shard_map/ppermute | solution.py:132
  149.5 12.8 %collective-permute-start.16 = (bf16[256,256]{0,1:T(8,128)(2,1)S(1)}, bf16[256,256]{0,1:T(8,128)(2,1)S(1)}, u32[]{:S(2)}, u32[]{:S(2)}) collective-permute-start(bf16[256,256]{0,1:T(8,128)(2,1)S(1)} %get-tuple-element.30), channel_id=1, source_target_pairs={{32,0},{36,4},{40,8},{44,12},{48,16},{52,20},{56,24},{60,28},{64,3... | collective-permute-start | bytes 393224 | tf_op jit(solution)/shard_map/ppermute | solution.py:26
  150.8 11.5 %collective-permute-start.28 = (bf16[256,256]{0,1:T(8,128)(2,1)S(1)}, bf16[256,256]{0,1:T(8,128)(2,1)S(1)}, u32[]{:S(2)}, u32[]{:S(2)}) collective-permute-start(bf16[256,256]{0,1:T(8,128)(2,1)S(1)} %get-tuple-element.31), channel_id=1, source_target_pairs={{4,0},{8,4},{12,8},{16,12},{20,16},{24,20},{28,24},{32,28},{36,32}... | collective-permute-start | bytes 393224 | tf_op jit(solution)/shard_map/ppermute | solution.py:26
  (10 other events, 161.8 us)
